TPU v7x, 128 devices: a whole 4x4x4 slice. The times are simulated.
128 devices in a mesh: seq: 64 (over z, x, y), tp: 2 (over core).
Axes of the slice: x: 4, y: 4, z: 4, core: 2. Of those that a mesh axis runs over, the one named last changes fastest.
Arguments:
- layer_input: bfloat16 [16384, 2048], P('seq'), may hold values from -1.5 to 1.5
- query: bfloat16 [16384, 2048], P('seq', 'tp'), may hold values from -6 to 6
- suffix_kv: bfloat16 [2, 16384, 2048], P(None, 'seq', 'tp'), may hold values from -6 to 6
- prefix_kv: bfloat16 [2, 2048, 2048], P(None, 'seq', 'tp'), may hold values from -6 to 6
- node_len: int32 [64], replicated, may hold values from 8 to 32, as said below
- path: int32 [64, 3], P('seq'), may hold values from 0 to 63, as said below
- out_weight: bfloat16 [2048, 2048], P('tp'), may hold values from -0.125 to 0.125
- norm_gain: float32 [2048], replicated, may hold values from 0.1 to 1.9
- expert_ids: int32 [16384, 8], P('seq'), may hold values from 0 to 63, all different within a row; in each aligned block of 256 rows (0 to 255, 256 to 511, ...) at most 40 rows name the same one
- gates: float32 [16384, 8], P('seq'), may hold values from 0.1 to 0.4
- w_gate: bfloat16 [64, 2048, 1024], P('seq', None, 'tp'), may hold values from -0.125 to 0.125
- w_up: bfloat16 [64, 2048, 1024], P('seq', None, 'tp'), may hold values from -0.125 to 0.125
- w_down: bfloat16 [64, 1024, 2048], P('seq', 'tp'), may hold values from -0.1875 to 0.1875
Outputs:
- layer_out: bfloat16 [16384, 2048], P('seq', 'tp')
Inputs may be any that keep to these rules, and one draw needn't show every extreme that they name: `path`: row r names three different nodes. Nodes are of three levels: roots, middle nodes and leaves; a middle node always comes with the same root, a leaf always with the same middle node, and every node is named by some request. `node_len`: some node holds exactly 32 tokens. `expert_ids`: within the 256 rows of one request no expert is named more than 40 times, a bound that some block reaches.
All inputs are finite; a program needn't handle non-finite values.
Results may differ from a plain program's by a relative error of at most 0.019.
Values may be sent and summed in bfloat16 or wider, within the bound.
No kernel may reach another device: no remote copies, remote signals or barrier semaphores. Data moves between devices by JAX's collectives and lax.ppermute only.
A program may use at most 128 MiB of HBM per device.

v0:
```python
import math

import jax
import jax.numpy as jnp
from jax import lax
from jax.sharding import PartitionSpec as P

D = 2048
HD = 128
TOPK = 8


def local(
    layer_input,
    query,
    suffix_kv,
    prefix_kv,
    node_len,
    path,
    out_weight,
    norm_gain,
    expert_ids,
    gates,
    w_gate,
    w_up,
    w_down,
):
    rows = query.shape[0]
    width = query.shape[1]
    heads_here = width // HD
    scale = 1.0 / math.sqrt(HD)
    seq_count = lax.axis_size("seq")
    tp_index = lax.axis_index("tp")
    tp_count = lax.axis_size("tp")
    depth = path.shape[1]
    slot = prefix_kv.shape[1]

    swap = [(i, (i + 1) % tp_count) for i in range(tp_count)]
    gate_full = jnp.concatenate([w_gate[0], lax.ppermute(w_gate[0], "tp", swap)], 1)
    up_full = jnp.concatenate([w_up[0], lax.ppermute(w_up[0], "tp", swap)], 1)
    down_full = jnp.concatenate([w_down[0], lax.ppermute(w_down[0], "tp", swap)], 0)

    pieces = prefix_kv.reshape(seq_count, -1)
    piece = pieces.shape[1]
    tag = jnp.zeros((seq_count, 128), pieces.dtype).at[:, :depth].set(
        jnp.broadcast_to(path.astype(pieces.dtype), (seq_count, depth))
    )
    outbound = jnp.concatenate([pieces, tag], 1)
    spread = lax.all_to_all(
        outbound.reshape(seq_count, -1, 128), "seq", 0, 0, tiled=True
    ).reshape(seq_count, -1)
    paths = spread[:, piece : piece + depth].astype(jnp.int32)
    spread = spread[:, :piece]
    node_ids = jnp.arange(spread.shape[0], dtype=jnp.int32)
    pick = (paths.reshape(-1)[:, None] == node_ids[None, :]).astype(spread.dtype)
    picked = jnp.dot(pick, spread, preferred_element_type=jnp.float32).astype(spread.dtype)
    got = lax.all_to_all(
        picked.reshape(seq_count, depth * piece // 128, 128), "seq", 0, 0, tiled=True
    )
    nodes_kv = got.reshape(seq_count, depth, piece).transpose(1, 0, 2).reshape(depth, 2, slot, width)
    prefix_keys = nodes_kv[:, 0].reshape(depth * slot, heads_here, HD)
    prefix_values = nodes_kv[:, 1].reshape(depth * slot, heads_here, HD)

    my_nodes = path[0]
    lengths = jnp.sum(
        jnp.where(my_nodes[:, None] == node_ids[None, :], node_len[None, :], 0), axis=1
    )
    live = (jnp.arange(slot, dtype=jnp.int32)[None, :] < lengths[:, None]).reshape(-1)
    live_all = jnp.concatenate([jnp.ones((rows,), dtype=bool), live])

    queries = query.reshape(rows, heads_here, HD)
    keys = jnp.concatenate([suffix_kv[0].reshape(rows, heads_here, HD), prefix_keys], 0)
    values = jnp.concatenate(
        [suffix_kv[1].reshape(rows, heads_here, HD), prefix_values], 0
    ).astype(jnp.float32)
    scores = (
        jnp.einsum("qhd,khd->hqk", queries, keys, preferred_element_type=jnp.float32) * scale
    )
    scores = jnp.where(live_all[None, None, :], scores, -jnp.inf)
    top = jnp.max(scores, axis=2)
    probs = jnp.exp(scores - top[:, :, None])
    total = jnp.sum(probs, axis=2)
    accum = jnp.einsum("hqk,khd->hqd", probs, values)
    attn = (accum / total[:, :, None]).astype(jnp.bfloat16)
    partial_value = jnp.einsum(
        "hqd,hdm->qm",
        attn,
        out_weight.reshape(heads_here, HD, D),
        preferred_element_type=jnp.float32,
    )
    heads_sum = partial_value + lax.ppermute(partial_value, "tp", swap)
    hidden_state = layer_input.astype(jnp.float32) + heads_sum
    mean_square = jnp.mean(hidden_state * hidden_state, axis=1, keepdims=True)
    normed = (hidden_state * lax.rsqrt(mean_square + 1e-06) * norm_gain).astype(jnp.bfloat16)

    experts = w_gate.shape[0] * seq_count
    cap = 5 * rows * TOPK // (4 * experts)
    share = -(-(-(-cap // tp_count)) // 8) * 8
    hit = expert_ids[:, :, None] == jnp.arange(experts, dtype=jnp.int32)[None, None, :]
    chosen = jnp.any(hit, axis=1)
    weight_of = jnp.sum(jnp.where(hit, gates[:, :, None], 0.0), axis=1)
    token = jnp.arange(rows, dtype=jnp.int32)
    earlier = (token[None, :] < token[:, None]).astype(jnp.bfloat16)
    ranks = jnp.dot(
        earlier, chosen.astype(jnp.bfloat16), preferred_element_type=jnp.float32
    ).astype(jnp.int32)
    half = D // tp_count
    down_cols = down_full.reshape(down_full.shape[0], tp_count, half)
    first = cap // tp_count // 8 * 8
    main = tp_count * first
    over = -(-(cap - main) // 8) * 8

    def combine_with(back, spot):
        combine = jnp.where(
            chosen.T[None, :, :, None] & (ranks.T[None, :, :, None] == spot[:, None, None, :]),
            weight_of.T[None, :, :, None],
            0.0,
        )
        combine = jnp.moveaxis(combine, 2, 0).reshape(rows, -1)
        combine_hi = combine.astype(jnp.bfloat16)
        combine_lo = (combine - combine_hi.astype(jnp.float32)).astype(jnp.bfloat16)
        both = lax.optimization_barrier(jnp.concatenate([combine_hi, combine_lo], 0))
        parts = jnp.dot(both, back, preferred_element_type=jnp.float32)
        return parts[:rows] + parts[rows:]

    def expert_rows(arrived):
        gate_part = jnp.dot(arrived, gate_full, preferred_element_type=jnp.float32)
        up_part = jnp.dot(arrived, up_full, preferred_element_type=jnp.float32)
        return (jax.nn.silu(gate_part) * up_part).astype(jnp.bfloat16)

    def select(wanted):
        sel = chosen[:, :, None] & (ranks[:, :, None] == wanted[None, None, :])
        return sel.reshape(rows, experts * wanted.shape[0]).astype(jnp.bfloat16)

    mine = lax.dynamic_slice_in_dim(normed, tp_index * half, half, 1)
    extra = jnp.arange(main, main + over, dtype=jnp.int32)
    outgoing = jnp.einsum(
        "ts,td->sd", select(extra), mine, preferred_element_type=jnp.float32
    ).astype(jnp.bfloat16)
    arrived = lax.all_to_all(outgoing.reshape(experts, over, half), "seq", 0, 0, tiled=True)
    arrived = arrived.reshape(experts * over, half)
    partner = lax.ppermute(arrived, "tp", swap)
    arrived = jnp.where(
        tp_index == 0,
        jnp.concatenate([arrived, partner], 1),
        jnp.concatenate([partner, arrived], 1),
    )
    act = expert_rows(arrived)
    result = jnp.dot(
        act, lax.dynamic_slice_in_dim(down_cols, tp_index, 1, 1)[:, 0],
        preferred_element_type=jnp.float32,
    ).astype(jnp.bfloat16)
    back = lax.all_to_all(result.reshape(experts, over, half), "seq", 0, 0, tiled=True)
    mixture = combine_with(back.reshape(experts * over, half), extra[None, :])

    target = tp_count * jnp.arange(first, dtype=jnp.int32) + tp_index
    outgoing = jnp.einsum(
        "ts,td->sd", select(target), normed, preferred_element_type=jnp.float32
    ).astype(jnp.bfloat16)
    arrived = lax.all_to_all(
        outgoing.reshape(experts, first, D), "seq", 0, 0, tiled=True
    ).reshape(experts * first, D)
    act = expert_rows(arrived)
    result = jnp.stack(
        [
            jnp.dot(act, down_cols[:, u], preferred_element_type=jnp.float32).astype(jnp.bfloat16)
            for u in range(tp_count)
        ]
    )
    back = lax.all_to_all(
        result.reshape(tp_count * experts, first, half), ("tp", "seq"), 0, 0, tiled=True
    )
    spot = (
        tp_count * jnp.arange(first, dtype=jnp.int32)[None, :]
        + jnp.arange(tp_count, dtype=jnp.int32)[:, None]
    )
    mixture = mixture + combine_with(back.reshape(-1, half), spot)
    residual = lax.dynamic_slice_in_dim(hidden_state, tp_index * half, half, 1)
    return (residual + mixture).astype(jnp.bfloat16)


def solution(mesh):
    in_specs = (
        P("seq", None),
        P("seq", "tp"),
        P(None, "seq", "tp"),
        P(None, "seq", "tp"),
        P(),
        P("seq", None),
        P("tp", None),
        P(),
        P("seq", None),
        P("seq", None),
        P("seq", None, "tp"),
        P("seq", None, "tp"),
        P("seq", "tp", None),
    )
    out_specs = P("seq", "tp")
    return jax.shard_map(local, mesh=mesh, in_specs=in_specs, out_specs=out_specs, check_vma=False)
```

profile of v0, /device:TPU:1, one launch (start us, length us, event | category | flops | bytes accessed | tf_op | source)
XLA Modules:
  0.0 248.3 jit_solution(3493454448753373261)
XLA Ops:
  0.0 0.6 compare_reduce_fusion
  0.6 1.3 fusion.81
  2.0 0.9 pad_maximum_fusion.16
  2.9 0.8 reshape.193
  3.7 12.0 %all-to-all-start = ((bf16[64,9,128]{2,1,0:T(8,128)(2,1)}), bf16[64,9,128]{2,1,0:T(8,128)(2,1)S(1)}, u32[]{:S(2)}, u32[]{:S(2)}) async-start(bf16[64,9,128]{2,1,0:T(8,128)(2,1)} %reshape.193), calls=%async_computation | async-start | bytes 524288 | tf_op jit(solution)/shard_map/all_to_all | solution.py:49
  15.7 0.9 select_reduce_fusion.1
  16.5 8.6 %all-to-all-done = bf16[64,9,128]{2,1,0:T(8,128)(2,1)S(1)} async-done(((bf16[64,9,128]{2,1,0:T(8,128)(2,1)}), bf16[64,9,128]{2,1,0:T(8,128)(2,1)S(1)}, u32[]{:S(2)}, u32[]{:S(2)}) %all-to-all-start) | async-done | bytes 147488 | tf_op jit(solution)/shard_map/all_to_all | solution.py:49
  25.3 0.3 convolution_convert_fusion.2
  25.6 0.9 reshape.195
  26.5 4.9 %all-to-all-start.1 = ((bf16[64,24,128]{2,1,0:T(8,128)(2,1)}), bf16[64,24,128]{2,1,0:T(8,128)(2,1)S(1)}, u32[]{:S(2)}, u32[]{:S(2)}) async-start(bf16[64,24,128]{2,1,0:T(8,128)(2,1)} %reshape.195), calls=%async_computation.1 | async-start | bytes 786432 | tf_op jit(solution)/shard_map/all_to_all | solution.py:57
  31.9 1.0 copy.62
  33.1 1.0 copy.67
  34.1 7.5 %all-to-all-done.1 = bf16[64,24,128]{2,1,0:T(8,128)(2,1)S(1)} async-done(((bf16[64,24,128]{2,1,0:T(8,128)(2,1)}), bf16[64,24,128]{2,1,0:T(8,128)(2,1)S(1)}, u32[]{:S(2)}, u32[]{:S(2)}) %all-to-all-start.1) | async-done | bytes 393248 | tf_op jit(solution)/shard_map/all_to_all | solution.py:57
  42.2 0.7 copy.68
  42.9 1.6 bitcast_reduce_fusion
  44.5 0.7 fusion.5
  45.2 0.4 copy-done.6
  45.6 5.7 %convolution_bitcast_fusion = f32[256,2048]{1,0:T(8,128)} fusion(bf16[8,128,2048]{2,1,0:T(8,128)(2,1)} %bitcast.180, f32[8,352,256]{2,1,0:T(8,128)S(1)} %get-tuple-element.24, f32[8,256]{1,0:T(8,128)S(1)} %get-tuple-element.23, pred[352]{0:T(512)(128)(4,1)S(1)} %concatenate.40, bf16[96,8,128]{2,0,1:T(8,128)(2,1)} %copy.68, ...), kind=kOutput, calls=%fused_computation.13 | convolution fusion | flops 1262419968 | bytes 9912672 | tf_op jit(solution)/shard_map/hqd,hdm->qm/dot_general | solution.py:85
  51.3 3.1 %collective-permute-start = (f32[256,2048]{1,0:T(8,128)}, f32[256,2048]{1,0:T(8,128)}, u32[]{:S(2)}, u32[]{:S(2)}) collective-permute-start(f32[256,2048]{1,0:T(8,128)} %convolution_bitcast_fusion), channel_id=1, source_target_pairs={{0,1},{1,0},{2,3},{3,2},{4,5},{5,4},{6,7},{7,6},{8,9},{9,8},{10,11... | collective-permute-start | bytes 6291464 | tf_op jit(solution)/shard_map/ppermute | solution.py:91
  54.8 3.7 %collective-permute-done = f32[256,2048]{1,0:T(8,128)} collective-permute-done((f32[256,2048]{1,0:T(8,128)}, f32[256,2048]{1,0:T(8,128)}, u32[]{:S(2)}, u32[]{:S(2)}) %collective-permute-start) | collective-permute-done | bytes 2097184 | tf_op jit(solution)/shard_map/ppermute | solution.py:91
  58.5 2.9 %multiply_reduce_fusion = (f32[256]{0:T(256)S(1)}, f32[256,2048]{1,0:T(8,128)S(1)}) fusion(f32[256,2048]{1,0:T(8,128)} %convolution_bitcast_fusion, f32[256,2048]{1,0:T(8,128)} %collective-permute-done, bf16[256,2048]{1,0:T(8,128)(2,1)} %param.15), kind=kLoop, calls=%fused_computation.41 | loop fusion | flops 2621184 | bytes 7341056 | tf_op jit(solution)/shard_map/reduce_sum | solution.py:93
  61.7 1.0 copy-done.3
  62.7 1.5 fusion.35
  64.1 5.5 %all-to-all-start.2 = ((bf16[64,8,1024]{2,1,0:T(8,128)(2,1)}), bf16[64,8,1024]{2,1,0:T(8,128)(2,1)}, u32[]{:S(2)}, u32[]{:S(2)}) async-start(bf16[64,8,1024]{2,1,0:T(8,128)(2,1)} %fusion.35), calls=%async_computation.2 | async-start | bytes 2097152 | tf_op jit(solution)/shard_map/all_to_all | solution.py:140
  70.0 4.4 %convolution_convert_fusion = bf16[1024,2048]{1,0:T(8,128)(2,1)} fusion(pred[256,1024]{0,1:T(32,128)(4,1)S(1)} %fusion.53, bf16[256,2048]{1,0:T(8,128)(2,1)} %copy-done.3), kind=kOutput, calls=%fused_computation.8 | convolution fusion | flops 1075838976 | bytes 5505024 | tf_op jit(solution)/shard_map/ts,td->sd/dot_general | solution.py:157
  74.5 12.9 %all-to-all-done.2 = bf16[64,8,1024]{2,1,0:T(8,128)(2,1)} async-done(((bf16[64,8,1024]{2,1,0:T(8,128)(2,1)}), bf16[64,8,1024]{2,1,0:T(8,128)(2,1)}, u32[]{:S(2)}, u32[]{:S(2)}) %all-to-all-start.2) | async-done | bytes 1048608 | tf_op jit(solution)/shard_map/all_to_all | solution.py:140
  87.4 5.8 %all-to-all-start.4 = ((bf16[64,16,2048]{2,1,0:T(8,128)(2,1)}), bf16[64,16,2048]{2,1,0:T(8,128)(2,1)}, u32[]{:S(2)}, u32[]{:S(2)}) async-start(bf16[64,16,2048]{2,1,0:T(8,128)(2,1)} %bitcast.157), calls=%async_computation.4 | async-start | bytes 8388608 | tf_op jit(solution)/shard_map/all_to_all | solution.py:160
  93.2 1.9 collective-permute-start.3
  95.1 3.9 %copy.69 = bf16[1,512,2048]{1,2,0:T(8,128)(2,1)} copy(bf16[1,512,2048]{2,1,0:T(8,128)(2,1)} %param.27) | data formatting | bytes 4194304 | tf_op args[12]
  99.0 0.5 collective-permute-start.2
  99.6 8.5 %collective-permute-done.1 = bf16[512,1024]{1,0:T(8,128)(2,1)} collective-permute-done((bf16[512,1024]{1,0:T(8,128)(2,1)}, bf16[512,1024]{1,0:T(8,128)(2,1)}, u32[]{:S(2)}, u32[]{:S(2)}) %collective-permute-start.1) | collective-permute-done | bytes 1048608 | tf_op jit(solution)/shard_map/ppermute | solution.py:142
  108.0 7.2 %fusion.2 = f32[512,1024]{1,0:T(8,128)} fusion(bf16[2048,512]{1,0:T(8,128)(2,1)} %collective-permute-done.3, bf16[2048,512]{1,0:T(8,128)(2,1)} %bitcast.185, bf16[512,1024]{1,0:T(8,128)(2,1)} %collective-permute-done.1, bf16[512,1024]{1,0:T(8,128)(2,1)} %bitcast.20, pred[]{:T(512)S(6)} %eq.146), kind=kOutput, calls=%fused_computation.15 | convolution fusion | flops 2165309440 | bytes 8388609 | tf_op jit(solution)/shard_map/dot_general | solution.py:128
  115.2 9.4 %fusion.36 = bf16[64,8,1024]{2,1,0:T(8,128)(2,1)} fusion(s32[]{:T(128)S(6)} %select_n.56, bf16[512,2,1024]{0,2,1:T(8,128)(2,1)} %bitcast.163, bf16[512,2,1024]{0,2,1:T(8,128)(2,1)} %bitcast.25, f32[512,1024]{1,0:T(8,128)} %fusion.2, bf16[2048,512]{1,0:T(8,128)(2,1)} %collective-permute-done.2, bf16[2048,512]{1,0:T(8,128)(2,1)} %bitcast.182, ...), kind=kOutput, calls=%fused_computation.51 | convolution fusion | flops 3246915584 | bytes 13631493 | tf_op jit(solution)/shard_map/dot_general | solution.py:149
  124.5 18.2 %all-to-all-done.4 = bf16[64,16,2048]{2,1,0:T(8,128)(2,1)} async-done(((bf16[64,16,2048]{2,1,0:T(8,128)(2,1)}), bf16[64,16,2048]{2,1,0:T(8,128)(2,1)}, u32[]{:S(2)}, u32[]{:S(2)}) %all-to-all-start.4) | async-done | bytes 4194336 | tf_op jit(solution)/shard_map/all_to_all | solution.py:160
  142.8 10.2 %all-to-all-start.3 = ((bf16[64,8,1024]{2,1,0:T(8,128)(2,1)}), bf16[64,8,1024]{2,1,0:T(8,128)(2,1)}, u32[]{:S(2)}, u32[]{:S(2)}) async-start(bf16[64,8,1024]{2,1,0:T(8,128)(2,1)} %fusion.36), calls=%async_computation.3 | async-start | bytes 2097152 | tf_op jit(solution)/shard_map/all_to_all | solution.py:153
  153.0 7.7 %fusion.3 = f32[1024,1024]{1,0:T(8,128)S(1)} fusion(bf16[1024,2048]{1,0:T(8,128)(2,1)} %bitcast.35, bf16[2048,512]{1,0:T(8,128)(2,1)} %collective-permute-done.2, bf16[2048,512]{1,0:T(8,128)(2,1)} %bitcast.183), kind=kOutput, calls=%fused_computation.16 | convolution fusion | flops 4303355904 | bytes 12582912 | tf_op jit(solution)/shard_map/dot_general | solution.py:127
  160.7 7.8 %multiply_convert_fusion = bf16[1024,1024]{1,0:T(8,128)(2,1)S(1)} fusion(f32[1024,1024]{1,0:T(8,128)S(1)} %fusion.3, bf16[1024,2048]{1,0:T(8,128)(2,1)} %bitcast.35, bf16[2048,512]{1,0:T(8,128)(2,1)} %collective-permute-done.3, bf16[2048,512]{1,0:T(8,128)(2,1)S(1)} %bitcast.186), kind=kOutput, calls=%fused_computation.7 | convolution fusion | flops 4309647360 | bytes 14680064 | tf_op jit(solution)/shard_map/dot_general | solution.py:128
  168.5 3.6 %convert_bitcast_fusion.1 = bf16[1,1024,1024]{2,1,0:T(8,128)(2,1)S(1)} fusion(bf16[1024,1024]{1,0:T(8,128)(2,1)S(1)} %multiply_convert_fusion, bf16[512,2,1024]{0,2,1:T(8,128)(2,1)S(1)} %bitcast.164, bf16[512,2,1024]{0,2,1:T(8,128)(2,1)} %bitcast.25), kind=kOutput, calls=%fused_computation.38 | convolution fusion | flops 2152726528 | bytes 8388608 | tf_op jit(solution)/shard_map/dot_general | solution.py:166
  172.2 3.6 %convert_bitcast_fusion = bf16[1,1024,1024]{2,1,0:T(8,128)(2,1)S(1)} fusion(bf16[1024,1024]{1,0:T(8,128)(2,1)S(1)} %multiply_convert_fusion, bf16[512,2,1024]{0,2,1:T(8,128)(2,1)} %bitcast.25, bf16[512,2,1024]{0,2,1:T(8,128)(2,1)S(1)} %bitcast.165), kind=kOutput, calls=%fused_computation.37 | convolution fusion | flops 2152726528 | bytes 8388608 | tf_op jit(solution)/shard_map/dot_general | solution.py:166
  175.8 2.3 pad_maximum_fusion.2
  178.1 10.8 %all-to-all-start.5 = ((bf16[128,16,1024]{2,1,0:T(8,128)(2,1)}), bf16[128,16,1024]{2,1,0:T(8,128)(2,1)}, u32[]{:S(2)}, u32[]{:S(2)}) async-start(bf16[128,16,1024]{2,1,0:T(8,128)(2,1)} %bitcast.158), calls=%async_computation.5 | async-start | bytes 8388608 | tf_op jit(solution)/shard_map/all_to_all | solution.py:170
  189.1 0.6 fusion.21
  189.7 0.7 fusion.22
  190.8 1.5 pad_maximum_fusion.10
  192.3 3.3 %fusion.50 = f32[512,1024]{1,0:T(8,128)} fusion(bf16[512,512]{0,1:T(8,128)(2,1)S(1)} %pad_maximum_fusion.15, bf16[64,8,1024]{2,1,0:T(8,128)(2,1)} %all-to-all-done.3), kind=kOutput, calls=%fused_computation.62 | convolution fusion | flops 536870912 | bytes 3670016 | tf_op jit(solution)/shard_map/dot_general | solution.py:123
  195.6 46.1 %all-to-all-done.5 = bf16[128,16,1024]{2,1,0:T(8,128)(2,1)} async-done(((bf16[128,16,1024]{2,1,0:T(8,128)(2,1)}), bf16[128,16,1024]{2,1,0:T(8,128)(2,1)}, u32[]{:S(2)}, u32[]{:S(2)}) %all-to-all-start.5) | async-done | bytes 4194336 | tf_op jit(solution)/shard_map/all_to_all | solution.py:170
  241.7 5.3 %fusion.99 = f32[512,1024]{1,0:T(8,128)S(1)} fusion(bf16[512,2048]{0,1:T(8,128)(2,1)} %pad_maximum_fusion.10, bf16[2048,1024]{1,0:T(8,128)(2,1)} %bitcast.41), kind=kOutput, calls=%fused_computation.126 | convolution fusion | flops 2147483648 | bytes 8388608 | tf_op jit(solution)/shard_map/dot_general | solution.py:123
  247.0 1.2 fusion.49
  (62 shorter events, 3.0 us)
Async XLA Ops:
  0.0 42.9 %copy-start = (bf16[256,1024]{1,0:T(8,128)(2,1)S(1)}, bf16[256,1024]{1,0:T(8,128)(2,1)}, u32[]{:S(2)}) copy-start(bf16[256,1024]{1,0:T(8,128)(2,1)} %param.16) | copy-start | bytes 1572868
  0.0 31.6 %copy-start.5 = (bf16[2,256,1024]{2,1,0:T(8,128)(2,1)S(1)}, bf16[2,256,1024]{2,1,0:T(8,128)(2,1)}, u32[]{:S(2)}) copy-start(bf16[2,256,1024]{2,1,0:T(8,128)(2,1)} %param.17) | copy-start | bytes 3145732
  3.7 21.4 %all-to-all-start = ((bf16[64,9,128]{2,1,0:T(8,128)(2,1)}), bf16[64,9,128]{2,1,0:T(8,128)(2,1)S(1)}, u32[]{:S(2)}, u32[]{:S(2)}) async-start(bf16[64,9,128]{2,1,0:T(8,128)(2,1)} %reshape.193), calls=%async_computation | async-start | bytes 524288 | tf_op jit(solution)/shard_map/all_to_all | solution.py:49
  26.5 15.1 %all-to-all-start.1 = ((bf16[64,24,128]{2,1,0:T(8,128)(2,1)}), bf16[64,24,128]{2,1,0:T(8,128)(2,1)S(1)}, u32[]{:S(2)}, u32[]{:S(2)}) async-start(bf16[64,24,128]{2,1,0:T(8,128)(2,1)} %reshape.195), calls=%async_computation.1 | async-start | bytes 786432 | tf_op jit(solution)/shard_map/all_to_all | solution.py:57
  44.5 1.0 copy-start.6
  45.6 8.9 %copy-start.7 = (s32[256,8]{0,1:T(8,128)S(1)}, s32[256,8]{0,1:T(8,128)}, u32[]{:S(2)}) copy-start(s32[256,8]{0,1:T(8,128)} %param.23) | copy-start | bytes 24580
  51.3 7.2 %collective-permute-start = (f32[256,2048]{1,0:T(8,128)}, f32[256,2048]{1,0:T(8,128)}, u32[]{:S(2)}, u32[]{:S(2)}) collective-permute-start(f32[256,2048]{1,0:T(8,128)} %convolution_bitcast_fusion), channel_id=1, source_target_pairs={{0,1},{1,0},{2,3},{3,2},{4,5},{5,4},{6,7},{7,6},{8,9},{9,8},{10,11... | collective-permute-start | bytes 6291464 | tf_op jit(solution)/shard_map/ppermute | solution.py:91
  54.8 6.7 %copy-start.8 = (f32[2048]{0:T(1024)S(1)}, f32[2048]{0:T(1024)}, u32[]{:S(2)}) copy-start(f32[2048]{0:T(1024)} %param.22) | copy-start | bytes 24580
  61.7 1.0 copy-start.3
  64.1 23.2 %all-to-all-start.2 = ((bf16[64,8,1024]{2,1,0:T(8,128)(2,1)}), bf16[64,8,1024]{2,1,0:T(8,128)(2,1)}, u32[]{:S(2)}, u32[]{:S(2)}) async-start(bf16[64,8,1024]{2,1,0:T(8,128)(2,1)} %fusion.35), calls=%async_computation.2 | async-start | bytes 2097152 | tf_op jit(solution)/shard_map/all_to_all | solution.py:140
  87.4 55.4 %all-to-all-start.4 = ((bf16[64,16,2048]{2,1,0:T(8,128)(2,1)}), bf16[64,16,2048]{2,1,0:T(8,128)(2,1)}, u32[]{:S(2)}, u32[]{:S(2)}) async-start(bf16[64,16,2048]{2,1,0:T(8,128)(2,1)} %bitcast.157), calls=%async_computation.4 | async-start | bytes 8388608 | tf_op jit(solution)/shard_map/all_to_all | solution.py:160
  93.2 6.3 %collective-permute-start.3 = (bf16[2048,512]{1,0:T(8,128)(2,1)}, bf16[2048,512]{1,0:T(8,128)(2,1)}, u32[]{:S(2)}, u32[]{:S(2)}) collective-permute-start(bf16[2048,512]{1,0:T(8,128)(2,1)} %bitcast.184), channel_id=1, source_target_pairs={{0,1},{1,0},{2,3},{3,2},{4,5},{5,4},{6,7},{7,6},{8,9},{9,8},{10,11... | collective-permute-start | bytes 6291464 | tf_op jit(solution)/shard_map/ppermute | solution.py:40
  99.0 16.2 %collective-permute-start.4 = (bf16[512,2048]{0,1:T(8,128)(2,1)}, bf16[512,2048]{0,1:T(8,128)(2,1)}, u32[]{:S(2)}, u32[]{:S(2)}) collective-permute-start(bf16[512,2048]{0,1:T(8,128)(2,1)} %bitcast.162), channel_id=1, source_target_pairs={{0,1},{1,0},{2,3},{3,2},{4,5},{5,4},{6,7},{7,6},{8,9},{9,8},{10,11... | collective-permute-start | bytes 6291464 | tf_op jit(solution)/shard_map/ppermute | solution.py:41
  99.0 16.1 %collective-permute-start.2 = (bf16[2048,512]{1,0:T(8,128)(2,1)}, bf16[2048,512]{1,0:T(8,128)(2,1)}, u32[]{:S(2)}, u32[]{:S(2)}) collective-permute-start(bf16[2048,512]{1,0:T(8,128)(2,1)} %bitcast.181), channel_id=1, source_target_pairs={{0,1},{1,0},{2,3},{3,2},{4,5},{5,4},{6,7},{7,6},{8,9},{9,8},{10,11... | collective-permute-start | bytes 6291464 | tf_op jit(solution)/shard_map/ppermute | solution.py:39
  99.5 8.5 %collective-permute-start.1 = (bf16[512,1024]{1,0:T(8,128)(2,1)}, bf16[512,1024]{1,0:T(8,128)(2,1)}, u32[]{:S(2)}, u32[]{:S(2)}) collective-permute-start(bf16[512,1024]{1,0:T(8,128)(2,1)} %bitcast.20), channel_id=1, source_target_pairs={{0,1},{1,0},{2,3},{3,2},{4,5},{5,4},{6,7},{7,6},{8,9},{9,8},{10,11... | collective-permute-start | bytes 3145736 | tf_op jit(solution)/shard_map/ppermute | solution.py:142
  142.8 35.3 %all-to-all-start.3 = ((bf16[64,8,1024]{2,1,0:T(8,128)(2,1)}), bf16[64,8,1024]{2,1,0:T(8,128)(2,1)}, u32[]{:S(2)}, u32[]{:S(2)}) async-start(bf16[64,8,1024]{2,1,0:T(8,128)(2,1)} %fusion.36), calls=%async_computation.3 | async-start | bytes 2097152 | tf_op jit(solution)/shard_map/all_to_all | solution.py:153
  152.9 7.7 %copy-start.10 = (bf16[1,2048,512]{2,1,0:T(8,128)(2,1)S(1)}, bf16[1,2048,512]{2,1,0:T(8,128)(2,1)}, u32[]{:S(2)}) copy-start(bf16[1,2048,512]{2,1,0:T(8,128)(2,1)} %param.26) | copy-start | bytes 6291460
  160.7 7.9 %copy-start.4 = (bf16[1,512,2048]{1,2,0:T(8,128)(2,1)S(1)}, bf16[1,512,2048]{1,2,0:T(8,128)(2,1)}, u32[]{:S(2)}) copy-start(bf16[1,512,2048]{1,2,0:T(8,128)(2,1)} %copy.69) | copy-start | bytes 6291460
  178.1 10.9 %copy-start.9 = (f32[256,8]{0,1:T(8,128)S(1)}, f32[256,8]{0,1:T(8,128)}, u32[]{:S(2)}) copy-start(f32[256,8]{0,1:T(8,128)} %param.24) | copy-start | bytes 24580
  178.1 63.6 %all-to-all-start.5 = ((bf16[128,16,1024]{2,1,0:T(8,128)(2,1)}), bf16[128,16,1024]{2,1,0:T(8,128)(2,1)}, u32[]{:S(2)}, u32[]{:S(2)}) async-start(bf16[128,16,1024]{2,1,0:T(8,128)(2,1)} %bitcast.158), calls=%async_computation.5 | async-start | bytes 8388608 | tf_op jit(solution)/shard_map/all_to_all | solution.py:170
  241.7 5.3 %copy-start.2 = (f32[512,1024]{1,0:T(8,128)S(1)}, f32[512,1024]{1,0:T(8,128)}, u32[]{:S(2)}) copy-start(f32[512,1024]{1,0:T(8,128)} %fusion.50) | copy-start | bytes 6291460
  241.7 6.6 %copy-start.1 = (bf16[256,1024]{1,0:T(8,128)(2,1)S(1)}, bf16[256,1024]{1,0:T(8,128)(2,1)}, u32[]{:S(2)}) copy-start(bf16[256,1024]{1,0:T(8,128)(2,1)} %param.16) | copy-start | bytes 1572868
where the time goes:
time: 250 us; the launch traced here: 248 us
  waiting for transfers between devices  105 us (42%)
  matrix products  61.6 us (25%)
  starting transfers between devices  54.7 us (22%)
  other arithmetic  14.8 us (6%)
  local copies, waits for them, and re-layouts  11.2 us (4%)
    all_to_all x1, waiting for transfers between devices, local(): lax.all_to_all(result.reshape(tp_count * experts, first, half), ('tp', 's...  46.1 us
    all_to_all x1, waiting for transfers between devices, local(): lax.all_to_all(outgoing.reshape(experts, first, D), 'seq', 0, 0, tiled=True)  18.2 us
    dot_general x2, matrix products, expert_rows(): up_part = jnp.dot(arrived, up_full, preferred_element_type=jnp.float32)  15 us
    all_to_all x1, waiting for transfers between devices, local(): lax.all_to_all(outgoing.reshape(experts, over, half), 'seq', 0, 0, tiled=...  12.9 us
    all_to_all x1, starting transfers between devices, local(): lax.all_to_all(outbound.reshape(seq_count, -1, 128), 'seq', 0, 0, tiled=T...  12 us
    all_to_all x1, starting transfers between devices, local(): lax.all_to_all(result.reshape(tp_count * experts, first, half), ('tp', 's...  10.8 us
    all_to_all x1, starting transfers between devices, local(): lax.all_to_all(result.reshape(experts, over, half), 'seq', 0, 0, tiled=True)  10.2 us
    dot_general x1, matrix products, local(): jnp.dot(act, lax.dynamic_slice_in_dim(down_cols, tp_index, 1, 1)[:, 0], p...  9.36 us
  transfers between devices with their start and end apart: 11, of which 7 were waited for; matrix products, arithmetic and copies ran while one was open for 24% of the time, Pallas kernels for 0%

commit v1 on v0

--- a/solution.py
+++ b/solution.py
@@ -81,7 +81,7 @@
     probs = jnp.exp(scores - top[:, :, None])
     total = jnp.sum(probs, axis=2)
     accum = jnp.einsum("hqk,khd->hqd", probs, values)
-    attn = (accum / total[:, :, None]).astype(jnp.bfloat16)
+    attn = lax.optimization_barrier((accum / total[:, :, None]).astype(jnp.bfloat16))
     partial_value = jnp.einsum(
         "hqd,hdm->qm",
         attn,

time: 250 us -> 245 us (0.980)
  matrix products: 61.6 us -> 57.3 us
    dot_general x1, matrix products: 5.72 us -> 1.25 us  [local(): jnp.einsum('hqd,hdm->qm', attn, out_weight.reshape(heads_here, HD, D), pr...]
    unnamed x30 -> x32, local copies, waits for them, and re-layouts: 5.97 us -> 6.65 us
where the time goes in v1:
time: 245 us; the launch traced here: 244 us
  waiting for transfers between devices  107 us (44%)
  matrix products  57.3 us (23%)
  starting transfers between devices  54.8 us (22%)
  other arithmetic  14.8 us (6%)
  local copies, waits for them, and re-layouts  9.81 us (4%)
    all_to_all x1, waiting for transfers between devices, local(): lax.all_to_all(result.reshape(tp_count * experts, first, half), ('tp', 's...  46.1 us
    all_to_all x1, waiting for transfers between devices, local(): lax.all_to_all(outgoing.reshape(experts, first, D), 'seq', 0, 0, tiled=True)  18.1 us
    dot_general x2, matrix products, expert_rows(): up_part = jnp.dot(arrived, up_full, preferred_element_type=jnp.float32)  15.1 us
    all_to_all x1, waiting for transfers between devices, local(): lax.all_to_all(outgoing.reshape(experts, over, half), 'seq', 0, 0, tiled=...  12.9 us
    all_to_all x1, starting transfers between devices, local(): lax.all_to_all(outbound.reshape(seq_count, -1, 128), 'seq', 0, 0, tiled=T...  12 us
    all_to_all x1, starting transfers between devices, local(): lax.all_to_all(result.reshape(tp_count * experts, first, half), ('tp', 's...  10.8 us
    all_to_all x1, starting transfers between devices, local(): lax.all_to_all(result.reshape(experts, over, half), 'seq', 0, 0, tiled=True)  10.2 us
    dot_general x1, matrix products, local(): jnp.dot(act, lax.dynamic_slice_in_dim(down_cols, tp_index, 1, 1)[:, 0], p...  9.39 us
  transfers between devices with their start and end apart: 11, of which 7 were waited for; matrix products, arithmetic and copies ran while one was open for 24% of the time, Pallas kernels for 0%

profile of v1, /device:TPU:1, one launch (start us, length us, event | category | flops | bytes accessed | tf_op | source)
XLA Modules:
  0.0 243.8 jit_solution(168280600042458926)
XLA Ops:
  0.0 0.6 compare_reduce_fusion
  0.6 1.3 fusion.75
  2.0 0.9 pad_maximum_fusion.16
  2.9 0.8 reshape.193
  3.7 12.0 %all-to-all-start = ((bf16[64,9,128]{2,1,0:T(8,128)(2,1)}), bf16[64,9,128]{2,1,0:T(8,128)(2,1)S(1)}, u32[]{:S(2)}, u32[]{:S(2)}) async-start(bf16[64,9,128]{2,1,0:T(8,128)(2,1)} %reshape.193), calls=%async_computation | async-start | bytes 524288 | tf_op jit(solution)/shard_map/all_to_all | solution.py:49
  15.7 0.9 select_reduce_fusion.1
  16.5 8.6 %all-to-all-done = bf16[64,9,128]{2,1,0:T(8,128)(2,1)S(1)} async-done(((bf16[64,9,128]{2,1,0:T(8,128)(2,1)}), bf16[64,9,128]{2,1,0:T(8,128)(2,1)S(1)}, u32[]{:S(2)}, u32[]{:S(2)}) %all-to-all-start) | async-done | bytes 147488 | tf_op jit(solution)/shard_map/all_to_all | solution.py:49
  25.3 0.3 convolution_convert_fusion.2
  25.6 0.9 reshape.195
  26.5 4.9 %all-to-all-start.1 = ((bf16[64,24,128]{2,1,0:T(8,128)(2,1)}), bf16[64,24,128]{2,1,0:T(8,128)(2,1)S(1)}, u32[]{:S(2)}, u32[]{:S(2)}) async-start(bf16[64,24,128]{2,1,0:T(8,128)(2,1)} %reshape.195), calls=%async_computation.1 | async-start | bytes 786432 | tf_op jit(solution)/shard_map/all_to_all | solution.py:57
  31.9 0.3 copy.62
  32.4 0.3 copy.67
  32.7 9.0 %all-to-all-done.1 = bf16[64,24,128]{2,1,0:T(8,128)(2,1)S(1)} async-done(((bf16[64,24,128]{2,1,0:T(8,128)(2,1)}), bf16[64,24,128]{2,1,0:T(8,128)(2,1)S(1)}, u32[]{:S(2)}, u32[]{:S(2)}) %all-to-all-start.1) | async-done | bytes 393248 | tf_op jit(solution)/shard_map/all_to_all | solution.py:57
  42.3 0.6 bitcast_reduce_fusion
  42.8 0.6 fusion.5
  43.5 1.1 fusion.42
  44.6 1.0 copy-done.10
  45.7 1.2 convolution_bitcast_fusion
  46.9 3.2 %collective-permute-start = (f32[256,2048]{1,0:T(8,128)S(1)}, f32[256,2048]{1,0:T(8,128)}, u32[]{:S(2)}, u32[]{:S(2)}) collective-permute-start(f32[256,2048]{1,0:T(8,128)S(1)} %convolution_bitcast_fusion), channel_id=1, source_target_pairs={{0,1},{1,0},{2,3},{3,2},{4,5},{5,4},{6,7},{7,6},{8,9},{9,8},{10,11... | collective-permute-start | bytes 6291464 | tf_op jit(solution)/shard_map/ppermute | solution.py:91
  50.5 3.5 %collective-permute-done = f32[256,2048]{1,0:T(8,128)} collective-permute-done((f32[256,2048]{1,0:T(8,128)S(1)}, f32[256,2048]{1,0:T(8,128)}, u32[]{:S(2)}, u32[]{:S(2)}) %collective-permute-start) | collective-permute-done | bytes 2097184 | tf_op jit(solution)/shard_map/ppermute | solution.py:91
  54.0 2.9 %multiply_reduce_fusion = (f32[256]{0:T(256)S(1)}, f32[256,2048]{1,0:T(8,128)S(1)}) fusion(f32[256,2048]{1,0:T(8,128)} %copy-done.5, f32[256,2048]{1,0:T(8,128)} %collective-permute-done, bf16[256,2048]{1,0:T(8,128)(2,1)} %param.15), kind=kLoop, calls=%fused_computation.41 | loop fusion | flops 2621184 | bytes 7341056 | tf_op jit(solution)/shard_map/reduce_sum | solution.py:93
  57.2 1.0 copy-done.3
  58.2 1.5 fusion.35
  59.7 5.5 %all-to-all-start.2 = ((bf16[64,8,1024]{2,1,0:T(8,128)(2,1)}), bf16[64,8,1024]{2,1,0:T(8,128)(2,1)}, u32[]{:S(2)}, u32[]{:S(2)}) async-start(bf16[64,8,1024]{2,1,0:T(8,128)(2,1)} %fusion.35), calls=%async_computation.2 | async-start | bytes 2097152 | tf_op jit(solution)/shard_map/all_to_all | solution.py:140
  65.6 4.4 %convolution_convert_fusion = bf16[1024,2048]{1,0:T(8,128)(2,1)} fusion(pred[256,1024]{0,1:T(32,128)(4,1)S(1)} %fusion.51, bf16[256,2048]{1,0:T(8,128)(2,1)} %copy-done.3), kind=kOutput, calls=%fused_computation.8 | convolution fusion | flops 1075838976 | bytes 5505024 | tf_op jit(solution)/shard_map/ts,td->sd/dot_general | solution.py:157
  70.0 12.9 %all-to-all-done.2 = bf16[64,8,1024]{2,1,0:T(8,128)(2,1)} async-done(((bf16[64,8,1024]{2,1,0:T(8,128)(2,1)}), bf16[64,8,1024]{2,1,0:T(8,128)(2,1)}, u32[]{:S(2)}, u32[]{:S(2)}) %all-to-all-start.2) | async-done | bytes 1048608 | tf_op jit(solution)/shard_map/all_to_all | solution.py:140
  82.9 5.9 %all-to-all-start.4 = ((bf16[64,16,2048]{2,1,0:T(8,128)(2,1)}), bf16[64,16,2048]{2,1,0:T(8,128)(2,1)}, u32[]{:S(2)}, u32[]{:S(2)}) async-start(bf16[64,16,2048]{2,1,0:T(8,128)(2,1)} %bitcast.156), calls=%async_computation.4 | async-start | bytes 8388608 | tf_op jit(solution)/shard_map/all_to_all | solution.py:160
  88.8 1.9 collective-permute-start.3
  90.6 3.9 %copy.69 = bf16[1,512,2048]{1,2,0:T(8,128)(2,1)} copy(bf16[1,512,2048]{2,1,0:T(8,128)(2,1)} %param.27) | data formatting | bytes 4194304 | tf_op args[12]
  94.6 0.5 collective-permute-start.2
  95.1 8.5 %collective-permute-done.1 = bf16[512,1024]{1,0:T(8,128)(2,1)} collective-permute-done((bf16[512,1024]{1,0:T(8,128)(2,1)}, bf16[512,1024]{1,0:T(8,128)(2,1)}, u32[]{:S(2)}, u32[]{:S(2)}) %collective-permute-start.1) | collective-permute-done | bytes 1048608 | tf_op jit(solution)/shard_map/ppermute | solution.py:142
  103.6 7.2 %fusion.2 = f32[512,1024]{1,0:T(8,128)} fusion(bf16[2048,512]{1,0:T(8,128)(2,1)} %collective-permute-done.3, bf16[2048,512]{1,0:T(8,128)(2,1)} %bitcast.184, bf16[512,1024]{1,0:T(8,128)(2,1)} %collective-permute-done.1, bf16[512,1024]{1,0:T(8,128)(2,1)} %bitcast.20, pred[]{:T(512)S(6)} %eq.146), kind=kOutput, calls=%fused_computation.15 | convolution fusion | flops 2165309440 | bytes 8388609 | tf_op jit(solution)/shard_map/dot_general | solution.py:128
  110.8 9.4 %fusion.36 = bf16[64,8,1024]{2,1,0:T(8,128)(2,1)} fusion(s32[]{:T(128)S(6)} %select_n.56, bf16[512,2,1024]{0,2,1:T(8,128)(2,1)} %bitcast.162, bf16[512,2,1024]{0,2,1:T(8,128)(2,1)} %bitcast.25, f32[512,1024]{1,0:T(8,128)} %fusion.2, bf16[2048,512]{1,0:T(8,128)(2,1)} %collective-permute-done.2, bf16[2048,512]{1,0:T(8,128)(2,1)} %bitcast.181, ...), kind=kOutput, calls=%fused_computation.51 | convolution fusion | flops 3246915584 | bytes 13631493 | tf_op jit(solution)/shard_map/dot_general | solution.py:149
  120.2 18.1 %all-to-all-done.4 = bf16[64,16,2048]{2,1,0:T(8,128)(2,1)} async-done(((bf16[64,16,2048]{2,1,0:T(8,128)(2,1)}), bf16[64,16,2048]{2,1,0:T(8,128)(2,1)}, u32[]{:S(2)}, u32[]{:S(2)}) %all-to-all-start.4) | async-done | bytes 4194336 | tf_op jit(solution)/shard_map/all_to_all | solution.py:160
  138.3 10.2 %all-to-all-start.3 = ((bf16[64,8,1024]{2,1,0:T(8,128)(2,1)}), bf16[64,8,1024]{2,1,0:T(8,128)(2,1)}, u32[]{:S(2)}, u32[]{:S(2)}) async-start(bf16[64,8,1024]{2,1,0:T(8,128)(2,1)} %fusion.36), calls=%async_computation.3 | async-start | bytes 2097152 | tf_op jit(solution)/shard_map/all_to_all | solution.py:153
  148.5 7.7 %fusion.3 = f32[1024,1024]{1,0:T(8,128)S(1)} fusion(bf16[1024,2048]{1,0:T(8,128)(2,1)} %bitcast.35, bf16[2048,512]{1,0:T(8,128)(2,1)} %collective-permute-done.2, bf16[2048,512]{1,0:T(8,128)(2,1)} %bitcast.182), kind=kOutput, calls=%fused_computation.16 | convolution fusion | flops 4303355904 | bytes 12582912 | tf_op jit(solution)/shard_map/dot_general | solution.py:127
  156.2 7.8 %multiply_convert_fusion = bf16[1024,1024]{1,0:T(8,128)(2,1)S(1)} fusion(f32[1024,1024]{1,0:T(8,128)S(1)} %fusion.3, bf16[1024,2048]{1,0:T(8,128)(2,1)} %bitcast.35, bf16[2048,512]{1,0:T(8,128)(2,1)} %collective-permute-done.3, bf16[2048,512]{1,0:T(8,128)(2,1)S(1)} %bitcast.185), kind=kOutput, calls=%fused_computation.7 | convolution fusion | flops 4309647360 | bytes 14680064 | tf_op jit(solution)/shard_map/dot_general | solution.py:128
  164.1 3.6 %convert_bitcast_fusion.1 = bf16[1,1024,1024]{2,1,0:T(8,128)(2,1)S(1)} fusion(bf16[1024,1024]{1,0:T(8,128)(2,1)S(1)} %multiply_convert_fusion, bf16[512,2,1024]{0,2,1:T(8,128)(2,1)S(1)} %bitcast.163, bf16[512,2,1024]{0,2,1:T(8,128)(2,1)} %bitcast.25), kind=kOutput, calls=%fused_computation.38 | convolution fusion | flops 2152726528 | bytes 8388608 | tf_op jit(solution)/shard_map/dot_general | solution.py:166
  167.7 3.6 %convert_bitcast_fusion = bf16[1,1024,1024]{2,1,0:T(8,128)(2,1)S(1)} fusion(bf16[1024,1024]{1,0:T(8,128)(2,1)S(1)} %multiply_convert_fusion, bf16[512,2,1024]{0,2,1:T(8,128)(2,1)} %bitcast.25, bf16[512,2,1024]{0,2,1:T(8,128)(2,1)S(1)} %bitcast.164), kind=kOutput, calls=%fused_computation.37 | convolution fusion | flops 2152726528 | bytes 8388608 | tf_op jit(solution)/shard_map/dot_general | solution.py:166
  171.4 2.3 pad_maximum_fusion.2
  173.7 10.8 %all-to-all-start.5 = ((bf16[128,16,1024]{2,1,0:T(8,128)(2,1)}), bf16[128,16,1024]{2,1,0:T(8,128)(2,1)}, u32[]{:S(2)}, u32[]{:S(2)}) async-start(bf16[128,16,1024]{2,1,0:T(8,128)(2,1)} %bitcast.157), calls=%async_computation.5 | async-start | bytes 8388608 | tf_op jit(solution)/shard_map/all_to_all | solution.py:170
  184.6 0.6 fusion.21
  185.2 0.7 fusion.22
  186.4 1.5 pad_maximum_fusion.10
  187.9 3.3 %fusion.48 = f32[512,1024]{1,0:T(8,128)} fusion(bf16[512,512]{0,1:T(8,128)(2,1)S(1)} %pad_maximum_fusion.15, bf16[64,8,1024]{2,1,0:T(8,128)(2,1)} %all-to-all-done.3), kind=kOutput, calls=%fused_computation.62 | convolution fusion | flops 536870912 | bytes 3670016 | tf_op jit(solution)/shard_map/dot_general | solution.py:123
  191.2 46.1 %all-to-all-done.5 = bf16[128,16,1024]{2,1,0:T(8,128)(2,1)} async-done(((bf16[128,16,1024]{2,1,0:T(8,128)(2,1)}), bf16[128,16,1024]{2,1,0:T(8,128)(2,1)}, u32[]{:S(2)}, u32[]{:S(2)}) %all-to-all-start.5) | async-done | bytes 4194336 | tf_op jit(solution)/shard_map/all_to_all | solution.py:170
  237.2 5.3 %fusion.90 = f32[512,1024]{1,0:T(8,128)S(1)} fusion(bf16[512,2048]{0,1:T(8,128)(2,1)} %pad_maximum_fusion.10, bf16[2048,1024]{1,0:T(8,128)(2,1)} %bitcast.41), kind=kOutput, calls=%fused_computation.125 | convolution fusion | flops 2147483648 | bytes 8388608 | tf_op jit(solution)/shard_map/dot_general | solution.py:123
  242.6 1.2 fusion.47
  (65 shorter events, 3.1 us)
Async XLA Ops:
  0.0 42.3 %copy-start = (bf16[256,1024]{1,0:T(8,128)(2,1)S(1)}, bf16[256,1024]{1,0:T(8,128)(2,1)}, u32[]{:S(2)}) copy-start(bf16[256,1024]{1,0:T(8,128)(2,1)} %param.16) | copy-start | bytes 1572868
  0.0 31.6 %copy-start.6 = (bf16[2,256,1024]{2,1,0:T(8,128)(2,1)S(1)}, bf16[2,256,1024]{2,1,0:T(8,128)(2,1)}, u32[]{:S(2)}) copy-start(bf16[2,256,1024]{2,1,0:T(8,128)(2,1)} %param.17) | copy-start | bytes 3145732
  3.7 21.4 %all-to-all-start = ((bf16[64,9,128]{2,1,0:T(8,128)(2,1)}), bf16[64,9,128]{2,1,0:T(8,128)(2,1)S(1)}, u32[]{:S(2)}, u32[]{:S(2)}) async-start(bf16[64,9,128]{2,1,0:T(8,128)(2,1)} %reshape.193), calls=%async_computation | async-start | bytes 524288 | tf_op jit(solution)/shard_map/all_to_all | solution.py:49
  26.5 15.1 %all-to-all-start.1 = ((bf16[64,24,128]{2,1,0:T(8,128)(2,1)}), bf16[64,24,128]{2,1,0:T(8,128)(2,1)S(1)}, u32[]{:S(2)}, u32[]{:S(2)}) async-start(bf16[64,24,128]{2,1,0:T(8,128)(2,1)} %reshape.195), calls=%async_computation.1 | async-start | bytes 786432 | tf_op jit(solution)/shard_map/all_to_all | solution.py:57
  43.5 2.2 copy-start.10
  45.7 4.6 %copy-start.7 = (s32[256,8]{0,1:T(8,128)S(1)}, s32[256,8]{0,1:T(8,128)}, u32[]{:S(2)}) copy-start(s32[256,8]{0,1:T(8,128)} %param.23) | copy-start | bytes 24580
  46.9 3.6 %copy-start.5 = (f32[256,2048]{1,0:T(8,128)}, f32[256,2048]{1,0:T(8,128)S(1)}, u32[]{:S(2)}) copy-start(f32[256,2048]{1,0:T(8,128)S(1)} %convolution_bitcast_fusion) | copy-start | bytes 6291460
  46.9 7.1 %collective-permute-start = (f32[256,2048]{1,0:T(8,128)S(1)}, f32[256,2048]{1,0:T(8,128)}, u32[]{:S(2)}, u32[]{:S(2)}) collective-permute-start(f32[256,2048]{1,0:T(8,128)S(1)} %convolution_bitcast_fusion), channel_id=1, source_target_pairs={{0,1},{1,0},{2,3},{3,2},{4,5},{5,4},{6,7},{7,6},{8,9},{9,8},{10,11... | collective-permute-start | bytes 6291464 | tf_op jit(solution)/shard_map/ppermute | solution.py:91
  50.5 6.4 %copy-start.8 = (f32[2048]{0:T(1024)S(1)}, f32[2048]{0:T(1024)}, u32[]{:S(2)}) copy-start(f32[2048]{0:T(1024)} %param.22) | copy-start | bytes 24580
  57.2 1.0 copy-start.3
  59.7 23.2 %all-to-all-start.2 = ((bf16[64,8,1024]{2,1,0:T(8,128)(2,1)}), bf16[64,8,1024]{2,1,0:T(8,128)(2,1)}, u32[]{:S(2)}, u32[]{:S(2)}) async-start(bf16[64,8,1024]{2,1,0:T(8,128)(2,1)} %fusion.35), calls=%async_computation.2 | async-start | bytes 2097152 | tf_op jit(solution)/shard_map/all_to_all | solution.py:140
  82.9 55.4 %all-to-all-start.4 = ((bf16[64,16,2048]{2,1,0:T(8,128)(2,1)}), bf16[64,16,2048]{2,1,0:T(8,128)(2,1)}, u32[]{:S(2)}, u32[]{:S(2)}) async-start(bf16[64,16,2048]{2,1,0:T(8,128)(2,1)} %bitcast.156), calls=%async_computation.4 | async-start | bytes 8388608 | tf_op jit(solution)/shard_map/all_to_all | solution.py:160
  88.8 6.3 %collective-permute-start.3 = (bf16[2048,512]{1,0:T(8,128)(2,1)}, bf16[2048,512]{1,0:T(8,128)(2,1)}, u32[]{:S(2)}, u32[]{:S(2)}) collective-permute-start(bf16[2048,512]{1,0:T(8,128)(2,1)} %bitcast.183), channel_id=1, source_target_pairs={{0,1},{1,0},{2,3},{3,2},{4,5},{5,4},{6,7},{7,6},{8,9},{9,8},{10,11... | collective-permute-start | bytes 6291464 | tf_op jit(solution)/shard_map/ppermute | solution.py:40
  94.6 16.2 %collective-permute-start.4 = (bf16[512,2048]{0,1:T(8,128)(2,1)}, bf16[512,2048]{0,1:T(8,128)(2,1)}, u32[]{:S(2)}, u32[]{:S(2)}) collective-permute-start(bf16[512,2048]{0,1:T(8,128)(2,1)} %bitcast.161), channel_id=1, source_target_pairs={{0,1},{1,0},{2,3},{3,2},{4,5},{5,4},{6,7},{7,6},{8,9},{9,8},{10,11... | collective-permute-start | bytes 6291464 | tf_op jit(solution)/shard_map/ppermute | solution.py:41
  94.6 16.2 %collective-permute-start.2 = (bf16[2048,512]{1,0:T(8,128)(2,1)}, bf16[2048,512]{1,0:T(8,128)(2,1)}, u32[]{:S(2)}, u32[]{:S(2)}) collective-permute-start(bf16[2048,512]{1,0:T(8,128)(2,1)} %bitcast.180), channel_id=1, source_target_pairs={{0,1},{1,0},{2,3},{3,2},{4,5},{5,4},{6,7},{7,6},{8,9},{9,8},{10,11... | collective-permute-start | bytes 6291464 | tf_op jit(solution)/shard_map/ppermute | solution.py:39
  95.1 8.5 %collective-permute-start.1 = (bf16[512,1024]{1,0:T(8,128)(2,1)}, bf16[512,1024]{1,0:T(8,128)(2,1)}, u32[]{:S(2)}, u32[]{:S(2)}) collective-permute-start(bf16[512,1024]{1,0:T(8,128)(2,1)} %bitcast.20), channel_id=1, source_target_pairs={{0,1},{1,0},{2,3},{3,2},{4,5},{5,4},{6,7},{7,6},{8,9},{9,8},{10,11... | collective-permute-start | bytes 3145736 | tf_op jit(solution)/shard_map/ppermute | solution.py:142
  138.3 35.4 %all-to-all-start.3 = ((bf16[64,8,1024]{2,1,0:T(8,128)(2,1)}), bf16[64,8,1024]{2,1,0:T(8,128)(2,1)}, u32[]{:S(2)}, u32[]{:S(2)}) async-start(bf16[64,8,1024]{2,1,0:T(8,128)(2,1)} %fusion.36), calls=%async_computation.3 | async-start | bytes 2097152 | tf_op jit(solution)/shard_map/all_to_all | solution.py:153
  148.5 7.7 %copy-start.11 = (bf16[1,2048,512]{2,1,0:T(8,128)(2,1)S(1)}, bf16[1,2048,512]{2,1,0:T(8,128)(2,1)}, u32[]{:S(2)}) copy-start(bf16[1,2048,512]{2,1,0:T(8,128)(2,1)} %param.26) | copy-start | bytes 6291460
  156.2 7.9 %copy-start.4 = (bf16[1,512,2048]{1,2,0:T(8,128)(2,1)S(1)}, bf16[1,512,2048]{1,2,0:T(8,128)(2,1)}, u32[]{:S(2)}) copy-start(bf16[1,512,2048]{1,2,0:T(8,128)(2,1)} %copy.69) | copy-start | bytes 6291460
  173.7 10.9 %copy-start.9 = (f32[256,8]{0,1:T(8,128)S(1)}, f32[256,8]{0,1:T(8,128)}, u32[]{:S(2)}) copy-start(f32[256,8]{0,1:T(8,128)} %param.24) | copy-start | bytes 24580
  173.7 63.5 %all-to-all-start.5 = ((bf16[128,16,1024]{2,1,0:T(8,128)(2,1)}), bf16[128,16,1024]{2,1,0:T(8,128)(2,1)}, u32[]{:S(2)}, u32[]{:S(2)}) async-start(bf16[128,16,1024]{2,1,0:T(8,128)(2,1)} %bitcast.157), calls=%async_computation.5 | async-start | bytes 8388608 | tf_op jit(solution)/shard_map/all_to_all | solution.py:170
  237.2 5.3 %copy-start.2 = (f32[512,1024]{1,0:T(8,128)S(1)}, f32[512,1024]{1,0:T(8,128)}, u32[]{:S(2)}) copy-start(f32[512,1024]{1,0:T(8,128)} %fusion.48) | copy-start | bytes 6291460
  237.2 6.6 %copy-start.1 = (bf16[256,1024]{1,0:T(8,128)(2,1)S(1)}, bf16[256,1024]{1,0:T(8,128)(2,1)}, u32[]{:S(2)}) copy-start(bf16[256,1024]{1,0:T(8,128)(2,1)} %param.16) | copy-start | bytes 1572868

commit v2 on v1

--- a/solution.py
+++ b/solution.py
@@ -95,7 +95,6 @@
 
     experts = w_gate.shape[0] * seq_count
     cap = 5 * rows * TOPK // (4 * experts)
-    share = -(-(-(-cap // tp_count)) // 8) * 8
     hit = expert_ids[:, :, None] == jnp.arange(experts, dtype=jnp.int32)[None, None, :]
     chosen = jnp.any(hit, axis=1)
     weight_of = jnp.sum(jnp.where(hit, gates[:, :, None], 0.0), axis=1)
@@ -123,9 +122,13 @@
         parts = jnp.dot(both, back, preferred_element_type=jnp.float32)
         return parts[:rows] + parts[rows:]
 
+    gate_up = jnp.concatenate([gate_full, up_full], 1)
+    hidden_units = gate_full.shape[1]
+
     def expert_rows(arrived):
-        gate_part = jnp.dot(arrived, gate_full, preferred_element_type=jnp.float32)
-        up_part = jnp.dot(arrived, up_full, preferred_element_type=jnp.float32)
+        both_parts = jnp.dot(arrived, gate_up, preferred_element_type=jnp.float32)
+        gate_part = both_parts[:, :hidden_units]
+        up_part = both_parts[:, hidden_units:]
         return (jax.nn.silu(gate_part) * up_part).astype(jnp.bfloat16)
 
     def select(wanted):

time: 245 us -> 244 us (level)
  matrix products: 57.3 us -> 53.1 us
    ppermute x1, waiting for transfers between devices: 8.46 us -> 1.5 us  [local(): partner = lax.ppermute(arrived, 'tp', swap)]
    dot_general x1, matrix products: 9.39 us -> 3.54 us  [local(): jnp.dot(act, lax.dynamic_slice_in_dim(down_cols, tp_index, 1, 1)[:, 0], p...]
    all_to_all x1, waiting for transfers between devices: 18.1 us -> 24 us  [local(): lax.all_to_all(outgoing.reshape(experts, first, D), 'seq', 0, 0, tiled=True)]
    ppermute x1, waiting for transfers between devices: 0.01 us -> 2.6 us  [local(): lax.ppermute(w_gate[0], 'tp', swap)]
    dot_general x3 -> x2, matrix products: 22.8 us -> 24.4 us  [expert_rows(): both_parts = jnp.dot(arrived, gate_up, preferred_element_type=jnp.float32)]
  transfers between devices with their start and end apart: 11 -> 11, of which waited for: 7 -> 8; matrix products, arithmetic and copies ran while one was open for 24% -> 23% of each run, Pallas kernels for 0% -> 0%
where the time goes in v2:
time: 244 us; the launch traced here: 243 us
  waiting for transfers between devices  108 us (44%)
  starting transfers between devices  54.8 us (22%)
  matrix products  53.1 us (22%)
  other arithmetic  16.1 us (7%)
  local copies, waits for them, and re-layouts  10 us (4%)
    all_to_all x1, waiting for transfers between devices, local(): lax.all_to_all(result.reshape(tp_count * experts, first, half), ('tp', 's...  46.1 us
    dot_general x2, matrix products, expert_rows(): both_parts = jnp.dot(arrived, gate_up, preferred_element_type=jnp.float32)  24.4 us
    all_to_all x1, waiting for transfers between devices, local(): lax.all_to_all(outgoing.reshape(experts, first, D), 'seq', 0, 0, tiled=True)  24 us
    all_to_all x1, waiting for transfers between devices, local(): lax.all_to_all(outgoing.reshape(experts, over, half), 'seq', 0, 0, tiled=...  12.9 us
    all_to_all x1, starting transfers between devices, local(): lax.all_to_all(outbound.reshape(seq_count, -1, 128), 'seq', 0, 0, tiled=T...  12 us
    all_to_all x1, starting transfers between devices, local(): lax.all_to_all(result.reshape(tp_count * experts, first, half), ('tp', 's...  10.8 us
    all_to_all x1, starting transfers between devices, local(): lax.all_to_all(result.reshape(experts, over, half), 'seq', 0, 0, tiled=True)  10.2 us
    all_to_all x1, waiting for transfers between devices, local(): lax.all_to_all(picked.reshape(seq_count, depth * piece // 128, 128), 'seq...  8.97 us
  transfers between devices with their start and end apart: 11, of which 8 were waited for; matrix products, arithmetic and copies ran while one was open for 23% of the time, Pallas kernels for 0%

profile of v2, /device:TPU:1, one launch (start us, length us, event | category | flops | bytes accessed | tf_op | source)
XLA Modules:
  0.0 242.6 jit_solution(13990208322791366661)
XLA Ops:
  0.0 0.6 compare_reduce_fusion
  0.6 1.3 fusion.82
  2.0 0.9 pad_maximum_fusion.7
  2.9 0.8 reshape.193
  3.7 12.0 %all-to-all-start = ((bf16[64,9,128]{2,1,0:T(8,128)(2,1)}), bf16[64,9,128]{2,1,0:T(8,128)(2,1)S(1)}, u32[]{:S(2)}, u32[]{:S(2)}) async-start(bf16[64,9,128]{2,1,0:T(8,128)(2,1)} %reshape.193), calls=%async_computation | async-start | bytes 524288 | tf_op jit(solution)/shard_map/all_to_all | solution.py:49
  15.7 0.9 select_reduce_fusion.1
  16.5 8.6 %all-to-all-done = bf16[64,9,128]{2,1,0:T(8,128)(2,1)S(1)} async-done(((bf16[64,9,128]{2,1,0:T(8,128)(2,1)}), bf16[64,9,128]{2,1,0:T(8,128)(2,1)S(1)}, u32[]{:S(2)}, u32[]{:S(2)}) %all-to-all-start) | async-done | bytes 147488 | tf_op jit(solution)/shard_map/all_to_all | solution.py:49
  25.3 0.3 convolution_convert_fusion.2
  25.6 0.9 reshape.195
  26.5 4.9 %all-to-all-start.1 = ((bf16[64,24,128]{2,1,0:T(8,128)(2,1)}), bf16[64,24,128]{2,1,0:T(8,128)(2,1)S(1)}, u32[]{:S(2)}, u32[]{:S(2)}) async-start(bf16[64,24,128]{2,1,0:T(8,128)(2,1)} %reshape.195), calls=%async_computation.1 | async-start | bytes 786432 | tf_op jit(solution)/shard_map/all_to_all | solution.py:57
  32.4 0.3 copy.67
  32.7 9.0 %all-to-all-done.1 = bf16[64,24,128]{2,1,0:T(8,128)(2,1)S(1)} async-done(((bf16[64,24,128]{2,1,0:T(8,128)(2,1)}), bf16[64,24,128]{2,1,0:T(8,128)(2,1)S(1)}, u32[]{:S(2)}, u32[]{:S(2)}) %all-to-all-start.1) | async-done | bytes 393248 | tf_op jit(solution)/shard_map/all_to_all | solution.py:57
  42.3 0.6 bitcast_reduce_fusion
  42.8 0.6 fusion.2
  43.5 1.1 fusion.48
  44.6 1.0 copy-done.11
  45.7 1.2 convolution_bitcast_fusion
  46.9 3.2 %collective-permute-start = (f32[256,2048]{1,0:T(8,128)S(1)}, f32[256,2048]{1,0:T(8,128)}, u32[]{:S(2)}, u32[]{:S(2)}) collective-permute-start(f32[256,2048]{1,0:T(8,128)S(1)} %convolution_bitcast_fusion), channel_id=1, source_target_pairs={{0,1},{1,0},{2,3},{3,2},{4,5},{5,4},{6,7},{7,6},{8,9},{9,8},{10,11... | collective-permute-start | bytes 6291464 | tf_op jit(solution)/shard_map/ppermute | solution.py:91
  50.5 3.5 %collective-permute-done = f32[256,2048]{1,0:T(8,128)} collective-permute-done((f32[256,2048]{1,0:T(8,128)S(1)}, f32[256,2048]{1,0:T(8,128)}, u32[]{:S(2)}, u32[]{:S(2)}) %collective-permute-start) | collective-permute-done | bytes 2097184 | tf_op jit(solution)/shard_map/ppermute | solution.py:91
  54.0 2.9 %multiply_reduce_fusion = (f32[256]{0:T(256)S(1)}, f32[256,2048]{1,0:T(8,128)S(1)}) fusion(f32[256,2048]{1,0:T(8,128)} %copy-done.6, f32[256,2048]{1,0:T(8,128)} %collective-permute-done, bf16[256,2048]{1,0:T(8,128)(2,1)} %param.15), kind=kLoop, calls=%fused_computation.44 | loop fusion | flops 2621184 | bytes 7341056 | tf_op jit(solution)/shard_map/reduce_sum | solution.py:93
  57.2 1.0 copy-done.3
  58.2 1.5 fusion.41
  59.7 5.5 %all-to-all-start.2 = ((bf16[64,8,1024]{2,1,0:T(8,128)(2,1)}), bf16[64,8,1024]{2,1,0:T(8,128)(2,1)}, u32[]{:S(2)}, u32[]{:S(2)}) async-start(bf16[64,8,1024]{2,1,0:T(8,128)(2,1)} %fusion.41), calls=%async_computation.2 | async-start | bytes 2097152 | tf_op jit(solution)/shard_map/all_to_all | solution.py:143
  65.5 4.4 %convolution_convert_fusion = bf16[1024,2048]{1,0:T(8,128)(2,1)} fusion(pred[256,1024]{0,1:T(32,128)(4,1)S(1)} %fusion.58, bf16[256,2048]{1,0:T(8,128)(2,1)} %copy-done.3), kind=kOutput, calls=%fused_computation.8 | convolution fusion | flops 1075838976 | bytes 5505024 | tf_op jit(solution)/shard_map/ts,td->sd/dot_general | solution.py:160
  70.0 12.9 %all-to-all-done.2 = bf16[64,8,1024]{2,1,0:T(8,128)(2,1)} async-done(((bf16[64,8,1024]{2,1,0:T(8,128)(2,1)}), bf16[64,8,1024]{2,1,0:T(8,128)(2,1)}, u32[]{:S(2)}, u32[]{:S(2)}) %all-to-all-start.2) | async-done | bytes 1048608 | tf_op jit(solution)/shard_map/all_to_all | solution.py:143
  82.9 5.8 %all-to-all-start.4 = ((bf16[64,16,2048]{2,1,0:T(8,128)(2,1)}), bf16[64,16,2048]{2,1,0:T(8,128)(2,1)}, u32[]{:S(2)}, u32[]{:S(2)}) async-start(bf16[64,16,2048]{2,1,0:T(8,128)(2,1)} %bitcast.155), calls=%async_computation.4 | async-start | bytes 8388608 | tf_op jit(solution)/shard_map/all_to_all | solution.py:163
  88.7 1.9 collective-permute-start.3
  90.7 0.4 collective-permute-start.1
  91.1 3.9 %copy.69 = bf16[1,512,2048]{1,2,0:T(8,128)(2,1)} copy(bf16[1,512,2048]{2,1,0:T(8,128)(2,1)} %param.27) | data formatting | bytes 4194304 | tf_op args[12]
  95.1 2.6 %collective-permute-done.2 = bf16[2048,512]{1,0:T(8,128)(2,1)} collective-permute-done((bf16[2048,512]{1,0:T(8,128)(2,1)}, bf16[2048,512]{1,0:T(8,128)(2,1)}, u32[]{:S(2)}, u32[]{:S(2)}) %collective-permute-start.2) | collective-permute-done | bytes 2097184 | tf_op jit(solution)/shard_map/ppermute | solution.py:39
  97.7 1.5 collective-permute-done.1
  99.2 11.5 %fusion.18 = f32[512,2048]{1,0:T(8,128)S(1)} fusion(bf16[512,1024]{1,0:T(8,128)(2,1)} %collective-permute-done.1, bf16[512,1024]{1,0:T(8,128)(2,1)} %bitcast.20, pred[]{:T(512)S(6)} %eq.146, bf16[2048,512]{1,0:T(8,128)(2,1)} %collective-permute-done.3, bf16[2048,512]{1,0:T(8,128)(2,1)} %bitcast.180, bf16[2048,512]{1,0:T(8,128)(2,1)} %collective-permute-done.2, ...), kind=kOutput, calls=%fused_computation.29 | convolution fusion | flops 4337958912 | bytes 14680065 | tf_op jit(solution)/shard_map/dot_general | solution.py:129
  110.8 3.5 %fusion.42 = bf16[64,8,1024]{2,1,0:T(8,128)(2,1)} fusion(s32[]{:T(128)S(6)} %select_n.56, bf16[512,2,1024]{0,2,1:T(8,128)(2,1)S(1)} %bitcast.161, bf16[512,2,1024]{0,2,1:T(8,128)(2,1)} %bitcast.25, f32[512,2048]{1,0:T(8,128)S(1)} %fusion.18), kind=kOutput, calls=%fused_computation.56 | convolution fusion | flops 1081606144 | bytes 9437188 | tf_op jit(solution)/shard_map/dot_general | solution.py:152
  114.3 24.0 %all-to-all-done.4 = bf16[64,16,2048]{2,1,0:T(8,128)(2,1)} async-done(((bf16[64,16,2048]{2,1,0:T(8,128)(2,1)}), bf16[64,16,2048]{2,1,0:T(8,128)(2,1)}, u32[]{:S(2)}, u32[]{:S(2)}) %all-to-all-start.4) | async-done | bytes 4194336 | tf_op jit(solution)/shard_map/all_to_all | solution.py:163
  138.3 10.2 %all-to-all-start.3 = ((bf16[64,8,1024]{2,1,0:T(8,128)(2,1)}), bf16[64,8,1024]{2,1,0:T(8,128)(2,1)}, u32[]{:S(2)}, u32[]{:S(2)}) async-start(bf16[64,8,1024]{2,1,0:T(8,128)(2,1)} %fusion.42), calls=%async_computation.3 | async-start | bytes 2097152 | tf_op jit(solution)/shard_map/all_to_all | solution.py:156
  148.5 12.9 %fusion.40 = f32[1024,2048]{1,0:T(8,128)S(1)} fusion(bf16[1024,2048]{1,0:T(8,128)(2,1)} %bitcast.35, bf16[2048,512]{1,0:T(8,128)(2,1)} %collective-permute-done.3, bf16[2048,512]{1,0:T(8,128)(2,1)} %bitcast.181, bf16[2048,512]{1,0:T(8,128)(2,1)} %collective-permute-done.2, bf16[2048,512]{1,0:T(8,128)(2,1)} %bitcast.184), kind=kOutput, calls=%fused_computation.54 | convolution fusion | flops 8623489024 | bytes 20971520 | tf_op jit(solution)/shard_map/dot_general | solution.py:129
  161.4 1.4 fusion
  163.0 3.6 %convert_bitcast_fusion = bf16[1,1024,1024]{2,1,0:T(8,128)(2,1)S(1)} fusion(bf16[1024,1024]{1,0:T(8,128)(2,1)S(1)} %fusion, bf16[512,2,1024]{0,2,1:T(8,128)(2,1)} %bitcast.25, bf16[512,2,1024]{0,2,1:T(8,128)(2,1)S(1)} %bitcast.162), kind=kOutput, calls=%fused_computation.41 | convolution fusion | flops 2152726528 | bytes 8388608 | tf_op jit(solution)/shard_map/dot_general | solution.py:169
  166.6 3.6 %convert_bitcast_fusion.1 = bf16[1,1024,1024]{2,1,0:T(8,128)(2,1)S(1)} fusion(bf16[1024,1024]{1,0:T(8,128)(2,1)S(1)} %fusion, bf16[512,2,1024]{0,2,1:T(8,128)(2,1)S(1)} %bitcast.163, bf16[512,2,1024]{0,2,1:T(8,128)(2,1)} %bitcast.25), kind=kOutput, calls=%fused_computation.42 | convolution fusion | flops 2152726528 | bytes 8388608 | tf_op jit(solution)/shard_map/dot_general | solution.py:169
  170.1 2.3 pad_maximum_fusion.1
  172.5 10.8 %all-to-all-start.5 = ((bf16[128,16,1024]{2,1,0:T(8,128)(2,1)}), bf16[128,16,1024]{2,1,0:T(8,128)(2,1)}, u32[]{:S(2)}, u32[]{:S(2)}) async-start(bf16[128,16,1024]{2,1,0:T(8,128)(2,1)} %bitcast.156), calls=%async_computation.5 | async-start | bytes 8388608 | tf_op jit(solution)/shard_map/all_to_all | solution.py:173
  183.4 0.7 fusion.26
  184.1 0.6 fusion.25
  184.7 1.5 pad_maximum_fusion.3
  186.7 3.3 %fusion.55 = f32[512,1024]{1,0:T(8,128)} fusion(bf16[512,512]{0,1:T(8,128)(2,1)S(1)} %pad_maximum_fusion.6, bf16[64,8,1024]{2,1,0:T(8,128)(2,1)} %all-to-all-done.3), kind=kOutput, calls=%fused_computation.67 | convolution fusion | flops 536870912 | bytes 3670016 | tf_op jit(solution)/shard_map/dot_general | solution.py:122
  190.0 46.1 %all-to-all-done.5 = bf16[128,16,1024]{2,1,0:T(8,128)(2,1)} async-done(((bf16[128,16,1024]{2,1,0:T(8,128)(2,1)}), bf16[128,16,1024]{2,1,0:T(8,128)(2,1)}, u32[]{:S(2)}, u32[]{:S(2)}) %all-to-all-start.5) | async-done | bytes 4194336 | tf_op jit(solution)/shard_map/all_to_all | solution.py:173
  236.0 5.3 %fusion.95 = f32[512,1024]{1,0:T(8,128)S(1)} fusion(bf16[512,2048]{0,1:T(8,128)(2,1)} %pad_maximum_fusion.3, bf16[2048,1024]{1,0:T(8,128)(2,1)} %bitcast.41), kind=kOutput, calls=%fused_computation.129 | convolution fusion | flops 2147483648 | bytes 8388608 | tf_op jit(solution)/shard_map/dot_general | solution.py:122
  241.3 1.2 fusion.54
  (65 shorter events, 3.7 us)
Async XLA Ops:
  0.0 42.3 %copy-start = (bf16[256,1024]{1,0:T(8,128)(2,1)S(1)}, bf16[256,1024]{1,0:T(8,128)(2,1)}, u32[]{:S(2)}) copy-start(bf16[256,1024]{1,0:T(8,128)(2,1)} %param.16) | copy-start | bytes 1572868
  0.0 31.6 %copy-start.7 = (bf16[2,256,1024]{2,1,0:T(8,128)(2,1)S(1)}, bf16[2,256,1024]{2,1,0:T(8,128)(2,1)}, u32[]{:S(2)}) copy-start(bf16[2,256,1024]{2,1,0:T(8,128)(2,1)} %param.17) | copy-start | bytes 3145732
  3.7 21.4 %all-to-all-start = ((bf16[64,9,128]{2,1,0:T(8,128)(2,1)}), bf16[64,9,128]{2,1,0:T(8,128)(2,1)S(1)}, u32[]{:S(2)}, u32[]{:S(2)}) async-start(bf16[64,9,128]{2,1,0:T(8,128)(2,1)} %reshape.193), calls=%async_computation | async-start | bytes 524288 | tf_op jit(solution)/shard_map/all_to_all | solution.py:49
  26.5 15.1 %all-to-all-start.1 = ((bf16[64,24,128]{2,1,0:T(8,128)(2,1)}), bf16[64,24,128]{2,1,0:T(8,128)(2,1)S(1)}, u32[]{:S(2)}, u32[]{:S(2)}) async-start(bf16[64,24,128]{2,1,0:T(8,128)(2,1)} %reshape.195), calls=%async_computation.1 | async-start | bytes 786432 | tf_op jit(solution)/shard_map/all_to_all | solution.py:57
  43.5 2.2 copy-start.11
  45.7 4.6 %copy-start.8 = (s32[256,8]{0,1:T(8,128)S(1)}, s32[256,8]{0,1:T(8,128)}, u32[]{:S(2)}) copy-start(s32[256,8]{0,1:T(8,128)} %param.23) | copy-start | bytes 24580
  46.9 3.6 %copy-start.6 = (f32[256,2048]{1,0:T(8,128)}, f32[256,2048]{1,0:T(8,128)S(1)}, u32[]{:S(2)}) copy-start(f32[256,2048]{1,0:T(8,128)S(1)} %convolution_bitcast_fusion) | copy-start | bytes 6291460
  46.9 7.1 %collective-permute-start = (f32[256,2048]{1,0:T(8,128)S(1)}, f32[256,2048]{1,0:T(8,128)}, u32[]{:S(2)}, u32[]{:S(2)}) collective-permute-start(f32[256,2048]{1,0:T(8,128)S(1)} %convolution_bitcast_fusion), channel_id=1, source_target_pairs={{0,1},{1,0},{2,3},{3,2},{4,5},{5,4},{6,7},{7,6},{8,9},{9,8},{10,11... | collective-permute-start | bytes 6291464 | tf_op jit(solution)/shard_map/ppermute | solution.py:91
  50.5 6.4 %copy-start.9 = (f32[2048]{0:T(1024)S(1)}, f32[2048]{0:T(1024)}, u32[]{:S(2)}) copy-start(f32[2048]{0:T(1024)} %param.22) | copy-start | bytes 24580
  57.2 1.0 copy-start.3
  59.7 23.2 %all-to-all-start.2 = ((bf16[64,8,1024]{2,1,0:T(8,128)(2,1)}), bf16[64,8,1024]{2,1,0:T(8,128)(2,1)}, u32[]{:S(2)}, u32[]{:S(2)}) async-start(bf16[64,8,1024]{2,1,0:T(8,128)(2,1)} %fusion.41), calls=%async_computation.2 | async-start | bytes 2097152 | tf_op jit(solution)/shard_map/all_to_all | solution.py:143
  82.9 55.4 %all-to-all-start.4 = ((bf16[64,16,2048]{2,1,0:T(8,128)(2,1)}), bf16[64,16,2048]{2,1,0:T(8,128)(2,1)}, u32[]{:S(2)}, u32[]{:S(2)}) async-start(bf16[64,16,2048]{2,1,0:T(8,128)(2,1)} %bitcast.155), calls=%async_computation.4 | async-start | bytes 8388608 | tf_op jit(solution)/shard_map/all_to_all | solution.py:163
  88.7 6.4 %collective-permute-start.3 = (bf16[2048,512]{1,0:T(8,128)(2,1)}, bf16[2048,512]{1,0:T(8,128)(2,1)}, u32[]{:S(2)}, u32[]{:S(2)}) collective-permute-start(bf16[2048,512]{1,0:T(8,128)(2,1)} %bitcast.179), channel_id=1, source_target_pairs={{0,1},{1,0},{2,3},{3,2},{4,5},{5,4},{6,7},{7,6},{8,9},{9,8},{10,11... | collective-permute-start | bytes 6291464 | tf_op jit(solution)/shard_map/ppermute | solution.py:40
  90.6 7.1 %collective-permute-start.2 = (bf16[2048,512]{1,0:T(8,128)(2,1)}, bf16[2048,512]{1,0:T(8,128)(2,1)}, u32[]{:S(2)}, u32[]{:S(2)}) collective-permute-start(bf16[2048,512]{1,0:T(8,128)(2,1)} %bitcast.182), channel_id=1, source_target_pairs={{0,1},{1,0},{2,3},{3,2},{4,5},{5,4},{6,7},{7,6},{8,9},{9,8},{10,11... | collective-permute-start | bytes 6291464 | tf_op jit(solution)/shard_map/ppermute | solution.py:39
  90.7 8.5 %collective-permute-start.1 = (bf16[512,1024]{1,0:T(8,128)(2,1)}, bf16[512,1024]{1,0:T(8,128)(2,1)}, u32[]{:S(2)}, u32[]{:S(2)}) collective-permute-start(bf16[512,1024]{1,0:T(8,128)(2,1)} %bitcast.20), channel_id=1, source_target_pairs={{0,1},{1,0},{2,3},{3,2},{4,5},{5,4},{6,7},{7,6},{8,9},{9,8},{10,11... | collective-permute-start | bytes 3145736 | tf_op jit(solution)/shard_map/ppermute | solution.py:145
  95.0 15.7 %collective-permute-start.4 = (bf16[512,2048]{0,1:T(8,128)(2,1)}, bf16[512,2048]{0,1:T(8,128)(2,1)}, u32[]{:S(2)}, u32[]{:S(2)}) collective-permute-start(bf16[512,2048]{0,1:T(8,128)(2,1)} %bitcast.160), channel_id=1, source_target_pairs={{0,1},{1,0},{2,3},{3,2},{4,5},{5,4},{6,7},{7,6},{8,9},{9,8},{10,11... | collective-permute-start | bytes 6291464 | tf_op jit(solution)/shard_map/ppermute | solution.py:41
  95.1 15.6 %copy-start.4 = (bf16[1,512,2048]{1,2,0:T(8,128)(2,1)S(1)}, bf16[1,512,2048]{1,2,0:T(8,128)(2,1)}, u32[]{:S(2)}) copy-start(bf16[1,512,2048]{1,2,0:T(8,128)(2,1)} %copy.69) | copy-start | bytes 6291460
  138.3 34.2 %all-to-all-start.3 = ((bf16[64,8,1024]{2,1,0:T(8,128)(2,1)}), bf16[64,8,1024]{2,1,0:T(8,128)(2,1)}, u32[]{:S(2)}, u32[]{:S(2)}) async-start(bf16[64,8,1024]{2,1,0:T(8,128)(2,1)} %fusion.42), calls=%async_computation.3 | async-start | bytes 2097152 | tf_op jit(solution)/shard_map/all_to_all | solution.py:156
  161.4 1.6 copy-start.5
  172.5 10.9 %copy-start.10 = (f32[256,8]{0,1:T(8,128)S(1)}, f32[256,8]{0,1:T(8,128)}, u32[]{:S(2)}) copy-start(f32[256,8]{0,1:T(8,128)} %param.24) | copy-start | bytes 24580
  172.5 63.6 %all-to-all-start.5 = ((bf16[128,16,1024]{2,1,0:T(8,128)(2,1)}), bf16[128,16,1024]{2,1,0:T(8,128)(2,1)}, u32[]{:S(2)}, u32[]{:S(2)}) async-start(bf16[128,16,1024]{2,1,0:T(8,128)(2,1)} %bitcast.156), calls=%async_computation.5 | async-start | bytes 8388608 | tf_op jit(solution)/shard_map/all_to_all | solution.py:173
  236.0 5.3 %copy-start.2 = (f32[512,1024]{1,0:T(8,128)S(1)}, f32[512,1024]{1,0:T(8,128)}, u32[]{:S(2)}) copy-start(f32[512,1024]{1,0:T(8,128)} %fusion.55) | copy-start | bytes 6291460
  236.0 6.6 %copy-start.1 = (bf16[256,1024]{1,0:T(8,128)(2,1)S(1)}, bf16[256,1024]{1,0:T(8,128)(2,1)}, u32[]{:S(2)}) copy-start(bf16[256,1024]{1,0:T(8,128)(2,1)} %param.16) | copy-start | bytes 1572868

commit v3 on v2

--- a/solution.py
+++ b/solution.py
@@ -104,7 +104,6 @@
         earlier, chosen.astype(jnp.bfloat16), preferred_element_type=jnp.float32
     ).astype(jnp.int32)
     half = D // tp_count
-    down_cols = down_full.reshape(down_full.shape[0], tp_count, half)
     first = cap // tp_count // 8 * 8
     main = tp_count * first
     over = -(-(cap - main) // 8) * 8
@@ -150,7 +149,7 @@
     )
     act = expert_rows(arrived)
     result = jnp.dot(
-        act, lax.dynamic_slice_in_dim(down_cols, tp_index, 1, 1)[:, 0],
+        act, lax.dynamic_slice_in_dim(down_full, tp_index * half, half, 1),
         preferred_element_type=jnp.float32,
     ).astype(jnp.bfloat16)
     back = lax.all_to_all(result.reshape(experts, over, half), "seq", 0, 0, tiled=True)
@@ -164,20 +163,12 @@
         outgoing.reshape(experts, first, D), "seq", 0, 0, tiled=True
     ).reshape(experts * first, D)
     act = expert_rows(arrived)
-    result = jnp.stack(
-        [
-            jnp.dot(act, down_cols[:, u], preferred_element_type=jnp.float32).astype(jnp.bfloat16)
-            for u in range(tp_count)
-        ]
-    )
-    back = lax.all_to_all(
-        result.reshape(tp_count * experts, first, half), ("tp", "seq"), 0, 0, tiled=True
-    )
-    spot = (
-        tp_count * jnp.arange(first, dtype=jnp.int32)[None, :]
-        + jnp.arange(tp_count, dtype=jnp.int32)[:, None]
-    )
-    mixture = mixture + combine_with(back.reshape(-1, half), spot)
+    result = jnp.dot(act, down_full, preferred_element_type=jnp.float32).astype(jnp.bfloat16)
+    back = lax.all_to_all(result.reshape(experts, first, D), "seq", 0, 0, tiled=True)
+    partial = combine_with(back.reshape(experts * first, D), target[None, :])
+    own = lax.dynamic_slice_in_dim(partial, tp_index * half, half, 1)
+    theirs = lax.dynamic_slice_in_dim(partial, (tp_index + 1) % tp_count * half, half, 1)
+    mixture = mixture + (own + lax.ppermute(theirs, "tp", swap))
     residual = lax.dynamic_slice_in_dim(hidden_state, tp_index * half, half, 1)
     return (residual + mixture).astype(jnp.bfloat16)
 

time: 244 us -> 248 us (1.016)
  starting transfers between devices: 54.8 us -> 60.3 us
  matrix products: 53.1 us -> 56.8 us
  other arithmetic: 16.1 us -> 12.7 us
  local copies, waits for them, and re-layouts: 10 us -> 7.24 us
    all_to_all x1, waiting for transfers between devices: 24 us -> 49 us  [local(): lax.all_to_all(outgoing.reshape(experts, first, D), 'seq', 0, 0, tiled=True)]
    all_to_all x1, waiting for transfers between devices: 46.1 us -> 30.3 us  [local(): lax.all_to_all(result.reshape(experts, first, D), 'seq', 0, 0, tiled=True)]
    all_to_all x1, waiting for transfers between devices: 12.9 us -> 0.01 us  [local(): lax.all_to_all(outgoing.reshape(experts, over, half), 'seq', 0, 0, tiled=...]
    all_to_all x1, waiting for transfers between devices: 0.01 us -> 6.42 us  [local(): lax.all_to_all(result.reshape(experts, over, half), 'seq', 0, 0, tiled=True)]
    all_to_all x1, starting transfers between devices: 5.51 us -> 9.91 us  [local(): lax.all_to_all(outgoing.reshape(experts, over, half), 'seq', 0, 0, tiled=...]
    unnamed x32 -> x33, local copies, waits for them, and re-layouts: 6.84 us -> 3.09 us
    dot_general x3 -> x2, matrix products: 10.7 us -> 14.1 us  [the longest x1 10.6 us: local(): jnp.dot(act, down_full, preferred_element_type=jnp.float32)]
    ppermute x1, waiting for transfers between devices: 2.6 us -> 0.01 us  [local(): lax.ppermute(w_gate[0], 'tp', swap)]
  transfers between devices with their start and end apart: 11 -> 12, of which waited for: 8 -> 7; matrix products, arithmetic and copies ran while one was open for 23% -> 23% of each run, Pallas kernels for 0% -> 0%
where the time goes in v3:
time: 248 us; the launch traced here: 245 us
  waiting for transfers between devices  108 us (44%)
  starting transfers between devices  60.3 us (24%)
  matrix products  56.8 us (23%)
  other arithmetic  12.7 us (5%)
  local copies, waits for them, and re-layouts  7.24 us (3%)
    all_to_all x1, waiting for transfers between devices, local(): lax.all_to_all(outgoing.reshape(experts, first, D), 'seq', 0, 0, tiled=True)  49 us
    all_to_all x1, waiting for transfers between devices, local(): lax.all_to_all(result.reshape(experts, first, D), 'seq', 0, 0, tiled=True)  30.3 us
    dot_general x2, matrix products, expert_rows(): both_parts = jnp.dot(arrived, gate_up, preferred_element_type=jnp.float32)  26.5 us
    all_to_all x1, starting transfers between devices, local(): lax.all_to_all(outbound.reshape(seq_count, -1, 128), 'seq', 0, 0, tiled=T...  12 us
    dot_general x1, matrix products, local(): jnp.dot(act, down_full, preferred_element_type=jnp.float32)  10.6 us
    all_to_all x1, starting transfers between devices, local(): lax.all_to_all(result.reshape(experts, first, D), 'seq', 0, 0, tiled=True)  10.1 us
    all_to_all x1, starting transfers between devices, local(): lax.all_to_all(result.reshape(experts, over, half), 'seq', 0, 0, tiled=True)  10.1 us
    all_to_all x1, starting transfers between devices, local(): lax.all_to_all(outgoing.reshape(experts, over, half), 'seq', 0, 0, tiled=...  9.91 us
  transfers between devices with their start and end apart: 12, of which 7 were waited for; matrix products, arithmetic and copies ran while one was open for 23% of the time, Pallas kernels for 0%

profile of v3, /device:TPU:1, one launch (start us, length us, event | category | flops | bytes accessed | tf_op | source)
XLA Modules:
  0.0 245.0 jit_solution(6465063899765429434)
XLA Ops:
  0.0 0.6 compare_reduce_fusion
  0.6 1.3 fusion.70
  2.0 0.9 pad_maximum_fusion.9
  2.9 0.8 reshape.196
  3.7 12.0 %all-to-all-start = ((bf16[64,9,128]{2,1,0:T(8,128)(2,1)}), bf16[64,9,128]{2,1,0:T(8,128)(2,1)S(1)}, u32[]{:S(2)}, u32[]{:S(2)}) async-start(bf16[64,9,128]{2,1,0:T(8,128)(2,1)} %reshape.196), calls=%async_computation | async-start | bytes 524288 | tf_op jit(solution)/shard_map/all_to_all | solution.py:49
  15.7 0.9 select_reduce_fusion.1
  16.5 8.6 %all-to-all-done = bf16[64,9,128]{2,1,0:T(8,128)(2,1)S(1)} async-done(((bf16[64,9,128]{2,1,0:T(8,128)(2,1)}), bf16[64,9,128]{2,1,0:T(8,128)(2,1)S(1)}, u32[]{:S(2)}, u32[]{:S(2)}) %all-to-all-start) | async-done | bytes 147488 | tf_op jit(solution)/shard_map/all_to_all | solution.py:49
  25.3 0.3 convolution_convert_fusion.2
  25.6 0.9 reshape.198
  26.5 4.9 %all-to-all-start.1 = ((bf16[64,24,128]{2,1,0:T(8,128)(2,1)}), bf16[64,24,128]{2,1,0:T(8,128)(2,1)S(1)}, u32[]{:S(2)}, u32[]{:S(2)}) async-start(bf16[64,24,128]{2,1,0:T(8,128)(2,1)} %reshape.198), calls=%async_computation.1 | async-start | bytes 786432 | tf_op jit(solution)/shard_map/all_to_all | solution.py:57
  31.9 0.3 copy.51
  32.4 0.3 copy.56
  32.7 9.0 %all-to-all-done.1 = bf16[64,24,128]{2,1,0:T(8,128)(2,1)S(1)} async-done(((bf16[64,24,128]{2,1,0:T(8,128)(2,1)}), bf16[64,24,128]{2,1,0:T(8,128)(2,1)S(1)}, u32[]{:S(2)}, u32[]{:S(2)}) %all-to-all-start.1) | async-done | bytes 393248 | tf_op jit(solution)/shard_map/all_to_all | solution.py:57
  42.3 0.6 bitcast_reduce_fusion
  42.8 0.6 fusion.4
  43.5 1.1 fusion.35
  44.6 1.0 copy-done.10
  45.7 1.2 convolution_bitcast_fusion
  46.9 3.2 %collective-permute-start = (f32[256,2048]{1,0:T(8,128)S(1)}, f32[256,2048]{1,0:T(8,128)}, u32[]{:S(2)}, u32[]{:S(2)}) collective-permute-start(f32[256,2048]{1,0:T(8,128)S(1)} %convolution_bitcast_fusion), channel_id=1, source_target_pairs={{0,1},{1,0},{2,3},{3,2},{4,5},{5,4},{6,7},{7,6},{8,9},{9,8},{10,11... | collective-permute-start | bytes 6291464 | tf_op jit(solution)/shard_map/ppermute | solution.py:91
  50.5 0.3 fusion.46
  50.8 3.3 %collective-permute-done = f32[256,2048]{1,0:T(8,128)} collective-permute-done((f32[256,2048]{1,0:T(8,128)S(1)}, f32[256,2048]{1,0:T(8,128)}, u32[]{:S(2)}, u32[]{:S(2)}) %collective-permute-start) | collective-permute-done | bytes 2097184 | tf_op jit(solution)/shard_map/ppermute | solution.py:91
  54.0 2.9 %multiply_reduce_fusion = (f32[256]{0:T(256)S(1)}, f32[256,2048]{1,0:T(8,128)S(1)}) fusion(f32[256,2048]{1,0:T(8,128)} %copy-done.5, f32[256,2048]{1,0:T(8,128)} %collective-permute-done, bf16[256,2048]{1,0:T(8,128)(2,1)} %param.15), kind=kLoop, calls=%fused_computation.30 | loop fusion | flops 2621184 | bytes 7341056 | tf_op jit(solution)/shard_map/reduce_sum | solution.py:93
  57.2 3.2 %convolution_convert_fusion = bf16[1024,2048]{1,0:T(8,128)(2,1)} fusion(pred[256,1024]{0,1:T(32,128)(4,1)S(1)} %fusion.46, bf16[256,2048]{1,0:T(8,128)(2,1)S(1)} %multiply_convert_fusion), kind=kOutput, calls=%fused_computation.8 | convolution fusion | flops 1075838976 | bytes 5505024 | tf_op jit(solution)/shard_map/ts,td->sd/dot_general | solution.py:159
  60.4 5.7 %all-to-all-start.4 = ((bf16[64,16,2048]{2,1,0:T(8,128)(2,1)}), bf16[64,16,2048]{2,1,0:T(8,128)(2,1)}, u32[]{:S(2)}, u32[]{:S(2)}) async-start(bf16[64,16,2048]{2,1,0:T(8,128)(2,1)} %bitcast.107), calls=%async_computation.4 | async-start | bytes 8388608 | tf_op jit(solution)/shard_map/all_to_all | solution.py:162
  66.1 0.5 collective-permute-start.2
  66.7 0.4 collective-permute-start.4
  67.2 2.5 %fusion.28 = bf16[64,8,1024]{2,1,0:T(8,128)(2,1)} fusion(bf16[256,2048]{1,0:T(8,128)(2,1)} %copy-done.4, s32[]{:T(128)S(6)} %select_n.66, s32[512]{0:T(512)S(1)} %eq.152, s32[256,64]{0,1:T(8,128)S(1)} %convolution_convert_fusion.3, pred[256,64]{0,1:T(8,128)(4,1)S(1)} %fusion.58), kind=kOutput, calls=%fused_computation.40 | convolution fusion | flops 269221888 | bytes 1656836 | tf_op jit(solution)/shard_map/ts,td->sd/dot_general | solution.py:139
  69.7 49.0 %all-to-all-done.4 = bf16[64,16,2048]{2,1,0:T(8,128)(2,1)} async-done(((bf16[64,16,2048]{2,1,0:T(8,128)(2,1)}), bf16[64,16,2048]{2,1,0:T(8,128)(2,1)}, u32[]{:S(2)}, u32[]{:S(2)}) %all-to-all-start.4) | async-done | bytes 4194336 | tf_op jit(solution)/shard_map/all_to_all | solution.py:162
  118.7 9.9 %all-to-all-start.2 = ((bf16[64,8,1024]{2,1,0:T(8,128)(2,1)}), bf16[64,8,1024]{2,1,0:T(8,128)(2,1)}, u32[]{:S(2)}, u32[]{:S(2)}) async-start(bf16[64,8,1024]{2,1,0:T(8,128)(2,1)} %fusion.28), calls=%async_computation.2 | async-start | bytes 2097152 | tf_op jit(solution)/shard_map/all_to_all | solution.py:142
  128.7 15.0 %fusion.27 = f32[1024,2048]{1,0:T(8,128)} fusion(bf16[1024,2048]{1,0:T(8,128)(2,1)} %bitcast.32, bf16[2048,512]{1,0:T(8,128)(2,1)} %collective-permute-done.3, bf16[2048,512]{1,0:T(8,128)(2,1)} %bitcast.131, bf16[2048,512]{1,0:T(8,128)(2,1)} %collective-permute-done.2, bf16[2048,512]{1,0:T(8,128)(2,1)} %bitcast.134), kind=kOutput, calls=%fused_computation.39 | convolution fusion | flops 8623489024 | bytes 20971520 | tf_op jit(solution)/shard_map/dot_general | solution.py:128
  143.7 10.6 %fusion.2 = bf16[1024,2048]{1,0:T(8,128)(2,1)} fusion(bf16[512,2048]{1,0:T(8,128)(2,1)} %collective-permute-done.4, bf16[512,2048]{1,0:T(8,128)(2,1)S(1)} %bitcast.137, f32[1024,2048]{1,0:T(8,128)} %fusion.27), kind=kOutput, calls=%fused_computation.7 | convolution fusion | flops 4311744512 | bytes 16777216 | tf_op jit(solution)/shard_map/dot_general | solution.py:166
  154.3 10.1 %all-to-all-start.5 = ((bf16[64,16,2048]{2,1,0:T(8,128)(2,1)}), bf16[64,16,2048]{2,1,0:T(8,128)(2,1)}, u32[]{:S(2)}, u32[]{:S(2)}) async-start(bf16[64,16,2048]{2,1,0:T(8,128)(2,1)} %bitcast.108), calls=%async_computation.5 | async-start | bytes 8388608 | tf_op jit(solution)/shard_map/all_to_all | solution.py:167
  164.4 1.8 collective-permute-start.1
  166.3 0.3 and_select_fusion
  166.7 1.1 pad_maximum_fusion.7
  167.7 1.1 collective-permute-done.1
  168.8 11.5 %fusion.12 = f32[512,2048]{1,0:T(8,128)S(1)} fusion(bf16[512,1024]{1,0:T(8,128)(2,1)} %collective-permute-done.1, bf16[512,1024]{1,0:T(8,128)(2,1)} %bitcast.20, pred[]{:T(512)S(6)} %eq.148, bf16[2048,512]{1,0:T(8,128)(2,1)} %collective-permute-done.3, bf16[2048,512]{1,0:T(8,128)(2,1)} %bitcast.132, bf16[2048,512]{1,0:T(8,128)(2,1)} %collective-permute-done.2, ...), kind=kOutput, calls=%fused_computation.22 | convolution fusion | flops 4337958912 | bytes 14680065 | tf_op jit(solution)/shard_map/dot_general | solution.py:128
  180.3 3.5 %fusion.29 = bf16[64,8,1024]{2,1,0:T(8,128)(2,1)} fusion(s32[]{:T(128)S(6)} %select_n.66, bf16[512,2048]{1,0:T(8,128)(2,1)S(1)} %bitcast.138, bf16[512,2048]{1,0:T(8,128)(2,1)} %collective-permute-done.4, f32[512,2048]{1,0:T(8,128)S(1)} %fusion.12), kind=kOutput, calls=%fused_computation.41 | convolution fusion | flops 1081606144 | bytes 9437188 | tf_op jit(solution)/shard_map/dot_general | solution.py:151
  183.8 30.3 %all-to-all-done.5 = bf16[64,16,2048]{2,1,0:T(8,128)(2,1)} async-done(((bf16[64,16,2048]{2,1,0:T(8,128)(2,1)}), bf16[64,16,2048]{2,1,0:T(8,128)(2,1)}, u32[]{:S(2)}, u32[]{:S(2)}) %all-to-all-start.5) | async-done | bytes 4194336 | tf_op jit(solution)/shard_map/all_to_all | solution.py:167
  214.1 10.1 %all-to-all-start.3 = ((bf16[64,8,1024]{2,1,0:T(8,128)(2,1)}), bf16[64,8,1024]{2,1,0:T(8,128)(2,1)}, u32[]{:S(2)}, u32[]{:S(2)}) async-start(bf16[64,8,1024]{2,1,0:T(8,128)(2,1)} %fusion.29), calls=%async_computation.3 | async-start | bytes 2097152 | tf_op jit(solution)/shard_map/all_to_all | solution.py:155
  224.2 5.0 %fusion.83 = f32[512,2048]{1,0:T(8,128)S(1)} fusion(bf16[512,1024]{0,1:T(8,128)(2,1)} %pad_maximum_fusion.7, bf16[1024,2048]{1,0:T(8,128)(2,1)} %bitcast.34), kind=kOutput, calls=%fused_computation.117 | convolution fusion | flops 2147483648 | bytes 9437184 | tf_op jit(solution)/shard_map/dot_general | solution.py:121
  229.1 0.3 slice_add_fusion
  229.5 1.3 copy-done.2
  230.8 1.1 constant_dynamic-slice_fusion
  231.9 1.7 collective-permute-start.5
  234.0 6.4 %all-to-all-done.3 = bf16[64,8,1024]{2,1,0:T(8,128)(2,1)} async-done(((bf16[64,8,1024]{2,1,0:T(8,128)(2,1)}), bf16[64,8,1024]{2,1,0:T(8,128)(2,1)}, u32[]{:S(2)}, u32[]{:S(2)}) %all-to-all-start.3) | async-done | bytes 1048608 | tf_op jit(solution)/shard_map/all_to_all | solution.py:155
  240.4 2.1 fusion.43
  242.6 2.5 %fusion.41 = bf16[256,1024]{1,0:T(8,128)(2,1)} fusion(f32[512,1024]{1,0:T(8,128)S(1)} %fusion.43, f32[256,1024]{1,0:T(8,128)} %collective-permute-done.5, f32[256,2048]{1,0:T(8,128)S(1)} %copy-done.3, s32[]{:T(128)S(6)} %select_n.66, f32[256,2048]{1,0:T(8,128)S(1)} %get-tuple-element.20), kind=kLoop, calls=%fused_computation.49 | loop fusion | flops 1310720 | bytes 5767172 | tf_op jit(solution)/shard_map/convert_element_type | solution.py:173
  (63 shorter events, 2.9 us)
Async XLA Ops:
  0.0 42.3 %copy-start = (bf16[256,1024]{1,0:T(8,128)(2,1)S(1)}, bf16[256,1024]{1,0:T(8,128)(2,1)}, u32[]{:S(2)}) copy-start(bf16[256,1024]{1,0:T(8,128)(2,1)} %param.16) | copy-start | bytes 1572868
  0.0 31.6 %copy-start.6 = (bf16[2,256,1024]{2,1,0:T(8,128)(2,1)S(1)}, bf16[2,256,1024]{2,1,0:T(8,128)(2,1)}, u32[]{:S(2)}) copy-start(bf16[2,256,1024]{2,1,0:T(8,128)(2,1)} %param.17) | copy-start | bytes 3145732
  3.7 21.4 %all-to-all-start = ((bf16[64,9,128]{2,1,0:T(8,128)(2,1)}), bf16[64,9,128]{2,1,0:T(8,128)(2,1)S(1)}, u32[]{:S(2)}, u32[]{:S(2)}) async-start(bf16[64,9,128]{2,1,0:T(8,128)(2,1)} %reshape.196), calls=%async_computation | async-start | bytes 524288 | tf_op jit(solution)/shard_map/all_to_all | solution.py:49
  26.5 15.1 %all-to-all-start.1 = ((bf16[64,24,128]{2,1,0:T(8,128)(2,1)}), bf16[64,24,128]{2,1,0:T(8,128)(2,1)S(1)}, u32[]{:S(2)}, u32[]{:S(2)}) async-start(bf16[64,24,128]{2,1,0:T(8,128)(2,1)} %reshape.198), calls=%async_computation.1 | async-start | bytes 786432 | tf_op jit(solution)/shard_map/all_to_all | solution.py:57
  43.5 2.2 copy-start.10
  45.7 4.6 %copy-start.7 = (s32[256,8]{0,1:T(8,128)S(1)}, s32[256,8]{0,1:T(8,128)}, u32[]{:S(2)}) copy-start(s32[256,8]{0,1:T(8,128)} %param.23) | copy-start | bytes 24580
  46.9 3.8 %copy-start.5 = (f32[256,2048]{1,0:T(8,128)}, f32[256,2048]{1,0:T(8,128)S(1)}, u32[]{:S(2)}) copy-start(f32[256,2048]{1,0:T(8,128)S(1)} %convolution_bitcast_fusion) | copy-start | bytes 6291460
  46.9 7.1 %collective-permute-start = (f32[256,2048]{1,0:T(8,128)S(1)}, f32[256,2048]{1,0:T(8,128)}, u32[]{:S(2)}, u32[]{:S(2)}) collective-permute-start(f32[256,2048]{1,0:T(8,128)S(1)} %convolution_bitcast_fusion), channel_id=1, source_target_pairs={{0,1},{1,0},{2,3},{3,2},{4,5},{5,4},{6,7},{7,6},{8,9},{9,8},{10,11... | collective-permute-start | bytes 6291464 | tf_op jit(solution)/shard_map/ppermute | solution.py:91
  50.8 6.2 %copy-start.8 = (f32[2048]{0:T(1024)S(1)}, f32[2048]{0:T(1024)}, u32[]{:S(2)}) copy-start(f32[2048]{0:T(1024)} %param.22) | copy-start | bytes 24580
  57.2 3.2 %copy-start.4 = (bf16[256,2048]{1,0:T(8,128)(2,1)}, bf16[256,2048]{1,0:T(8,128)(2,1)S(1)}, u32[]{:S(2)}) copy-start(bf16[256,2048]{1,0:T(8,128)(2,1)S(1)} %multiply_convert_fusion) | copy-start | bytes 3145732
  60.4 58.3 %all-to-all-start.4 = ((bf16[64,16,2048]{2,1,0:T(8,128)(2,1)}), bf16[64,16,2048]{2,1,0:T(8,128)(2,1)}, u32[]{:S(2)}, u32[]{:S(2)}) async-start(bf16[64,16,2048]{2,1,0:T(8,128)(2,1)} %bitcast.107), calls=%async_computation.4 | async-start | bytes 8388608 | tf_op jit(solution)/shard_map/all_to_all | solution.py:162
  66.1 62.5 %collective-permute-start.2 = (bf16[2048,512]{1,0:T(8,128)(2,1)}, bf16[2048,512]{1,0:T(8,128)(2,1)}, u32[]{:S(2)}, u32[]{:S(2)}) collective-permute-start(bf16[2048,512]{1,0:T(8,128)(2,1)} %bitcast.133), channel_id=1, source_target_pairs={{0,1},{1,0},{2,3},{3,2},{4,5},{5,4},{6,7},{7,6},{8,9},{9,8},{10,11... | collective-permute-start | bytes 6291464 | tf_op jit(solution)/shard_map/ppermute | solution.py:39
  66.6 62.1 %collective-permute-start.3 = (bf16[2048,512]{1,0:T(8,128)(2,1)}, bf16[2048,512]{1,0:T(8,128)(2,1)}, u32[]{:S(2)}, u32[]{:S(2)}) collective-permute-start(bf16[2048,512]{1,0:T(8,128)(2,1)} %bitcast.130), channel_id=1, source_target_pairs={{0,1},{1,0},{2,3},{3,2},{4,5},{5,4},{6,7},{7,6},{8,9},{9,8},{10,11... | collective-permute-start | bytes 6291464 | tf_op jit(solution)/shard_map/ppermute | solution.py:40
  66.7 77.0 %collective-permute-start.4 = (bf16[512,2048]{1,0:T(8,128)(2,1)}, bf16[512,2048]{1,0:T(8,128)(2,1)}, u32[]{:S(2)}, u32[]{:S(2)}) collective-permute-start(bf16[512,2048]{1,0:T(8,128)(2,1)} %bitcast.136), channel_id=1, source_target_pairs={{0,1},{1,0},{2,3},{3,2},{4,5},{5,4},{6,7},{7,6},{8,9},{9,8},{10,11... | collective-permute-start | bytes 6291464 | tf_op jit(solution)/shard_map/ppermute | solution.py:41
  118.7 35.5 %all-to-all-start.2 = ((bf16[64,8,1024]{2,1,0:T(8,128)(2,1)}), bf16[64,8,1024]{2,1,0:T(8,128)(2,1)}, u32[]{:S(2)}, u32[]{:S(2)}) async-start(bf16[64,8,1024]{2,1,0:T(8,128)(2,1)} %fusion.28), calls=%async_computation.2 | async-start | bytes 2097152 | tf_op jit(solution)/shard_map/all_to_all | solution.py:142
  128.7 15.0 %copy-start.11 = (bf16[1,512,2048]{2,1,0:T(8,128)(2,1)S(1)}, bf16[1,512,2048]{2,1,0:T(8,128)(2,1)}, u32[]{:S(2)}) copy-start(bf16[1,512,2048]{2,1,0:T(8,128)(2,1)} %param.27) | copy-start | bytes 6291460
  154.3 11.9 %copy-start.9 = (f32[256,8]{0,1:T(8,128)S(1)}, f32[256,8]{0,1:T(8,128)}, u32[]{:S(2)}) copy-start(f32[256,8]{0,1:T(8,128)} %param.24) | copy-start | bytes 24580
  154.3 59.9 %all-to-all-start.5 = ((bf16[64,16,2048]{2,1,0:T(8,128)(2,1)}), bf16[64,16,2048]{2,1,0:T(8,128)(2,1)}, u32[]{:S(2)}, u32[]{:S(2)}) async-start(bf16[64,16,2048]{2,1,0:T(8,128)(2,1)} %bitcast.108), calls=%async_computation.5 | async-start | bytes 8388608 | tf_op jit(solution)/shard_map/all_to_all | solution.py:167
  164.4 4.5 %collective-permute-start.1 = (bf16[512,1024]{1,0:T(8,128)(2,1)}, bf16[512,1024]{1,0:T(8,128)(2,1)}, u32[]{:S(2)}, u32[]{:S(2)}) collective-permute-start(bf16[512,1024]{1,0:T(8,128)(2,1)} %bitcast.20), channel_id=1, source_target_pairs={{0,1},{1,0},{2,3},{3,2},{4,5},{5,4},{6,7},{7,6},{8,9},{9,8},{10,11... | collective-permute-start | bytes 3145736 | tf_op jit(solution)/shard_map/ppermute | solution.py:144
  167.7 12.6 %copy-start.12 = (bf16[1,512,2048]{2,1,0:T(8,128)(2,1)S(1)}, bf16[1,512,2048]{2,1,0:T(8,128)(2,1)}, u32[]{:S(2)}) copy-start(bf16[1,512,2048]{2,1,0:T(8,128)(2,1)} %param.27) | copy-start | bytes 6291460
  214.1 26.3 %all-to-all-start.3 = ((bf16[64,8,1024]{2,1,0:T(8,128)(2,1)}), bf16[64,8,1024]{2,1,0:T(8,128)(2,1)}, u32[]{:S(2)}, u32[]{:S(2)}) async-start(bf16[64,8,1024]{2,1,0:T(8,128)(2,1)} %fusion.29), calls=%async_computation.3 | async-start | bytes 2097152 | tf_op jit(solution)/shard_map/all_to_all | solution.py:155
  229.5 1.3 copy-start.2
  231.9 10.7 %collective-permute-start.5 = (f32[256,1024]{1,0:T(8,128)}, f32[256,1024]{1,0:T(8,128)}, u32[]{:S(2)}, u32[]{:S(2)}) collective-permute-start(f32[256,1024]{1,0:T(8,128)} %constant_dynamic-slice_fusion), channel_id=1, source_target_pairs={{0,1},{1,0},{2,3},{3,2},{4,5},{5,4},{6,7},{7,6},{8,9},{9,8},{10,11... | collective-permute-start | bytes 3145736 | tf_op jit(solution)/shard_map/ppermute | solution.py:171
  240.4 2.1 copy-start.3
  240.4 4.6 %copy-start.1 = (bf16[256,1024]{1,0:T(8,128)(2,1)S(1)}, bf16[256,1024]{1,0:T(8,128)(2,1)}, u32[]{:S(2)}) copy-start(bf16[256,1024]{1,0:T(8,128)(2,1)} %param.16) | copy-start | bytes 1572868

commit v4 on v3

--- a/solution.py
+++ b/solution.py
@@ -104,6 +104,7 @@
         earlier, chosen.astype(jnp.bfloat16), preferred_element_type=jnp.float32
     ).astype(jnp.int32)
     half = D // tp_count
+    down_cols = down_full.reshape(down_full.shape[0], tp_count, half)
     first = cap // tp_count // 8 * 8
     main = tp_count * first
     over = -(-(cap - main) // 8) * 8
@@ -134,11 +135,36 @@
         sel = chosen[:, :, None] & (ranks[:, :, None] == wanted[None, None, :])
         return sel.reshape(rows, experts * wanted.shape[0]).astype(jnp.bfloat16)
 
+    target = tp_count * jnp.arange(first, dtype=jnp.int32) + tp_index
+    outgoing = jnp.einsum(
+        "ts,td->sd", select(target), normed, preferred_element_type=jnp.float32
+    ).astype(jnp.bfloat16)
+    arrived = lax.all_to_all(
+        outgoing.reshape(experts, first, D), "seq", 0, 0, tiled=True
+    ).reshape(experts * first, D)
+    arrived_main = arrived
+    act = expert_rows(arrived)
+    result = jnp.stack(
+        [
+            jnp.dot(act, down_cols[:, u], preferred_element_type=jnp.float32).astype(jnp.bfloat16)
+            for u in range(tp_count)
+        ]
+    )
+    back = lax.all_to_all(
+        result.reshape(tp_count * experts, first, half), ("tp", "seq"), 0, 0, tiled=True
+    )
+    spot = (
+        tp_count * jnp.arange(first, dtype=jnp.int32)[None, :]
+        + jnp.arange(tp_count, dtype=jnp.int32)[:, None]
+    )
+    back_main = back
+    mixture = combine_with(back.reshape(-1, half), spot)
     mine = lax.dynamic_slice_in_dim(normed, tp_index * half, half, 1)
     extra = jnp.arange(main, main + over, dtype=jnp.int32)
     outgoing = jnp.einsum(
         "ts,td->sd", select(extra), mine, preferred_element_type=jnp.float32
     ).astype(jnp.bfloat16)
+    outgoing, _ = lax.optimization_barrier((outgoing, arrived_main))
     arrived = lax.all_to_all(outgoing.reshape(experts, over, half), "seq", 0, 0, tiled=True)
     arrived = arrived.reshape(experts * over, half)
     partner = lax.ppermute(arrived, "tp", swap)
@@ -149,26 +175,13 @@
     )
     act = expert_rows(arrived)
     result = jnp.dot(
-        act, lax.dynamic_slice_in_dim(down_full, tp_index * half, half, 1),
+        act, lax.dynamic_slice_in_dim(down_cols, tp_index, 1, 1)[:, 0],
         preferred_element_type=jnp.float32,
     ).astype(jnp.bfloat16)
+    result, _ = lax.optimization_barrier((result, back_main))
     back = lax.all_to_all(result.reshape(experts, over, half), "seq", 0, 0, tiled=True)
-    mixture = combine_with(back.reshape(experts * over, half), extra[None, :])
-
-    target = tp_count * jnp.arange(first, dtype=jnp.int32) + tp_index
-    outgoing = jnp.einsum(
-        "ts,td->sd", select(target), normed, preferred_element_type=jnp.float32
-    ).astype(jnp.bfloat16)
-    arrived = lax.all_to_all(
-        outgoing.reshape(experts, first, D), "seq", 0, 0, tiled=True
-    ).reshape(experts * first, D)
-    act = expert_rows(arrived)
-    result = jnp.dot(act, down_full, preferred_element_type=jnp.float32).astype(jnp.bfloat16)
-    back = lax.all_to_all(result.reshape(experts, first, D), "seq", 0, 0, tiled=True)
-    partial = combine_with(back.reshape(experts * first, D), target[None, :])
-    own = lax.dynamic_slice_in_dim(partial, tp_index * half, half, 1)
-    theirs = lax.dynamic_slice_in_dim(partial, (tp_index + 1) % tp_count * half, half, 1)
-    mixture = mixture + (own + lax.ppermute(theirs, "tp", swap))
+    mixture = mixture + combine_with(back.reshape(experts * over, half), extra[None, :])
+
     residual = lax.dynamic_slice_in_dim(hidden_state, tp_index * half, half, 1)
     return (residual + mixture).astype(jnp.bfloat16)
 

time: 248 us -> 246 us (level)
  matrix products: 56.8 us -> 49.5 us
  other arithmetic: 12.7 us -> 19.4 us
  starting transfers between devices: 60.3 us -> 56.4 us
    dot_general x2, matrix products: 26.5 us -> 21 us  [expert_rows(): both_parts = jnp.dot(arrived, gate_up, preferred_element_type=jnp.float32)]
    all_to_all x1, waiting for transfers between devices: 6.42 us -> 10.5 us  [local(): lax.all_to_all(result.reshape(experts, over, half), 'seq', 0, 0, tiled=True)]
    all_to_all x1, waiting for transfers between devices: 49 us -> 45.1 us  [local(): lax.all_to_all(outgoing.reshape(experts, first, D), 'seq', 0, 0, tiled=True)]
    dot_general x2 -> x3, matrix products: 14.1 us -> 10.7 us  [the longest x2 7.17 us: local(): jnp.dot(act, down_cols[:, u], preferred_element_type=jnp.float32)]
    all_to_all x1, waiting for transfers between devices: 30.3 us -> 33.5 us  [local(): lax.all_to_all(result.reshape(tp_count * experts, first, half), ('tp', 's...]
    unnamed x33 -> x36, local copies, waits for them, and re-layouts: 3.09 us -> 5.88 us
  transfers between devices with their start and end apart: 12 -> 11, of which waited for: 7 -> 6; matrix products, arithmetic and copies ran while one was open for 23% -> 24% of each run, Pallas kernels for 0% -> 0%
where the time goes in v4:
time: 246 us; the launch traced here: 245 us
  waiting for transfers between devices  110 us (45%)
  starting transfers between devices  56.4 us (23%)
  matrix products  49.5 us (20%)
  other arithmetic  19.4 us (8%)
  local copies, waits for them, and re-layouts  9.05 us (4%)
    all_to_all x1, waiting for transfers between devices, local(): lax.all_to_all(outgoing.reshape(experts, first, D), 'seq', 0, 0, tiled=True)  45.1 us
    all_to_all x1, waiting for transfers between devices, local(): lax.all_to_all(result.reshape(tp_count * experts, first, half), ('tp', 's...  33.5 us
    dot_general x2, matrix products, expert_rows(): both_parts = jnp.dot(arrived, gate_up, preferred_element_type=jnp.float32)  21 us
    all_to_all x1, starting transfers between devices, local(): lax.all_to_all(outbound.reshape(seq_count, -1, 128), 'seq', 0, 0, tiled=T...  12 us
    all_to_all x1, waiting for transfers between devices, local(): lax.all_to_all(result.reshape(experts, over, half), 'seq', 0, 0, tiled=True)  10.5 us
    all_to_all x1, starting transfers between devices, local(): lax.all_to_all(result.reshape(tp_count * experts, first, half), ('tp', 's...  10.3 us
    all_to_all x1, starting transfers between devices, local(): lax.all_to_all(outgoing.reshape(experts, over, half), 'seq', 0, 0, tiled=...  9.91 us
    all_to_all x1, waiting for transfers between devices, local(): lax.all_to_all(picked.reshape(seq_count, depth * piece // 128, 128), 'seq...  8.97 us
  transfers between devices with their start and end apart: 11, of which 6 were waited for; matrix products, arithmetic and copies ran while one was open for 24% of the time, Pallas kernels for 0%

profile of v4, /device:TPU:1, one launch (start us, length us, event | category | flops | bytes accessed | tf_op | source)
XLA Modules:
  0.0 244.7 jit_solution(11589108719267524091)
XLA Ops:
  0.0 0.6 compare_reduce_fusion
  0.6 1.3 fusion.78
  2.0 0.9 pad_maximum_fusion.6
  2.9 0.8 reshape.190
  3.7 12.0 %all-to-all-start = ((bf16[64,9,128]{2,1,0:T(8,128)(2,1)}), bf16[64,9,128]{2,1,0:T(8,128)(2,1)S(1)}, u32[]{:S(2)}, u32[]{:S(2)}) async-start(bf16[64,9,128]{2,1,0:T(8,128)(2,1)} %reshape.190), calls=%async_computation | async-start | bytes 524288 | tf_op jit(solution)/shard_map/all_to_all | solution.py:49
  15.7 0.9 select_reduce_fusion.1
  16.5 8.6 %all-to-all-done = bf16[64,9,128]{2,1,0:T(8,128)(2,1)S(1)} async-done(((bf16[64,9,128]{2,1,0:T(8,128)(2,1)}), bf16[64,9,128]{2,1,0:T(8,128)(2,1)S(1)}, u32[]{:S(2)}, u32[]{:S(2)}) %all-to-all-start) | async-done | bytes 147488 | tf_op jit(solution)/shard_map/all_to_all | solution.py:49
  25.3 0.3 convolution_convert_fusion.2
  25.6 0.9 reshape.192
  26.5 4.9 %all-to-all-start.1 = ((bf16[64,24,128]{2,1,0:T(8,128)(2,1)}), bf16[64,24,128]{2,1,0:T(8,128)(2,1)S(1)}, u32[]{:S(2)}, u32[]{:S(2)}) async-start(bf16[64,24,128]{2,1,0:T(8,128)(2,1)} %reshape.192), calls=%async_computation.1 | async-start | bytes 786432 | tf_op jit(solution)/shard_map/all_to_all | solution.py:57
  31.9 0.3 copy.62
  32.4 0.3 copy.67
  32.7 9.0 %all-to-all-done.1 = bf16[64,24,128]{2,1,0:T(8,128)(2,1)S(1)} async-done(((bf16[64,24,128]{2,1,0:T(8,128)(2,1)}), bf16[64,24,128]{2,1,0:T(8,128)(2,1)S(1)}, u32[]{:S(2)}, u32[]{:S(2)}) %all-to-all-start.1) | async-done | bytes 393248 | tf_op jit(solution)/shard_map/all_to_all | solution.py:57
  42.3 0.6 bitcast_reduce_fusion
  42.8 0.6 fusion.2
  43.5 1.1 fusion.44
  44.6 1.0 copy-done.11
  45.7 1.2 convolution_bitcast_fusion
  46.9 3.2 %collective-permute-start = (f32[256,2048]{1,0:T(8,128)S(1)}, f32[256,2048]{1,0:T(8,128)}, u32[]{:S(2)}, u32[]{:S(2)}) collective-permute-start(f32[256,2048]{1,0:T(8,128)S(1)} %convolution_bitcast_fusion), channel_id=1, source_target_pairs={{0,1},{1,0},{2,3},{3,2},{4,5},{5,4},{6,7},{7,6},{8,9},{9,8},{10,11... | collective-permute-start | bytes 6291464 | tf_op jit(solution)/shard_map/ppermute | solution.py:91
  50.5 0.3 fusion.54
  50.8 3.3 %collective-permute-done = f32[256,2048]{1,0:T(8,128)} collective-permute-done((f32[256,2048]{1,0:T(8,128)S(1)}, f32[256,2048]{1,0:T(8,128)}, u32[]{:S(2)}, u32[]{:S(2)}) %collective-permute-start) | collective-permute-done | bytes 2097184 | tf_op jit(solution)/shard_map/ppermute | solution.py:91
  54.0 2.9 %multiply_reduce_fusion = (f32[256]{0:T(256)S(1)}, f32[256,2048]{1,0:T(8,128)S(1)}) fusion(f32[256,2048]{1,0:T(8,128)} %copy-done.6, f32[256,2048]{1,0:T(8,128)} %collective-permute-done, bf16[256,2048]{1,0:T(8,128)(2,1)} %param.15), kind=kLoop, calls=%fused_computation.45 | loop fusion | flops 2621184 | bytes 7341056 | tf_op jit(solution)/shard_map/reduce_sum | solution.py:93
  57.2 3.2 %convolution_convert_fusion = bf16[1024,2048]{1,0:T(8,128)(2,1)} fusion(pred[256,1024]{0,1:T(32,128)(4,1)S(1)} %fusion.54, bf16[256,2048]{1,0:T(8,128)(2,1)S(1)} %multiply_convert_fusion), kind=kOutput, calls=%fused_computation.10 | convolution fusion | flops 1075838976 | bytes 5505024 | tf_op jit(solution)/shard_map/ts,td->sd/dot_general | solution.py:139
  60.5 5.7 %all-to-all-start.2 = ((bf16[64,16,2048]{2,1,0:T(8,128)(2,1)}), bf16[64,16,2048]{2,1,0:T(8,128)(2,1)}, u32[]{:S(2)}, u32[]{:S(2)}) async-start(bf16[64,16,2048]{2,1,0:T(8,128)(2,1)} %bitcast.151), calls=%async_computation.2 | async-start | bytes 8388608 | tf_op jit(solution)/shard_map/all_to_all | solution.py:142
  66.1 0.5 collective-permute-start.1
  66.7 3.9 %copy.69 = bf16[1,512,2048]{1,2,0:T(8,128)(2,1)} copy(bf16[1,512,2048]{2,1,0:T(8,128)(2,1)} %param.27) | data formatting | bytes 4194304 | tf_op args[12]
  70.6 0.4 collective-permute-start.3
  71.1 2.5 %convolution_convert_fusion.1 = bf16[512,1024]{1,0:T(8,128)(2,1)} fusion(bf16[256,2048]{1,0:T(8,128)(2,1)} %copy-done.2, s32[]{:T(128)S(6)} %select_n.51, s32[512]{0:T(512)S(1)} %eq.162, s32[256,64]{0,1:T(8,128)S(1)} %convolution_convert_fusion.3, pred[256,64]{0,1:T(8,128)(4,1)S(1)} %fusion.66), kind=kOutput, calls=%fused_computation.50 | convolution fusion | flops 269221888 | bytes 1656836 | tf_op jit(solution)/shard_map/ts,td->sd/dot_general | solution.py:164
  73.6 45.1 %all-to-all-done.2 = bf16[64,16,2048]{2,1,0:T(8,128)(2,1)} async-done(((bf16[64,16,2048]{2,1,0:T(8,128)(2,1)}), bf16[64,16,2048]{2,1,0:T(8,128)(2,1)}, u32[]{:S(2)}, u32[]{:S(2)}) %all-to-all-start.2) | async-done | bytes 4194336 | tf_op jit(solution)/shard_map/all_to_all | solution.py:142
  118.7 9.9 %all-to-all-start.4 = ((bf16[64,8,1024]{2,1,0:T(8,128)(2,1)}), bf16[64,8,1024]{2,1,0:T(8,128)(2,1)}, u32[]{:S(2)}, u32[]{:S(2)}) async-start(bf16[64,8,1024]{2,1,0:T(8,128)(2,1)} %bitcast.153), calls=%async_computation.4 | async-start | bytes 2097152 | tf_op jit(solution)/shard_map/all_to_all | solution.py:168
  128.7 12.9 %fusion.40 = f32[1024,2048]{1,0:T(8,128)S(1)} fusion(bf16[1024,2048]{1,0:T(8,128)(2,1)} %bitcast.17, bf16[2048,512]{1,0:T(8,128)(2,1)} %collective-permute-done.2, bf16[2048,512]{1,0:T(8,128)(2,1)} %bitcast.178, bf16[2048,512]{1,0:T(8,128)(2,1)} %collective-permute-done.1, bf16[2048,512]{1,0:T(8,128)(2,1)} %bitcast.181), kind=kOutput, calls=%fused_computation.55 | convolution fusion | flops 8623489024 | bytes 20971520 | tf_op jit(solution)/shard_map/dot_general | solution.py:129
  141.6 1.4 fusion
  143.2 3.6 %convert_bitcast_fusion = bf16[1,1024,1024]{2,1,0:T(8,128)(2,1)S(1)} fusion(bf16[1024,1024]{1,0:T(8,128)(2,1)S(1)} %fusion, bf16[512,2,1024]{0,2,1:T(8,128)(2,1)S(1)} %bitcast.158, bf16[512,2,1024]{0,2,1:T(8,128)(2,1)} %bitcast.22), kind=kOutput, calls=%fused_computation.42 | convolution fusion | flops 2152726528 | bytes 8388608 | tf_op jit(solution)/shard_map/dot_general | solution.py:149
  146.8 3.6 %convert_bitcast_fusion.1 = bf16[1,1024,1024]{2,1,0:T(8,128)(2,1)S(1)} fusion(bf16[1024,1024]{1,0:T(8,128)(2,1)S(1)} %fusion, bf16[512,2,1024]{0,2,1:T(8,128)(2,1)S(1)} %bitcast.159, bf16[512,2,1024]{0,2,1:T(8,128)(2,1)} %bitcast.22), kind=kOutput, calls=%fused_computation.43 | convolution fusion | flops 2152726528 | bytes 8388608 | tf_op jit(solution)/shard_map/dot_general | solution.py:149
  150.4 2.3 pad_maximum_fusion.1
  152.7 10.3 %all-to-all-start.3 = ((bf16[128,16,1024]{2,1,0:T(8,128)(2,1)}), bf16[128,16,1024]{2,1,0:T(8,128)(2,1)}, u32[]{:S(2)}, u32[]{:S(2)}) async-start(bf16[128,16,1024]{2,1,0:T(8,128)(2,1)} %bitcast.152), calls=%async_computation.3 | async-start | bytes 8388608 | tf_op jit(solution)/shard_map/all_to_all | solution.py:153
  163.0 1.4 collective-permute-start.4
  164.6 1.4 fusion.25
  166.0 1.4 fusion.26
  167.4 3.2 %pad_maximum_fusion.2 = bf16[512,2048]{0,1:T(8,128)(2,1)} fusion(bf16[256,2048]{0,1:T(8,128)(2,1)} %fusion.26, bf16[256,2048]{0,1:T(8,128)(2,1)} %fusion.25), kind=kLoop, calls=%fused_computation.29 | loop fusion | flops 4194304 | bytes 4194304 | tf_op jit(solution)/shard_map/concatenate | solution.py:121
  170.6 8.1 %fusion.18 = f32[512,2048]{1,0:T(8,128)S(1)} fusion(bf16[512,1024]{1,0:T(8,128)(2,1)} %collective-permute-done.4, bf16[512,1024]{1,0:T(8,128)(2,1)} %bitcast.38, pred[]{:T(512)S(6)} %eq.158, bf16[2048,512]{1,0:T(8,128)(2,1)} %collective-permute-done.2, bf16[2048,512]{1,0:T(8,128)(2,1)S(1)} %bitcast.179, bf16[2048,512]{1,0:T(8,128)(2,1)} %collective-permute-done.1, ...), kind=kOutput, calls=%fused_computation.31 | convolution fusion | flops 4337958912 | bytes 14680065 | tf_op jit(solution)/shard_map/dot_general | solution.py:129
  178.8 3.5 %fusion.33 = bf16[512,1024]{1,0:T(8,128)(2,1)} fusion(s32[]{:T(128)S(6)} %select_n.57, bf16[512,2,1024]{0,2,1:T(8,128)(2,1)S(1)} %bitcast.160, bf16[512,2,1024]{0,2,1:T(8,128)(2,1)} %bitcast.22, f32[512,2048]{1,0:T(8,128)S(1)} %fusion.18), kind=kOutput, calls=%fused_computation.49 | convolution fusion | flops 1081606144 | bytes 9437188 | tf_op jit(solution)/shard_map/dot_general | solution.py:177
  182.3 33.5 %all-to-all-done.3 = bf16[128,16,1024]{2,1,0:T(8,128)(2,1)} async-done(((bf16[128,16,1024]{2,1,0:T(8,128)(2,1)}), bf16[128,16,1024]{2,1,0:T(8,128)(2,1)}, u32[]{:S(2)}, u32[]{:S(2)}) %all-to-all-start.3) | async-done | bytes 4194336 | tf_op jit(solution)/shard_map/all_to_all | solution.py:153
  215.8 8.1 %all-to-all-start.5 = ((bf16[64,8,1024]{2,1,0:T(8,128)(2,1)}), bf16[64,8,1024]{2,1,0:T(8,128)(2,1)}, u32[]{:S(2)}, u32[]{:S(2)}) async-start(bf16[64,8,1024]{2,1,0:T(8,128)(2,1)} %bitcast.165), calls=%async_computation.5 | async-start | bytes 2097152 | tf_op jit(solution)/shard_map/all_to_all | solution.py:182
  224.3 6.5 %fusion.91 = f32[512,1024]{1,0:T(8,128)} fusion(bf16[512,2048]{0,1:T(8,128)(2,1)} %pad_maximum_fusion.2, bf16[2048,1024]{1,0:T(8,128)(2,1)} %bitcast.28), kind=kOutput, calls=%fused_computation.128 | convolution fusion | flops 2147483648 | bytes 8388608 | tf_op jit(solution)/shard_map/dot_general | solution.py:122
  230.9 10.5 %all-to-all-done.5 = bf16[64,8,1024]{2,1,0:T(8,128)(2,1)} async-done(((bf16[64,8,1024]{2,1,0:T(8,128)(2,1)}), bf16[64,8,1024]{2,1,0:T(8,128)(2,1)}, u32[]{:S(2)}, u32[]{:S(2)}) %all-to-all-start.5) | async-done | bytes 1048608 | tf_op jit(solution)/shard_map/all_to_all | solution.py:182
  241.4 2.1 fusion.51
  243.5 1.2 fusion.50
  (69 shorter events, 3.1 us)
Async XLA Ops:
  0.0 42.3 %copy-start = (bf16[256,1024]{1,0:T(8,128)(2,1)S(1)}, bf16[256,1024]{1,0:T(8,128)(2,1)}, u32[]{:S(2)}) copy-start(bf16[256,1024]{1,0:T(8,128)(2,1)} %param.16) | copy-start | bytes 1572868
  0.0 31.6 %copy-start.7 = (bf16[2,256,1024]{2,1,0:T(8,128)(2,1)S(1)}, bf16[2,256,1024]{2,1,0:T(8,128)(2,1)}, u32[]{:S(2)}) copy-start(bf16[2,256,1024]{2,1,0:T(8,128)(2,1)} %param.17) | copy-start | bytes 3145732
  3.7 21.4 %all-to-all-start = ((bf16[64,9,128]{2,1,0:T(8,128)(2,1)}), bf16[64,9,128]{2,1,0:T(8,128)(2,1)S(1)}, u32[]{:S(2)}, u32[]{:S(2)}) async-start(bf16[64,9,128]{2,1,0:T(8,128)(2,1)} %reshape.190), calls=%async_computation | async-start | bytes 524288 | tf_op jit(solution)/shard_map/all_to_all | solution.py:49
  26.5 15.1 %all-to-all-start.1 = ((bf16[64,24,128]{2,1,0:T(8,128)(2,1)}), bf16[64,24,128]{2,1,0:T(8,128)(2,1)S(1)}, u32[]{:S(2)}, u32[]{:S(2)}) async-start(bf16[64,24,128]{2,1,0:T(8,128)(2,1)} %reshape.192), calls=%async_computation.1 | async-start | bytes 786432 | tf_op jit(solution)/shard_map/all_to_all | solution.py:57
  43.5 2.2 copy-start.11
  45.7 4.6 %copy-start.8 = (s32[256,8]{0,1:T(8,128)S(1)}, s32[256,8]{0,1:T(8,128)}, u32[]{:S(2)}) copy-start(s32[256,8]{0,1:T(8,128)} %param.23) | copy-start | bytes 24580
  46.9 3.8 %copy-start.6 = (f32[256,2048]{1,0:T(8,128)}, f32[256,2048]{1,0:T(8,128)S(1)}, u32[]{:S(2)}) copy-start(f32[256,2048]{1,0:T(8,128)S(1)} %convolution_bitcast_fusion) | copy-start | bytes 6291460
  46.9 7.1 %collective-permute-start = (f32[256,2048]{1,0:T(8,128)S(1)}, f32[256,2048]{1,0:T(8,128)}, u32[]{:S(2)}, u32[]{:S(2)}) collective-permute-start(f32[256,2048]{1,0:T(8,128)S(1)} %convolution_bitcast_fusion), channel_id=1, source_target_pairs={{0,1},{1,0},{2,3},{3,2},{4,5},{5,4},{6,7},{7,6},{8,9},{9,8},{10,11... | collective-permute-start | bytes 6291464 | tf_op jit(solution)/shard_map/ppermute | solution.py:91
  50.8 6.2 %copy-start.9 = (f32[2048]{0:T(1024)S(1)}, f32[2048]{0:T(1024)}, u32[]{:S(2)}) copy-start(f32[2048]{0:T(1024)} %param.22) | copy-start | bytes 24580
  57.2 3.2 %copy-start.2 = (bf16[256,2048]{1,0:T(8,128)(2,1)}, bf16[256,2048]{1,0:T(8,128)(2,1)S(1)}, u32[]{:S(2)}) copy-start(bf16[256,2048]{1,0:T(8,128)(2,1)S(1)} %multiply_convert_fusion) | copy-start | bytes 3145732
  60.5 58.3 %all-to-all-start.2 = ((bf16[64,16,2048]{2,1,0:T(8,128)(2,1)}), bf16[64,16,2048]{2,1,0:T(8,128)(2,1)}, u32[]{:S(2)}, u32[]{:S(2)}) async-start(bf16[64,16,2048]{2,1,0:T(8,128)(2,1)} %bitcast.151), calls=%async_computation.2 | async-start | bytes 8388608 | tf_op jit(solution)/shard_map/all_to_all | solution.py:142
  66.1 62.5 %collective-permute-start.1 = (bf16[2048,512]{1,0:T(8,128)(2,1)}, bf16[2048,512]{1,0:T(8,128)(2,1)}, u32[]{:S(2)}, u32[]{:S(2)}) collective-permute-start(bf16[2048,512]{1,0:T(8,128)(2,1)} %bitcast.180), channel_id=1, source_target_pairs={{0,1},{1,0},{2,3},{3,2},{4,5},{5,4},{6,7},{7,6},{8,9},{9,8},{10,11... | collective-permute-start | bytes 6291464 | tf_op jit(solution)/shard_map/ppermute | solution.py:39
  66.6 62.1 %collective-permute-start.2 = (bf16[2048,512]{1,0:T(8,128)(2,1)}, bf16[2048,512]{1,0:T(8,128)(2,1)}, u32[]{:S(2)}, u32[]{:S(2)}) collective-permute-start(bf16[2048,512]{1,0:T(8,128)(2,1)} %bitcast.177), channel_id=1, source_target_pairs={{0,1},{1,0},{2,3},{3,2},{4,5},{5,4},{6,7},{7,6},{8,9},{9,8},{10,11... | collective-permute-start | bytes 6291464 | tf_op jit(solution)/shard_map/ppermute | solution.py:40
  70.6 72.4 %collective-permute-start.3 = (bf16[512,2048]{0,1:T(8,128)(2,1)}, bf16[512,2048]{0,1:T(8,128)(2,1)}, u32[]{:S(2)}, u32[]{:S(2)}) collective-permute-start(bf16[512,2048]{0,1:T(8,128)(2,1)} %bitcast.157), channel_id=1, source_target_pairs={{0,1},{1,0},{2,3},{3,2},{4,5},{5,4},{6,7},{7,6},{8,9},{9,8},{10,11... | collective-permute-start | bytes 6291464 | tf_op jit(solution)/shard_map/ppermute | solution.py:41
  118.7 34.0 %all-to-all-start.4 = ((bf16[64,8,1024]{2,1,0:T(8,128)(2,1)}), bf16[64,8,1024]{2,1,0:T(8,128)(2,1)}, u32[]{:S(2)}, u32[]{:S(2)}) async-start(bf16[64,8,1024]{2,1,0:T(8,128)(2,1)} %bitcast.153), calls=%async_computation.4 | async-start | bytes 2097152 | tf_op jit(solution)/shard_map/all_to_all | solution.py:168
  141.6 1.6 copy-start.4
  152.7 11.8 %copy-start.10 = (f32[256,8]{0,1:T(8,128)S(1)}, f32[256,8]{0,1:T(8,128)}, u32[]{:S(2)}) copy-start(f32[256,8]{0,1:T(8,128)} %param.24) | copy-start | bytes 24580
  152.7 63.1 %all-to-all-start.3 = ((bf16[128,16,1024]{2,1,0:T(8,128)(2,1)}), bf16[128,16,1024]{2,1,0:T(8,128)(2,1)}, u32[]{:S(2)}, u32[]{:S(2)}) async-start(bf16[128,16,1024]{2,1,0:T(8,128)(2,1)} %bitcast.152), calls=%async_computation.3 | async-start | bytes 8388608 | tf_op jit(solution)/shard_map/all_to_all | solution.py:153
  163.0 7.6 %collective-permute-start.4 = (bf16[512,1024]{1,0:T(8,128)(2,1)}, bf16[512,1024]{1,0:T(8,128)(2,1)}, u32[]{:S(2)}, u32[]{:S(2)}) collective-permute-start(bf16[512,1024]{1,0:T(8,128)(2,1)} %bitcast.38), channel_id=1, source_target_pairs={{0,1},{1,0},{2,3},{3,2},{4,5},{5,4},{6,7},{7,6},{8,9},{9,8},{10,11... | collective-permute-start | bytes 3145736 | tf_op jit(solution)/shard_map/ppermute | solution.py:170
  167.4 3.2 %copy-start.12 = (bf16[1,2048,512]{2,1,0:T(8,128)(2,1)S(1)}, bf16[1,2048,512]{2,1,0:T(8,128)(2,1)}, u32[]{:S(2)}) copy-start(bf16[1,2048,512]{2,1,0:T(8,128)(2,1)} %param.26) | copy-start | bytes 6291460
  167.4 3.2 %copy-start.13 = (bf16[1,2048,512]{2,1,0:T(8,128)(2,1)S(1)}, bf16[1,2048,512]{2,1,0:T(8,128)(2,1)}, u32[]{:S(2)}) copy-start(bf16[1,2048,512]{2,1,0:T(8,128)(2,1)} %param.25) | copy-start | bytes 6291460
  170.6 8.1 %copy-start.5 = (bf16[1,512,2048]{1,2,0:T(8,128)(2,1)S(1)}, bf16[1,512,2048]{1,2,0:T(8,128)(2,1)}, u32[]{:S(2)}) copy-start(bf16[1,512,2048]{1,2,0:T(8,128)(2,1)} %copy.69) | copy-start | bytes 6291460
  215.8 25.6 %all-to-all-start.5 = ((bf16[64,8,1024]{2,1,0:T(8,128)(2,1)}), bf16[64,8,1024]{2,1,0:T(8,128)(2,1)}, u32[]{:S(2)}, u32[]{:S(2)}) async-start(bf16[64,8,1024]{2,1,0:T(8,128)(2,1)} %bitcast.165), calls=%async_computation.5 | async-start | bytes 2097152 | tf_op jit(solution)/shard_map/all_to_all | solution.py:182
  241.4 2.1 copy-start.3
  241.4 3.4 %copy-start.1 = (bf16[256,1024]{1,0:T(8,128)(2,1)S(1)}, bf16[256,1024]{1,0:T(8,128)(2,1)}, u32[]{:S(2)}) copy-start(bf16[256,1024]{1,0:T(8,128)(2,1)} %param.16) | copy-start | bytes 1572868

commit v5 on v2

--- a/solution.py
+++ b/solution.py
@@ -115,12 +115,9 @@
             weight_of.T[None, :, :, None],
             0.0,
         )
-        combine = jnp.moveaxis(combine, 2, 0).reshape(rows, -1)
-        combine_hi = combine.astype(jnp.bfloat16)
-        combine_lo = (combine - combine_hi.astype(jnp.float32)).astype(jnp.bfloat16)
-        both = lax.optimization_barrier(jnp.concatenate([combine_hi, combine_lo], 0))
-        parts = jnp.dot(both, back, preferred_element_type=jnp.float32)
-        return parts[:rows] + parts[rows:]
+        combine = jnp.moveaxis(combine, 2, 0).reshape(rows, -1).astype(jnp.bfloat16)
+        combine = lax.optimization_barrier(combine)
+        return jnp.dot(combine, back, preferred_element_type=jnp.float32)
 
     gate_up = jnp.concatenate([gate_full, up_full], 1)
     hidden_units = gate_full.shape[1]

time: 244 us -> 246 us (level)
  waiting for transfers between devices: 108 us -> 114 us
  other arithmetic: 16.1 us -> 12.6 us
    all_to_all x1, waiting for transfers between devices: 24 us -> 45.1 us  [local(): lax.all_to_all(outgoing.reshape(experts, first, D), 'seq', 0, 0, tiled=True)]
    all_to_all x1, waiting for transfers between devices: 12.9 us -> 0.01 us  [local(): lax.all_to_all(outgoing.reshape(experts, over, half), 'seq', 0, 0, tiled=...]
    all_to_all x1, waiting for transfers between devices: 46.1 us -> 33.7 us  [local(): lax.all_to_all(result.reshape(tp_count * experts, first, half), ('tp', 's...]
    all_to_all x1, waiting for transfers between devices: 0.01 us -> 11.9 us  [local(): lax.all_to_all(result.reshape(experts, over, half), 'seq', 0, 0, tiled=True)]
    all_to_all x1, starting transfers between devices: 5.51 us -> 9.91 us  [local(): lax.all_to_all(outgoing.reshape(experts, over, half), 'seq', 0, 0, tiled=...]
    ppermute x1, waiting for transfers between devices: 2.6 us -> 0.01 us  [local(): lax.ppermute(w_gate[0], 'tp', swap)]
    unnamed x32 -> x30, local copies, waits for them, and re-layouts: 6.84 us -> 5.89 us
  transfers between devices with their start and end apart: 11 -> 11, of which waited for: 8 -> 7; matrix products, arithmetic and copies ran while one was open for 23% -> 22% of each run, Pallas kernels for 0% -> 0%
where the time goes in v5:
time: 246 us; the launch traced here: 244 us
  waiting for transfers between devices  114 us (46%)
  starting transfers between devices  56.4 us (23%)
  matrix products  51.5 us (21%)
  other arithmetic  12.6 us (5%)
  local copies, waits for them, and re-layouts  9.05 us (4%)
    all_to_all x1, waiting for transfers between devices, local(): lax.all_to_all(outgoing.reshape(experts, first, D), 'seq', 0, 0, tiled=True)  45.1 us
    all_to_all x1, waiting for transfers between devices, local(): lax.all_to_all(result.reshape(tp_count * experts, first, half), ('tp', 's...  33.7 us
    dot_general x2, matrix products, expert_rows(): both_parts = jnp.dot(arrived, gate_up, preferred_element_type=jnp.float32)  24.3 us
    all_to_all x1, starting transfers between devices, local(): lax.all_to_all(outbound.reshape(seq_count, -1, 128), 'seq', 0, 0, tiled=T...  12 us
    all_to_all x1, waiting for transfers between devices, local(): lax.all_to_all(result.reshape(experts, over, half), 'seq', 0, 0, tiled=True)  11.9 us
    all_to_all x1, starting transfers between devices, local(): lax.all_to_all(result.reshape(tp_count * experts, first, half), ('tp', 's...  10.3 us
    all_to_all x1, starting transfers between devices, local(): lax.all_to_all(outgoing.reshape(experts, over, half), 'seq', 0, 0, tiled=...  9.91 us
    all_to_all x1, waiting for transfers between devices, local(): lax.all_to_all(picked.reshape(seq_count, depth * piece // 128, 128), 'seq...  8.97 us
  transfers between devices with their start and end apart: 11, of which 7 were waited for; matrix products, arithmetic and copies ran while one was open for 22% of the time, Pallas kernels for 0%

profile of v5, /device:TPU:1, one launch (start us, length us, event | category | flops | bytes accessed | tf_op | source)
XLA Modules:
  0.0 244.2 jit_solution(1540289147392939512)
XLA Ops:
  0.0 0.6 compare_reduce_fusion
  0.6 1.3 fusion.76
  2.0 0.9 pad_maximum_fusion.5
  2.9 0.8 reshape.192
  3.7 12.0 %all-to-all-start = ((bf16[64,9,128]{2,1,0:T(8,128)(2,1)}), bf16[64,9,128]{2,1,0:T(8,128)(2,1)S(1)}, u32[]{:S(2)}, u32[]{:S(2)}) async-start(bf16[64,9,128]{2,1,0:T(8,128)(2,1)} %reshape.192), calls=%async_computation | async-start | bytes 524288 | tf_op jit(solution)/shard_map/all_to_all | solution.py:49
  15.7 0.9 select_reduce_fusion.1
  16.5 8.6 %all-to-all-done = bf16[64,9,128]{2,1,0:T(8,128)(2,1)S(1)} async-done(((bf16[64,9,128]{2,1,0:T(8,128)(2,1)}), bf16[64,9,128]{2,1,0:T(8,128)(2,1)S(1)}, u32[]{:S(2)}, u32[]{:S(2)}) %all-to-all-start) | async-done | bytes 147488 | tf_op jit(solution)/shard_map/all_to_all | solution.py:49
  25.3 0.3 convolution_convert_fusion.2
  25.6 0.9 reshape.194
  26.5 4.9 %all-to-all-start.1 = ((bf16[64,24,128]{2,1,0:T(8,128)(2,1)}), bf16[64,24,128]{2,1,0:T(8,128)(2,1)S(1)}, u32[]{:S(2)}, u32[]{:S(2)}) async-start(bf16[64,24,128]{2,1,0:T(8,128)(2,1)} %reshape.194), calls=%async_computation.1 | async-start | bytes 786432 | tf_op jit(solution)/shard_map/all_to_all | solution.py:57
  31.9 0.3 copy.62
  32.4 0.3 copy.67
  32.7 9.0 %all-to-all-done.1 = bf16[64,24,128]{2,1,0:T(8,128)(2,1)S(1)} async-done(((bf16[64,24,128]{2,1,0:T(8,128)(2,1)}), bf16[64,24,128]{2,1,0:T(8,128)(2,1)S(1)}, u32[]{:S(2)}, u32[]{:S(2)}) %all-to-all-start.1) | async-done | bytes 393248 | tf_op jit(solution)/shard_map/all_to_all | solution.py:57
  42.3 0.6 bitcast_reduce_fusion
  42.8 0.6 fusion.2
  43.5 1.1 fusion.46
  44.6 1.0 copy-done.10
  45.7 1.2 convolution_bitcast_fusion
  46.9 3.2 %collective-permute-start = (f32[256,2048]{1,0:T(8,128)S(1)}, f32[256,2048]{1,0:T(8,128)}, u32[]{:S(2)}, u32[]{:S(2)}) collective-permute-start(f32[256,2048]{1,0:T(8,128)S(1)} %convolution_bitcast_fusion), channel_id=1, source_target_pairs={{0,1},{1,0},{2,3},{3,2},{4,5},{5,4},{6,7},{7,6},{8,9},{9,8},{10,11... | collective-permute-start | bytes 6291464 | tf_op jit(solution)/shard_map/ppermute | solution.py:91
  50.5 0.3 fusion.52
  50.8 3.3 %collective-permute-done = f32[256,2048]{1,0:T(8,128)} collective-permute-done((f32[256,2048]{1,0:T(8,128)S(1)}, f32[256,2048]{1,0:T(8,128)}, u32[]{:S(2)}, u32[]{:S(2)}) %collective-permute-start) | collective-permute-done | bytes 2097184 | tf_op jit(solution)/shard_map/ppermute | solution.py:91
  54.0 2.9 %multiply_reduce_fusion = (f32[256]{0:T(256)S(1)}, f32[256,2048]{1,0:T(8,128)S(1)}) fusion(f32[256,2048]{1,0:T(8,128)} %copy-done.5, f32[256,2048]{1,0:T(8,128)} %collective-permute-done, bf16[256,2048]{1,0:T(8,128)(2,1)} %param.15), kind=kLoop, calls=%fused_computation.41 | loop fusion | flops 2621184 | bytes 7341056 | tf_op jit(solution)/shard_map/reduce_sum | solution.py:93
  57.0 0.2 multiply_convert_fusion
  57.2 3.2 %convolution_convert_fusion = bf16[1024,2048]{1,0:T(8,128)(2,1)} fusion(pred[256,1024]{0,1:T(32,128)(4,1)S(1)} %fusion.52, bf16[256,2048]{1,0:T(8,128)(2,1)S(1)} %multiply_convert_fusion), kind=kOutput, calls=%fused_computation.8 | convolution fusion | flops 1075838976 | bytes 5505024 | tf_op jit(solution)/shard_map/ts,td->sd/dot_general | solution.py:157
  60.4 5.7 %all-to-all-start.4 = ((bf16[64,16,2048]{2,1,0:T(8,128)(2,1)}), bf16[64,16,2048]{2,1,0:T(8,128)(2,1)}, u32[]{:S(2)}, u32[]{:S(2)}) async-start(bf16[64,16,2048]{2,1,0:T(8,128)(2,1)} %bitcast.136), calls=%async_computation.4 | async-start | bytes 8388608 | tf_op jit(solution)/shard_map/all_to_all | solution.py:160
  66.1 0.5 collective-permute-start.3
  66.7 3.9 %copy.69 = bf16[1,512,2048]{1,2,0:T(8,128)(2,1)} copy(bf16[1,512,2048]{2,1,0:T(8,128)(2,1)} %param.27) | data formatting | bytes 4194304 | tf_op args[12]
  70.6 0.4 collective-permute-start.4
  71.1 2.5 %fusion.39 = bf16[64,8,1024]{2,1,0:T(8,128)(2,1)} fusion(bf16[256,2048]{1,0:T(8,128)(2,1)} %copy-done.2, s32[]{:T(128)S(6)} %select_n.51, s32[512]{0:T(512)S(1)} %eq.150, s32[256,64]{0,1:T(8,128)S(1)} %convolution_convert_fusion.3, pred[256,64]{0,1:T(8,128)(4,1)S(1)} %fusion.63), kind=kOutput, calls=%fused_computation.52 | convolution fusion | flops 269221888 | bytes 1656836 | tf_op jit(solution)/shard_map/ts,td->sd/dot_general | solution.py:137
  73.7 45.1 %all-to-all-done.4 = bf16[64,16,2048]{2,1,0:T(8,128)(2,1)} async-done(((bf16[64,16,2048]{2,1,0:T(8,128)(2,1)}), bf16[64,16,2048]{2,1,0:T(8,128)(2,1)}, u32[]{:S(2)}, u32[]{:S(2)}) %all-to-all-start.4) | async-done | bytes 4194336 | tf_op jit(solution)/shard_map/all_to_all | solution.py:160
  118.7 9.9 %all-to-all-start.2 = ((bf16[64,8,1024]{2,1,0:T(8,128)(2,1)}), bf16[64,8,1024]{2,1,0:T(8,128)(2,1)}, u32[]{:S(2)}, u32[]{:S(2)}) async-start(bf16[64,8,1024]{2,1,0:T(8,128)(2,1)} %fusion.39), calls=%async_computation.2 | async-start | bytes 2097152 | tf_op jit(solution)/shard_map/all_to_all | solution.py:140
  128.7 12.9 %fusion.38 = f32[1024,2048]{1,0:T(8,128)S(1)} fusion(bf16[1024,2048]{1,0:T(8,128)(2,1)} %bitcast.34, bf16[2048,512]{1,0:T(8,128)(2,1)} %collective-permute-done.3, bf16[2048,512]{1,0:T(8,128)(2,1)} %bitcast.158, bf16[2048,512]{1,0:T(8,128)(2,1)} %collective-permute-done.2, bf16[2048,512]{1,0:T(8,128)(2,1)} %bitcast.161), kind=kOutput, calls=%fused_computation.51 | convolution fusion | flops 8623489024 | bytes 20971520 | tf_op jit(solution)/shard_map/dot_general | solution.py:126
  141.6 1.4 fusion
  143.2 3.6 %convert_bitcast_fusion = bf16[1,1024,1024]{2,1,0:T(8,128)(2,1)S(1)} fusion(bf16[1024,1024]{1,0:T(8,128)(2,1)S(1)} %fusion, bf16[512,2,1024]{0,2,1:T(8,128)(2,1)} %bitcast.24, bf16[512,2,1024]{0,2,1:T(8,128)(2,1)S(1)} %bitcast.140), kind=kOutput, calls=%fused_computation.38 | convolution fusion | flops 2152726528 | bytes 8388608 | tf_op jit(solution)/shard_map/dot_general | solution.py:166
  146.8 3.6 %convert_bitcast_fusion.1 = bf16[1,1024,1024]{2,1,0:T(8,128)(2,1)S(1)} fusion(bf16[1024,1024]{1,0:T(8,128)(2,1)S(1)} %fusion, bf16[512,2,1024]{0,2,1:T(8,128)(2,1)S(1)} %bitcast.141, bf16[512,2,1024]{0,2,1:T(8,128)(2,1)} %bitcast.24), kind=kOutput, calls=%fused_computation.39 | convolution fusion | flops 2152726528 | bytes 8388608 | tf_op jit(solution)/shard_map/dot_general | solution.py:166
  150.4 2.3 pad_maximum_fusion.1
  152.7 10.3 %all-to-all-start.5 = ((bf16[128,16,1024]{2,1,0:T(8,128)(2,1)}), bf16[128,16,1024]{2,1,0:T(8,128)(2,1)}, u32[]{:S(2)}, u32[]{:S(2)}) async-start(bf16[128,16,1024]{2,1,0:T(8,128)(2,1)} %bitcast.137), calls=%async_computation.5 | async-start | bytes 8388608 | tf_op jit(solution)/shard_map/all_to_all | solution.py:170
  163.0 1.4 collective-permute-start.1
  164.4 2.6 %collective-permute-done.1 = bf16[512,1024]{1,0:T(8,128)(2,1)} collective-permute-done((bf16[512,1024]{1,0:T(8,128)(2,1)}, bf16[512,1024]{1,0:T(8,128)(2,1)}, u32[]{:S(2)}, u32[]{:S(2)}) %collective-permute-start.1) | collective-permute-done | bytes 1048608 | tf_op jit(solution)/shard_map/ppermute | solution.py:142
  167.1 11.4 %fusion.18 = f32[512,2048]{1,0:T(8,128)S(1)} fusion(bf16[512,1024]{1,0:T(8,128)(2,1)} %collective-permute-done.1, bf16[512,1024]{1,0:T(8,128)(2,1)} %bitcast.19, pred[]{:T(512)S(6)} %eq.146, bf16[2048,512]{1,0:T(8,128)(2,1)} %collective-permute-done.3, bf16[2048,512]{1,0:T(8,128)(2,1)} %bitcast.159, bf16[2048,512]{1,0:T(8,128)(2,1)} %collective-permute-done.2, ...), kind=kOutput, calls=%fused_computation.29 | convolution fusion | flops 4337958912 | bytes 14680065 | tf_op jit(solution)/shard_map/dot_general | solution.py:126
  178.5 3.5 %fusion.40 = bf16[64,8,1024]{2,1,0:T(8,128)(2,1)} fusion(s32[]{:T(128)S(6)} %select_n.56, bf16[512,2,1024]{0,2,1:T(8,128)(2,1)S(1)} %bitcast.142, bf16[512,2,1024]{0,2,1:T(8,128)(2,1)} %bitcast.24, f32[512,2048]{1,0:T(8,128)S(1)} %fusion.18), kind=kOutput, calls=%fused_computation.53 | convolution fusion | flops 1081606144 | bytes 9437188 | tf_op jit(solution)/shard_map/dot_general | solution.py:149
  182.0 33.7 %all-to-all-done.5 = bf16[128,16,1024]{2,1,0:T(8,128)(2,1)} async-done(((bf16[128,16,1024]{2,1,0:T(8,128)(2,1)}), bf16[128,16,1024]{2,1,0:T(8,128)(2,1)}, u32[]{:S(2)}, u32[]{:S(2)}) %all-to-all-start.5) | async-done | bytes 4194336 | tf_op jit(solution)/shard_map/all_to_all | solution.py:170
  215.8 8.1 %all-to-all-start.3 = ((bf16[64,8,1024]{2,1,0:T(8,128)(2,1)}), bf16[64,8,1024]{2,1,0:T(8,128)(2,1)}, u32[]{:S(2)}, u32[]{:S(2)}) async-start(bf16[64,8,1024]{2,1,0:T(8,128)(2,1)} %fusion.40), calls=%async_computation.3 | async-start | bytes 2097152 | tf_op jit(solution)/shard_map/all_to_all | solution.py:153
  224.1 0.6 fusion.24
  224.7 0.2 fusion.67
  224.9 4.5 %fusion.89 = f32[256,1024]{1,0:T(8,128)} fusion(bf16[256,2048]{0,1:T(8,128)(2,1)S(1)} %fusion.24, bf16[2048,1024]{1,0:T(8,128)(2,1)} %bitcast.40), kind=kOutput, calls=%fused_computation.119 | convolution fusion | flops 1073741824 | bytes 6291456 | tf_op jit(solution)/shard_map/dot_general | solution.py:120
  229.5 11.9 %all-to-all-done.3 = bf16[64,8,1024]{2,1,0:T(8,128)(2,1)} async-done(((bf16[64,8,1024]{2,1,0:T(8,128)(2,1)}), bf16[64,8,1024]{2,1,0:T(8,128)(2,1)}, u32[]{:S(2)}, u32[]{:S(2)}) %all-to-all-start.3) | async-done | bytes 1048608 | tf_op jit(solution)/shard_map/all_to_all | solution.py:153
  241.3 2.8 %add_convert_fusion = bf16[256,1024]{1,0:T(8,128)(2,1)} fusion(f32[256,2048]{1,0:T(8,128)S(1)} %get-tuple-element.18, s32[]{:T(128)S(6)} %select_n.51, f32[256,1024]{1,0:T(8,128)} %fusion.89, bf16[256,512]{0,1:T(8,128)(2,1)S(1)} %fusion.67, bf16[64,8,1024]{2,1,0:T(8,128)(2,1)} %all-to-all-done.3), kind=kOutput, calls=%fused_computation.61 | convolution fusion | flops 269221888 | bytes 3932164 | tf_op jit(solution)/shard_map/dot_general | solution.py:120
  (58 shorter events, 2.4 us)
Async XLA Ops:
  0.0 42.3 %copy-start = (bf16[256,1024]{1,0:T(8,128)(2,1)S(1)}, bf16[256,1024]{1,0:T(8,128)(2,1)}, u32[]{:S(2)}) copy-start(bf16[256,1024]{1,0:T(8,128)(2,1)} %param.16) | copy-start | bytes 1572868
  0.0 31.6 %copy-start.6 = (bf16[2,256,1024]{2,1,0:T(8,128)(2,1)S(1)}, bf16[2,256,1024]{2,1,0:T(8,128)(2,1)}, u32[]{:S(2)}) copy-start(bf16[2,256,1024]{2,1,0:T(8,128)(2,1)} %param.17) | copy-start | bytes 3145732
  3.7 21.4 %all-to-all-start = ((bf16[64,9,128]{2,1,0:T(8,128)(2,1)}), bf16[64,9,128]{2,1,0:T(8,128)(2,1)S(1)}, u32[]{:S(2)}, u32[]{:S(2)}) async-start(bf16[64,9,128]{2,1,0:T(8,128)(2,1)} %reshape.192), calls=%async_computation | async-start | bytes 524288 | tf_op jit(solution)/shard_map/all_to_all | solution.py:49
  26.5 15.1 %all-to-all-start.1 = ((bf16[64,24,128]{2,1,0:T(8,128)(2,1)}), bf16[64,24,128]{2,1,0:T(8,128)(2,1)S(1)}, u32[]{:S(2)}, u32[]{:S(2)}) async-start(bf16[64,24,128]{2,1,0:T(8,128)(2,1)} %reshape.194), calls=%async_computation.1 | async-start | bytes 786432 | tf_op jit(solution)/shard_map/all_to_all | solution.py:57
  43.5 2.2 copy-start.10
  45.7 4.6 %copy-start.7 = (s32[256,8]{0,1:T(8,128)S(1)}, s32[256,8]{0,1:T(8,128)}, u32[]{:S(2)}) copy-start(s32[256,8]{0,1:T(8,128)} %param.23) | copy-start | bytes 24580
  46.9 3.8 %copy-start.5 = (f32[256,2048]{1,0:T(8,128)}, f32[256,2048]{1,0:T(8,128)S(1)}, u32[]{:S(2)}) copy-start(f32[256,2048]{1,0:T(8,128)S(1)} %convolution_bitcast_fusion) | copy-start | bytes 6291460
  46.9 7.1 %collective-permute-start = (f32[256,2048]{1,0:T(8,128)S(1)}, f32[256,2048]{1,0:T(8,128)}, u32[]{:S(2)}, u32[]{:S(2)}) collective-permute-start(f32[256,2048]{1,0:T(8,128)S(1)} %convolution_bitcast_fusion), channel_id=1, source_target_pairs={{0,1},{1,0},{2,3},{3,2},{4,5},{5,4},{6,7},{7,6},{8,9},{9,8},{10,11... | collective-permute-start | bytes 6291464 | tf_op jit(solution)/shard_map/ppermute | solution.py:91
  50.8 6.2 %copy-start.8 = (f32[2048]{0:T(1024)S(1)}, f32[2048]{0:T(1024)}, u32[]{:S(2)}) copy-start(f32[2048]{0:T(1024)} %param.22) | copy-start | bytes 24580
  57.2 3.2 %copy-start.2 = (bf16[256,2048]{1,0:T(8,128)(2,1)}, bf16[256,2048]{1,0:T(8,128)(2,1)S(1)}, u32[]{:S(2)}) copy-start(bf16[256,2048]{1,0:T(8,128)(2,1)S(1)} %multiply_convert_fusion) | copy-start | bytes 3145732
  60.4 58.3 %all-to-all-start.4 = ((bf16[64,16,2048]{2,1,0:T(8,128)(2,1)}), bf16[64,16,2048]{2,1,0:T(8,128)(2,1)}, u32[]{:S(2)}, u32[]{:S(2)}) async-start(bf16[64,16,2048]{2,1,0:T(8,128)(2,1)} %bitcast.136), calls=%async_computation.4 | async-start | bytes 8388608 | tf_op jit(solution)/shard_map/all_to_all | solution.py:160
  66.1 62.5 %collective-permute-start.3 = (bf16[2048,512]{1,0:T(8,128)(2,1)}, bf16[2048,512]{1,0:T(8,128)(2,1)}, u32[]{:S(2)}, u32[]{:S(2)}) collective-permute-start(bf16[2048,512]{1,0:T(8,128)(2,1)} %bitcast.157), channel_id=1, source_target_pairs={{0,1},{1,0},{2,3},{3,2},{4,5},{5,4},{6,7},{7,6},{8,9},{9,8},{10,11... | collective-permute-start | bytes 6291464 | tf_op jit(solution)/shard_map/ppermute | solution.py:40
  66.6 62.1 %collective-permute-start.2 = (bf16[2048,512]{1,0:T(8,128)(2,1)}, bf16[2048,512]{1,0:T(8,128)(2,1)}, u32[]{:S(2)}, u32[]{:S(2)}) collective-permute-start(bf16[2048,512]{1,0:T(8,128)(2,1)} %bitcast.160), channel_id=1, source_target_pairs={{0,1},{1,0},{2,3},{3,2},{4,5},{5,4},{6,7},{7,6},{8,9},{9,8},{10,11... | collective-permute-start | bytes 6291464 | tf_op jit(solution)/shard_map/ppermute | solution.py:39
  70.6 72.3 %collective-permute-start.4 = (bf16[512,2048]{0,1:T(8,128)(2,1)}, bf16[512,2048]{0,1:T(8,128)(2,1)}, u32[]{:S(2)}, u32[]{:S(2)}) collective-permute-start(bf16[512,2048]{0,1:T(8,128)(2,1)} %bitcast.139), channel_id=1, source_target_pairs={{0,1},{1,0},{2,3},{3,2},{4,5},{5,4},{6,7},{7,6},{8,9},{9,8},{10,11... | collective-permute-start | bytes 6291464 | tf_op jit(solution)/shard_map/ppermute | solution.py:41
  118.7 34.0 %all-to-all-start.2 = ((bf16[64,8,1024]{2,1,0:T(8,128)(2,1)}), bf16[64,8,1024]{2,1,0:T(8,128)(2,1)}, u32[]{:S(2)}, u32[]{:S(2)}) async-start(bf16[64,8,1024]{2,1,0:T(8,128)(2,1)} %fusion.39), calls=%async_computation.2 | async-start | bytes 2097152 | tf_op jit(solution)/shard_map/all_to_all | solution.py:140
  141.6 1.6 copy-start.3
  152.7 63.1 %all-to-all-start.5 = ((bf16[128,16,1024]{2,1,0:T(8,128)(2,1)}), bf16[128,16,1024]{2,1,0:T(8,128)(2,1)}, u32[]{:S(2)}, u32[]{:S(2)}) async-start(bf16[128,16,1024]{2,1,0:T(8,128)(2,1)} %bitcast.137), calls=%async_computation.5 | async-start | bytes 8388608 | tf_op jit(solution)/shard_map/all_to_all | solution.py:170
  163.0 4.1 %collective-permute-start.1 = (bf16[512,1024]{1,0:T(8,128)(2,1)}, bf16[512,1024]{1,0:T(8,128)(2,1)}, u32[]{:S(2)}, u32[]{:S(2)}) collective-permute-start(bf16[512,1024]{1,0:T(8,128)(2,1)} %bitcast.19), channel_id=1, source_target_pairs={{0,1},{1,0},{2,3},{3,2},{4,5},{5,4},{6,7},{7,6},{8,9},{9,8},{10,11... | collective-permute-start | bytes 3145736 | tf_op jit(solution)/shard_map/ppermute | solution.py:142
  164.4 14.0 %copy-start.4 = (bf16[1,512,2048]{1,2,0:T(8,128)(2,1)S(1)}, bf16[1,512,2048]{1,2,0:T(8,128)(2,1)}, u32[]{:S(2)}) copy-start(bf16[1,512,2048]{1,2,0:T(8,128)(2,1)} %copy.69) | copy-start | bytes 6291460
  178.5 45.5 %copy-start.9 = (f32[256,8]{0,1:T(8,128)S(1)}, f32[256,8]{0,1:T(8,128)}, u32[]{:S(2)}) copy-start(f32[256,8]{0,1:T(8,128)} %param.24) | copy-start | bytes 24580
  215.8 25.6 %all-to-all-start.3 = ((bf16[64,8,1024]{2,1,0:T(8,128)(2,1)}), bf16[64,8,1024]{2,1,0:T(8,128)(2,1)}, u32[]{:S(2)}, u32[]{:S(2)}) async-start(bf16[64,8,1024]{2,1,0:T(8,128)(2,1)} %fusion.40), calls=%async_computation.3 | async-start | bytes 2097152 | tf_op jit(solution)/shard_map/all_to_all | solution.py:153
  224.9 19.2 %copy-start.1 = (bf16[256,1024]{1,0:T(8,128)(2,1)S(1)}, bf16[256,1024]{1,0:T(8,128)(2,1)}, u32[]{:S(2)}) copy-start(bf16[256,1024]{1,0:T(8,128)(2,1)} %param.16) | copy-start | bytes 1572868

commit v6 on v2

--- a/solution.py
+++ b/solution.py
@@ -166,18 +166,31 @@
     act = expert_rows(arrived)
     result = jnp.stack(
         [
-            jnp.dot(act, down_cols[:, u], preferred_element_type=jnp.float32).astype(jnp.bfloat16)
+            jnp.dot(act, down_cols[:, u], preferred_element_type=jnp.float32)
+            .astype(jnp.bfloat16)
+            .reshape(experts, first, half)
             for u in range(tp_count)
-        ]
+        ],
+        axis=1,
     )
     back = lax.all_to_all(
-        result.reshape(tp_count * experts, first, half), ("tp", "seq"), 0, 0, tiled=True
+        result.reshape(experts * tp_count, first, half), ("seq", "tp"), 0, 0, tiled=True
     )
     spot = (
         tp_count * jnp.arange(first, dtype=jnp.int32)[None, :]
         + jnp.arange(tp_count, dtype=jnp.int32)[:, None]
     )
-    mixture = mixture + combine_with(back.reshape(-1, half), spot)
+    combine = jnp.where(
+        chosen.T[:, None, :, None] & (ranks.T[:, None, :, None] == spot[None, :, None, :]),
+        weight_of.T[:, None, :, None],
+        0.0,
+    )
+    combine = jnp.moveaxis(combine, 2, 0).reshape(rows, -1)
+    combine_hi = combine.astype(jnp.bfloat16)
+    combine_lo = (combine - combine_hi.astype(jnp.float32)).astype(jnp.bfloat16)
+    both = lax.optimization_barrier(jnp.concatenate([combine_hi, combine_lo], 0))
+    parts = jnp.dot(both, back.reshape(-1, half), preferred_element_type=jnp.float32)
+    mixture = mixture + (parts[:rows] + parts[rows:])
     residual = lax.dynamic_slice_in_dim(hidden_state, tp_index * half, half, 1)
     return (residual + mixture).astype(jnp.bfloat16)
 

time: 244 us -> 244 us (level)
    dot_general x2 -> x1, matrix products: 8.59 us -> 3.27 us  [combine_with(): parts = jnp.dot(both, back, preferred_element_type=jnp.float32)]
    dot_general x0 -> x1, matrix products: none -> 5.31 us  [local(): jnp.dot(both, back.reshape(-1, half), preferred_element_type=jnp.float32)]
where the time goes in v6:
time: 244 us; the launch traced here: 243 us
  waiting for transfers between devices  108 us (44%)
  starting transfers between devices  54.8 us (22%)
  matrix products  53.1 us (22%)
  other arithmetic  16.1 us (7%)
  local copies, waits for them, and re-layouts  10.1 us (4%)
    all_to_all x1, waiting for transfers between devices, local(): lax.all_to_all(result.reshape(experts * tp_count, first, half), ('seq', '...  46.1 us
    dot_general x2, matrix products, expert_rows(): both_parts = jnp.dot(arrived, gate_up, preferred_element_type=jnp.float32)  24.4 us
    all_to_all x1, waiting for transfers between devices, local(): lax.all_to_all(outgoing.reshape(experts, first, D), 'seq', 0, 0, tiled=True)  24 us
    all_to_all x1, waiting for transfers between devices, local(): lax.all_to_all(outgoing.reshape(experts, over, half), 'seq', 0, 0, tiled=...  12.9 us
    all_to_all x1, starting transfers between devices, local(): lax.all_to_all(outbound.reshape(seq_count, -1, 128), 'seq', 0, 0, tiled=T...  12 us
    all_to_all x1, starting transfers between devices, local(): lax.all_to_all(result.reshape(experts * tp_count, first, half), ('seq', '...  10.8 us
    all_to_all x1, starting transfers between devices, local(): lax.all_to_all(result.reshape(experts, over, half), 'seq', 0, 0, tiled=True)  10.2 us
    all_to_all x1, waiting for transfers between devices, local(): lax.all_to_all(picked.reshape(seq_count, depth * piece // 128, 128), 'seq...  8.97 us
  transfers between devices with their start and end apart: 11, of which 8 were waited for; matrix products, arithmetic and copies ran while one was open for 23% of the time, Pallas kernels for 0%

profile of v6, /device:TPU:1, one launch (start us, length us, event | category | flops | bytes accessed | tf_op | source)
XLA Modules:
  0.0 242.6 jit_solution(16774197050859327315)
XLA Ops:
  0.0 0.6 compare_reduce_fusion
  0.6 1.3 fusion.84
  2.0 0.9 pad_maximum_fusion.7
  2.9 0.8 reshape.196
  3.7 12.0 %all-to-all-start = ((bf16[64,9,128]{2,1,0:T(8,128)(2,1)}), bf16[64,9,128]{2,1,0:T(8,128)(2,1)S(1)}, u32[]{:S(2)}, u32[]{:S(2)}) async-start(bf16[64,9,128]{2,1,0:T(8,128)(2,1)} %reshape.196), calls=%async_computation | async-start | bytes 524288 | tf_op jit(solution)/shard_map/all_to_all | solution.py:49
  15.7 0.9 select_reduce_fusion.1
  16.5 8.6 %all-to-all-done = bf16[64,9,128]{2,1,0:T(8,128)(2,1)S(1)} async-done(((bf16[64,9,128]{2,1,0:T(8,128)(2,1)}), bf16[64,9,128]{2,1,0:T(8,128)(2,1)S(1)}, u32[]{:S(2)}, u32[]{:S(2)}) %all-to-all-start) | async-done | bytes 147488 | tf_op jit(solution)/shard_map/all_to_all | solution.py:49
  25.3 0.3 convolution_convert_fusion.2
  25.6 0.9 reshape.198
  26.5 4.9 %all-to-all-start.1 = ((bf16[64,24,128]{2,1,0:T(8,128)(2,1)}), bf16[64,24,128]{2,1,0:T(8,128)(2,1)S(1)}, u32[]{:S(2)}, u32[]{:S(2)}) async-start(bf16[64,24,128]{2,1,0:T(8,128)(2,1)} %reshape.198), calls=%async_computation.1 | async-start | bytes 786432 | tf_op jit(solution)/shard_map/all_to_all | solution.py:57
  31.9 0.3 copy.68
  32.7 9.0 %all-to-all-done.1 = bf16[64,24,128]{2,1,0:T(8,128)(2,1)S(1)} async-done(((bf16[64,24,128]{2,1,0:T(8,128)(2,1)}), bf16[64,24,128]{2,1,0:T(8,128)(2,1)S(1)}, u32[]{:S(2)}, u32[]{:S(2)}) %all-to-all-start.1) | async-done | bytes 393248 | tf_op jit(solution)/shard_map/all_to_all | solution.py:57
  42.3 0.6 bitcast_reduce_fusion
  42.8 0.6 fusion.2
  43.5 1.1 fusion.50
  44.6 1.0 copy-done.11
  45.7 1.2 convolution_bitcast_fusion
  46.9 3.2 %collective-permute-start = (f32[256,2048]{1,0:T(8,128)S(1)}, f32[256,2048]{1,0:T(8,128)}, u32[]{:S(2)}, u32[]{:S(2)}) collective-permute-start(f32[256,2048]{1,0:T(8,128)S(1)} %convolution_bitcast_fusion), channel_id=1, source_target_pairs={{0,1},{1,0},{2,3},{3,2},{4,5},{5,4},{6,7},{7,6},{8,9},{9,8},{10,11... | collective-permute-start | bytes 6291464 | tf_op jit(solution)/shard_map/ppermute | solution.py:91
  50.5 3.5 %collective-permute-done = f32[256,2048]{1,0:T(8,128)} collective-permute-done((f32[256,2048]{1,0:T(8,128)S(1)}, f32[256,2048]{1,0:T(8,128)}, u32[]{:S(2)}, u32[]{:S(2)}) %collective-permute-start) | collective-permute-done | bytes 2097184 | tf_op jit(solution)/shard_map/ppermute | solution.py:91
  54.0 2.9 %multiply_reduce_fusion = (f32[256]{0:T(256)S(1)}, f32[256,2048]{1,0:T(8,128)S(1)}) fusion(f32[256,2048]{1,0:T(8,128)} %copy-done.6, f32[256,2048]{1,0:T(8,128)} %collective-permute-done, bf16[256,2048]{1,0:T(8,128)(2,1)} %param.15), kind=kLoop, calls=%fused_computation.42 | loop fusion | flops 2621184 | bytes 7341056 | tf_op jit(solution)/shard_map/reduce_sum | solution.py:93
  57.2 1.0 copy-done.3
  58.2 1.5 fusion.43
  59.7 5.5 %all-to-all-start.2 = ((bf16[64,8,1024]{2,1,0:T(8,128)(2,1)}), bf16[64,8,1024]{2,1,0:T(8,128)(2,1)}, u32[]{:S(2)}, u32[]{:S(2)}) async-start(bf16[64,8,1024]{2,1,0:T(8,128)(2,1)} %fusion.43), calls=%async_computation.2 | async-start | bytes 2097152 | tf_op jit(solution)/shard_map/all_to_all | solution.py:143
  65.5 4.4 %convolution_convert_fusion = bf16[1024,2048]{1,0:T(8,128)(2,1)} fusion(pred[256,1024]{0,1:T(32,128)(4,1)S(1)} %fusion.60, bf16[256,2048]{1,0:T(8,128)(2,1)} %copy-done.3), kind=kOutput, calls=%fused_computation.8 | convolution fusion | flops 1075838976 | bytes 5505024 | tf_op jit(solution)/shard_map/ts,td->sd/dot_general | solution.py:160
  70.0 12.9 %all-to-all-done.2 = bf16[64,8,1024]{2,1,0:T(8,128)(2,1)} async-done(((bf16[64,8,1024]{2,1,0:T(8,128)(2,1)}), bf16[64,8,1024]{2,1,0:T(8,128)(2,1)}, u32[]{:S(2)}, u32[]{:S(2)}) %all-to-all-start.2) | async-done | bytes 1048608 | tf_op jit(solution)/shard_map/all_to_all | solution.py:143
  82.9 5.8 %all-to-all-start.4 = ((bf16[64,16,2048]{2,1,0:T(8,128)(2,1)}), bf16[64,16,2048]{2,1,0:T(8,128)(2,1)}, u32[]{:S(2)}, u32[]{:S(2)}) async-start(bf16[64,16,2048]{2,1,0:T(8,128)(2,1)} %bitcast.157), calls=%async_computation.4 | async-start | bytes 8388608 | tf_op jit(solution)/shard_map/all_to_all | solution.py:163
  88.7 1.9 collective-permute-start.3
  90.7 0.4 collective-permute-start.1
  91.1 3.9 %copy.75 = bf16[1,512,2048]{1,2,0:T(8,128)(2,1)} copy(bf16[1,512,2048]{2,1,0:T(8,128)(2,1)} %param.27) | data formatting | bytes 4194304 | tf_op args[12]
  95.1 2.6 %collective-permute-done.2 = bf16[2048,512]{1,0:T(8,128)(2,1)} collective-permute-done((bf16[2048,512]{1,0:T(8,128)(2,1)}, bf16[2048,512]{1,0:T(8,128)(2,1)}, u32[]{:S(2)}, u32[]{:S(2)}) %collective-permute-start.2) | collective-permute-done | bytes 2097184 | tf_op jit(solution)/shard_map/ppermute | solution.py:39
  97.7 1.5 collective-permute-done.1
  99.2 11.5 %fusion.18 = f32[512,2048]{1,0:T(8,128)S(1)} fusion(bf16[512,1024]{1,0:T(8,128)(2,1)} %collective-permute-done.1, bf16[512,1024]{1,0:T(8,128)(2,1)} %bitcast.20, pred[]{:T(512)S(6)} %eq.146, bf16[2048,512]{1,0:T(8,128)(2,1)} %collective-permute-done.3, bf16[2048,512]{1,0:T(8,128)(2,1)} %bitcast.184, bf16[2048,512]{1,0:T(8,128)(2,1)} %collective-permute-done.2, ...), kind=kOutput, calls=%fused_computation.29 | convolution fusion | flops 4337958912 | bytes 14680065 | tf_op jit(solution)/shard_map/dot_general | solution.py:129
  110.8 3.5 %fusion.44 = bf16[64,8,1024]{2,1,0:T(8,128)(2,1)} fusion(s32[]{:T(128)S(6)} %select_n.56, bf16[512,2,1024]{0,2,1:T(8,128)(2,1)S(1)} %bitcast.163, bf16[512,2,1024]{0,2,1:T(8,128)(2,1)} %bitcast.25, f32[512,2048]{1,0:T(8,128)S(1)} %fusion.18), kind=kOutput, calls=%fused_computation.56 | convolution fusion | flops 1081606144 | bytes 9437188 | tf_op jit(solution)/shard_map/dot_general | solution.py:152
  114.3 24.0 %all-to-all-done.4 = bf16[64,16,2048]{2,1,0:T(8,128)(2,1)} async-done(((bf16[64,16,2048]{2,1,0:T(8,128)(2,1)}), bf16[64,16,2048]{2,1,0:T(8,128)(2,1)}, u32[]{:S(2)}, u32[]{:S(2)}) %all-to-all-start.4) | async-done | bytes 4194336 | tf_op jit(solution)/shard_map/all_to_all | solution.py:163
  138.3 10.2 %all-to-all-start.3 = ((bf16[64,8,1024]{2,1,0:T(8,128)(2,1)}), bf16[64,8,1024]{2,1,0:T(8,128)(2,1)}, u32[]{:S(2)}, u32[]{:S(2)}) async-start(bf16[64,8,1024]{2,1,0:T(8,128)(2,1)} %fusion.44), calls=%async_computation.3 | async-start | bytes 2097152 | tf_op jit(solution)/shard_map/all_to_all | solution.py:156
  148.5 12.9 %fusion.42 = f32[1024,2048]{1,0:T(8,128)S(1)} fusion(bf16[1024,2048]{1,0:T(8,128)(2,1)} %bitcast.35, bf16[2048,512]{1,0:T(8,128)(2,1)} %collective-permute-done.3, bf16[2048,512]{1,0:T(8,128)(2,1)} %bitcast.185, bf16[2048,512]{1,0:T(8,128)(2,1)} %collective-permute-done.2, bf16[2048,512]{1,0:T(8,128)(2,1)} %bitcast.188), kind=kOutput, calls=%fused_computation.54 | convolution fusion | flops 8623489024 | bytes 20971520 | tf_op jit(solution)/shard_map/dot_general | solution.py:129
  161.4 1.4 fusion
  163.0 3.6 %fusion.29 = bf16[1024,1024]{1,0:T(8,128)(2,1)S(1)} fusion(bf16[1024,1024]{1,0:T(8,128)(2,1)S(1)} %fusion, bf16[512,2,1024]{0,2,1:T(8,128)(2,1)} %bitcast.25, bf16[512,2,1024]{0,2,1:T(8,128)(2,1)S(1)} %bitcast.164), kind=kOutput, calls=%fused_computation.46 | convolution fusion | flops 2152726528 | bytes 8388608 | tf_op jit(solution)/shard_map/dot_general | solution.py:169
  166.6 3.6 %fusion.32 = bf16[1024,1024]{1,0:T(8,128)(2,1)S(1)} fusion(bf16[1024,1024]{1,0:T(8,128)(2,1)S(1)} %fusion, bf16[512,2,1024]{0,2,1:T(8,128)(2,1)S(1)} %bitcast.165, bf16[512,2,1024]{0,2,1:T(8,128)(2,1)} %bitcast.25), kind=kOutput, calls=%fused_computation.47 | convolution fusion | flops 2152726528 | bytes 8388608 | tf_op jit(solution)/shard_map/dot_general | solution.py:169
  170.1 2.3 pad_maximum_fusion.1
  172.5 10.8 %all-to-all-start.5 = ((bf16[128,16,1024]{2,1,0:T(8,128)(2,1)}), bf16[128,16,1024]{2,1,0:T(8,128)(2,1)}, u32[]{:S(2)}, u32[]{:S(2)}) async-start(bf16[128,16,1024]{2,1,0:T(8,128)(2,1)} %bitcast.158), calls=%async_computation.5 | async-start | bytes 8388608 | tf_op jit(solution)/shard_map/all_to_all | solution.py:176
  183.5 0.6 fusion.26
  184.2 0.6 fusion.25
  184.7 1.5 pad_maximum_fusion.3
  186.7 3.3 %fusion.57 = f32[512,1024]{1,0:T(8,128)} fusion(bf16[512,512]{0,1:T(8,128)(2,1)S(1)} %pad_maximum_fusion.6, bf16[64,8,1024]{2,1,0:T(8,128)(2,1)} %all-to-all-done.3), kind=kOutput, calls=%fused_computation.67 | convolution fusion | flops 536870912 | bytes 3670016 | tf_op jit(solution)/shard_map/dot_general | solution.py:122
  190.0 46.1 %all-to-all-done.5 = bf16[128,16,1024]{2,1,0:T(8,128)(2,1)} async-done(((bf16[128,16,1024]{2,1,0:T(8,128)(2,1)}), bf16[128,16,1024]{2,1,0:T(8,128)(2,1)}, u32[]{:S(2)}, u32[]{:S(2)}) %all-to-all-start.5) | async-done | bytes 4194336 | tf_op jit(solution)/shard_map/all_to_all | solution.py:176
  236.1 5.3 %fusion.97 = f32[512,1024]{1,0:T(8,128)S(1)} fusion(bf16[512,2048]{0,1:T(8,128)(2,1)} %pad_maximum_fusion.3, bf16[2048,1024]{1,0:T(8,128)(2,1)} %bitcast.43), kind=kOutput, calls=%fused_computation.129 | convolution fusion | flops 2147483648 | bytes 8388608 | tf_op jit(solution)/shard_map/dot_general | solution.py:192
  241.4 1.2 fusion.56
  (65 shorter events, 3.7 us)
Async XLA Ops:
  0.0 42.3 %copy-start = (bf16[256,1024]{1,0:T(8,128)(2,1)S(1)}, bf16[256,1024]{1,0:T(8,128)(2,1)}, u32[]{:S(2)}) copy-start(bf16[256,1024]{1,0:T(8,128)(2,1)} %param.16) | copy-start | bytes 1572868
  0.0 31.6 %copy-start.7 = (bf16[2,256,1024]{2,1,0:T(8,128)(2,1)S(1)}, bf16[2,256,1024]{2,1,0:T(8,128)(2,1)}, u32[]{:S(2)}) copy-start(bf16[2,256,1024]{2,1,0:T(8,128)(2,1)} %param.17) | copy-start | bytes 3145732
  3.7 21.4 %all-to-all-start = ((bf16[64,9,128]{2,1,0:T(8,128)(2,1)}), bf16[64,9,128]{2,1,0:T(8,128)(2,1)S(1)}, u32[]{:S(2)}, u32[]{:S(2)}) async-start(bf16[64,9,128]{2,1,0:T(8,128)(2,1)} %reshape.196), calls=%async_computation | async-start | bytes 524288 | tf_op jit(solution)/shard_map/all_to_all | solution.py:49
  26.5 15.1 %all-to-all-start.1 = ((bf16[64,24,128]{2,1,0:T(8,128)(2,1)}), bf16[64,24,128]{2,1,0:T(8,128)(2,1)S(1)}, u32[]{:S(2)}, u32[]{:S(2)}) async-start(bf16[64,24,128]{2,1,0:T(8,128)(2,1)} %reshape.198), calls=%async_computation.1 | async-start | bytes 786432 | tf_op jit(solution)/shard_map/all_to_all | solution.py:57
  43.5 2.2 copy-start.11
  45.7 4.6 %copy-start.8 = (s32[256,8]{0,1:T(8,128)S(1)}, s32[256,8]{0,1:T(8,128)}, u32[]{:S(2)}) copy-start(s32[256,8]{0,1:T(8,128)} %param.23) | copy-start | bytes 24580
  46.9 3.6 %copy-start.6 = (f32[256,2048]{1,0:T(8,128)}, f32[256,2048]{1,0:T(8,128)S(1)}, u32[]{:S(2)}) copy-start(f32[256,2048]{1,0:T(8,128)S(1)} %convolution_bitcast_fusion) | copy-start | bytes 6291460
  46.9 7.1 %collective-permute-start = (f32[256,2048]{1,0:T(8,128)S(1)}, f32[256,2048]{1,0:T(8,128)}, u32[]{:S(2)}, u32[]{:S(2)}) collective-permute-start(f32[256,2048]{1,0:T(8,128)S(1)} %convolution_bitcast_fusion), channel_id=1, source_target_pairs={{0,1},{1,0},{2,3},{3,2},{4,5},{5,4},{6,7},{7,6},{8,9},{9,8},{10,11... | collective-permute-start | bytes 6291464 | tf_op jit(solution)/shard_map/ppermute | solution.py:91
  50.5 6.4 %copy-start.9 = (f32[2048]{0:T(1024)S(1)}, f32[2048]{0:T(1024)}, u32[]{:S(2)}) copy-start(f32[2048]{0:T(1024)} %param.22) | copy-start | bytes 24580
  57.2 1.0 copy-start.3
  59.7 23.2 %all-to-all-start.2 = ((bf16[64,8,1024]{2,1,0:T(8,128)(2,1)}), bf16[64,8,1024]{2,1,0:T(8,128)(2,1)}, u32[]{:S(2)}, u32[]{:S(2)}) async-start(bf16[64,8,1024]{2,1,0:T(8,128)(2,1)} %fusion.43), calls=%async_computation.2 | async-start | bytes 2097152 | tf_op jit(solution)/shard_map/all_to_all | solution.py:143
  82.9 55.4 %all-to-all-start.4 = ((bf16[64,16,2048]{2,1,0:T(8,128)(2,1)}), bf16[64,16,2048]{2,1,0:T(8,128)(2,1)}, u32[]{:S(2)}, u32[]{:S(2)}) async-start(bf16[64,16,2048]{2,1,0:T(8,128)(2,1)} %bitcast.157), calls=%async_computation.4 | async-start | bytes 8388608 | tf_op jit(solution)/shard_map/all_to_all | solution.py:163
  88.7 6.4 %collective-permute-start.3 = (bf16[2048,512]{1,0:T(8,128)(2,1)}, bf16[2048,512]{1,0:T(8,128)(2,1)}, u32[]{:S(2)}, u32[]{:S(2)}) collective-permute-start(bf16[2048,512]{1,0:T(8,128)(2,1)} %bitcast.183), channel_id=1, source_target_pairs={{0,1},{1,0},{2,3},{3,2},{4,5},{5,4},{6,7},{7,6},{8,9},{9,8},{10,11... | collective-permute-start | bytes 6291464 | tf_op jit(solution)/shard_map/ppermute | solution.py:40
  90.6 7.1 %collective-permute-start.2 = (bf16[2048,512]{1,0:T(8,128)(2,1)}, bf16[2048,512]{1,0:T(8,128)(2,1)}, u32[]{:S(2)}, u32[]{:S(2)}) collective-permute-start(bf16[2048,512]{1,0:T(8,128)(2,1)} %bitcast.186), channel_id=1, source_target_pairs={{0,1},{1,0},{2,3},{3,2},{4,5},{5,4},{6,7},{7,6},{8,9},{9,8},{10,11... | collective-permute-start | bytes 6291464 | tf_op jit(solution)/shard_map/ppermute | solution.py:39
  90.7 8.5 %collective-permute-start.1 = (bf16[512,1024]{1,0:T(8,128)(2,1)}, bf16[512,1024]{1,0:T(8,128)(2,1)}, u32[]{:S(2)}, u32[]{:S(2)}) collective-permute-start(bf16[512,1024]{1,0:T(8,128)(2,1)} %bitcast.20), channel_id=1, source_target_pairs={{0,1},{1,0},{2,3},{3,2},{4,5},{5,4},{6,7},{7,6},{8,9},{9,8},{10,11... | collective-permute-start | bytes 3145736 | tf_op jit(solution)/shard_map/ppermute | solution.py:145
  95.0 15.7 %collective-permute-start.4 = (bf16[512,2048]{0,1:T(8,128)(2,1)}, bf16[512,2048]{0,1:T(8,128)(2,1)}, u32[]{:S(2)}, u32[]{:S(2)}) collective-permute-start(bf16[512,2048]{0,1:T(8,128)(2,1)} %bitcast.162), channel_id=1, source_target_pairs={{0,1},{1,0},{2,3},{3,2},{4,5},{5,4},{6,7},{7,6},{8,9},{9,8},{10,11... | collective-permute-start | bytes 6291464 | tf_op jit(solution)/shard_map/ppermute | solution.py:41
  95.1 15.6 %copy-start.4 = (bf16[1,512,2048]{1,2,0:T(8,128)(2,1)S(1)}, bf16[1,512,2048]{1,2,0:T(8,128)(2,1)}, u32[]{:S(2)}) copy-start(bf16[1,512,2048]{1,2,0:T(8,128)(2,1)} %copy.75) | copy-start | bytes 6291460
  138.3 34.2 %all-to-all-start.3 = ((bf16[64,8,1024]{2,1,0:T(8,128)(2,1)}), bf16[64,8,1024]{2,1,0:T(8,128)(2,1)}, u32[]{:S(2)}, u32[]{:S(2)}) async-start(bf16[64,8,1024]{2,1,0:T(8,128)(2,1)} %fusion.44), calls=%async_computation.3 | async-start | bytes 2097152 | tf_op jit(solution)/shard_map/all_to_all | solution.py:156
  161.4 1.6 copy-start.5
  172.5 11.0 %copy-start.10 = (f32[256,8]{0,1:T(8,128)S(1)}, f32[256,8]{0,1:T(8,128)}, u32[]{:S(2)}) copy-start(f32[256,8]{0,1:T(8,128)} %param.24) | copy-start | bytes 24580
  172.5 63.6 %all-to-all-start.5 = ((bf16[128,16,1024]{2,1,0:T(8,128)(2,1)}), bf16[128,16,1024]{2,1,0:T(8,128)(2,1)}, u32[]{:S(2)}, u32[]{:S(2)}) async-start(bf16[128,16,1024]{2,1,0:T(8,128)(2,1)} %bitcast.158), calls=%async_computation.5 | async-start | bytes 8388608 | tf_op jit(solution)/shard_map/all_to_all | solution.py:176
  236.1 5.3 %copy-start.2 = (f32[512,1024]{1,0:T(8,128)S(1)}, f32[512,1024]{1,0:T(8,128)}, u32[]{:S(2)}) copy-start(f32[512,1024]{1,0:T(8,128)} %fusion.57) | copy-start | bytes 6291460
  236.1 6.6 %copy-start.1 = (bf16[256,1024]{1,0:T(8,128)(2,1)S(1)}, bf16[256,1024]{1,0:T(8,128)(2,1)}, u32[]{:S(2)}) copy-start(bf16[256,1024]{1,0:T(8,128)(2,1)} %param.16) | copy-start | bytes 1572868

commit v7 on v6

--- a/solution.py
+++ b/solution.py
@@ -66,21 +66,35 @@
         jnp.where(my_nodes[:, None] == node_ids[None, :], node_len[None, :], 0), axis=1
     )
     live = (jnp.arange(slot, dtype=jnp.int32)[None, :] < lengths[:, None]).reshape(-1)
-    live_all = jnp.concatenate([jnp.ones((rows,), dtype=bool), live])
 
     queries = query.reshape(rows, heads_here, HD)
-    keys = jnp.concatenate([suffix_kv[0].reshape(rows, heads_here, HD), prefix_keys], 0)
-    values = jnp.concatenate(
-        [suffix_kv[1].reshape(rows, heads_here, HD), prefix_values], 0
-    ).astype(jnp.float32)
+    own_scores = (
+        jnp.einsum(
+            "qhd,khd->hqk",
+            queries,
+            suffix_kv[0].reshape(rows, heads_here, HD),
+            preferred_element_type=jnp.float32,
+        )
+        * scale
+    )
+    own_top = jnp.max(own_scores, axis=2)
+    own_probs = jnp.exp(own_scores - own_top[:, :, None])
+    own_total = jnp.sum(own_probs, axis=2)
+    own_accum = jnp.einsum(
+        "hqk,khd->hqd", own_probs, suffix_kv[1].reshape(rows, heads_here, HD).astype(jnp.float32)
+    )
     scores = (
-        jnp.einsum("qhd,khd->hqk", queries, keys, preferred_element_type=jnp.float32) * scale
-    )
-    scores = jnp.where(live_all[None, None, :], scores, -jnp.inf)
-    top = jnp.max(scores, axis=2)
+        jnp.einsum("qhd,khd->hqk", queries, prefix_keys, preferred_element_type=jnp.float32)
+        * scale
+    )
+    scores = jnp.where(live[None, None, :], scores, -jnp.inf)
+    top = jnp.maximum(own_top, jnp.max(scores, axis=2))
     probs = jnp.exp(scores - top[:, :, None])
-    total = jnp.sum(probs, axis=2)
-    accum = jnp.einsum("hqk,khd->hqd", probs, values)
+    factor = jnp.exp(own_top - top)
+    total = own_total * factor + jnp.sum(probs, axis=2)
+    accum = own_accum * factor[:, :, None] + jnp.einsum(
+        "hqk,khd->hqd", probs, prefix_values.astype(jnp.float32)
+    )
     attn = lax.optimization_barrier((accum / total[:, :, None]).astype(jnp.bfloat16))
     partial_value = jnp.einsum(
         "hqd,hdm->qm",

time: 244 us -> 244 us (level)
  waiting for transfers between devices: 108 us -> 105 us
    all_to_all x1, waiting for transfers between devices: 8.57 us -> 5.42 us  [local(): lax.all_to_all(outbound.reshape(seq_count, -1, 128), 'seq', 0, 0, tiled=T...]
  transfers between devices with their start and end apart: 11 -> 11, of which waited for: 8 -> 8; matrix products, arithmetic and copies ran while one was open for 23% -> 24% of each run, Pallas kernels for 0% -> 0%
where the time goes in v7:
time: 244 us; the launch traced here: 243 us
  waiting for transfers between devices  105 us (43%)
  starting transfers between devices  54.9 us (22%)
  matrix products  54.4 us (22%)
  other arithmetic  16 us (7%)
  local copies, waits for them, and re-layouts  12.3 us (5%)
    all_to_all x1, waiting for transfers between devices, local(): lax.all_to_all(result.reshape(experts * tp_count, first, half), ('seq', '...  46.1 us
    dot_general x2, matrix products, expert_rows(): both_parts = jnp.dot(arrived, gate_up, preferred_element_type=jnp.float32)  24.5 us
    all_to_all x1, waiting for transfers between devices, local(): lax.all_to_all(outgoing.reshape(experts, first, D), 'seq', 0, 0, tiled=True)  23.9 us
    all_to_all x1, waiting for transfers between devices, local(): lax.all_to_all(outgoing.reshape(experts, over, half), 'seq', 0, 0, tiled=...  12.9 us
    all_to_all x1, starting transfers between devices, local(): lax.all_to_all(outbound.reshape(seq_count, -1, 128), 'seq', 0, 0, tiled=T...  12 us
    all_to_all x1, starting transfers between devices, local(): lax.all_to_all(result.reshape(experts * tp_count, first, half), ('seq', '...  10.8 us
    all_to_all x1, starting transfers between devices, local(): lax.all_to_all(result.reshape(experts, over, half), 'seq', 0, 0, tiled=True)  10.2 us
    all_to_all x1, waiting for transfers between devices, local(): lax.all_to_all(picked.reshape(seq_count, depth * piece // 128, 128), 'seq...  9.32 us
  transfers between devices with their start and end apart: 11, of which 8 were waited for; matrix products, arithmetic and copies ran while one was open for 24% of the time, Pallas kernels for 0%

profile of v7, /device:TPU:1, one launch (start us, length us, event | category | flops | bytes accessed | tf_op | source)
XLA Modules:
  0.0 243.2 jit_solution(11482956544605337402)
XLA Ops:
  0.0 0.6 compare_reduce_fusion
  0.6 1.3 fusion.81
  2.0 0.9 pad_maximum_fusion.7
  2.9 0.8 reshape.226
  3.7 12.0 %all-to-all-start = ((bf16[64,9,128]{2,1,0:T(8,128)(2,1)}), bf16[64,9,128]{2,1,0:T(8,128)(2,1)S(1)}, u32[]{:S(2)}, u32[]{:S(2)}) async-start(bf16[64,9,128]{2,1,0:T(8,128)(2,1)} %reshape.226), calls=%async_computation | async-start | bytes 524288 | tf_op jit(solution)/shard_map/all_to_all | solution.py:49
  15.6 0.9 select_reduce_fusion.1
  16.6 0.6 lt.43
  17.2 1.3 fusion.89
  18.6 1.0 copy.94
  19.6 5.4 %all-to-all-done = bf16[64,9,128]{2,1,0:T(8,128)(2,1)S(1)} async-done(((bf16[64,9,128]{2,1,0:T(8,128)(2,1)}), bf16[64,9,128]{2,1,0:T(8,128)(2,1)S(1)}, u32[]{:S(2)}, u32[]{:S(2)}) %all-to-all-start) | async-done | bytes 147488 | tf_op jit(solution)/shard_map/all_to_all | solution.py:49
  25.6 0.9 reshape.228
  26.5 4.9 %all-to-all-start.1 = ((bf16[64,24,128]{2,1,0:T(8,128)(2,1)}), bf16[64,24,128]{2,1,0:T(8,128)(2,1)S(1)}, u32[]{:S(2)}, u32[]{:S(2)}) async-start(bf16[64,24,128]{2,1,0:T(8,128)(2,1)} %reshape.228), calls=%async_computation.1 | async-start | bytes 786432 | tf_op jit(solution)/shard_map/all_to_all | solution.py:57
  31.4 0.5 multiply_reduce_fusion.1
  32.3 9.3 %all-to-all-done.1 = bf16[64,24,128]{2,1,0:T(8,128)(2,1)S(1)} async-done(((bf16[64,24,128]{2,1,0:T(8,128)(2,1)}), bf16[64,24,128]{2,1,0:T(8,128)(2,1)S(1)}, u32[]{:S(2)}, u32[]{:S(2)}) %all-to-all-start.1) | async-done | bytes 393248 | tf_op jit(solution)/shard_map/all_to_all | solution.py:57
  42.0 0.9 fusion.91
  44.0 1.1 fusion.46
  45.1 1.1 copy-done.11
  46.2 1.3 convolution_bitcast_fusion
  47.5 3.2 %collective-permute-start = (f32[256,2048]{1,0:T(8,128)S(1)}, f32[256,2048]{1,0:T(8,128)}, u32[]{:S(2)}, u32[]{:S(2)}) collective-permute-start(f32[256,2048]{1,0:T(8,128)S(1)} %convolution_bitcast_fusion), channel_id=1, source_target_pairs={{0,1},{1,0},{2,3},{3,2},{4,5},{5,4},{6,7},{7,6},{8,9},{9,8},{10,11... | collective-permute-start | bytes 6291464 | tf_op jit(solution)/shard_map/ppermute | solution.py:105
  51.1 3.5 %collective-permute-done = f32[256,2048]{1,0:T(8,128)} collective-permute-done((f32[256,2048]{1,0:T(8,128)S(1)}, f32[256,2048]{1,0:T(8,128)}, u32[]{:S(2)}, u32[]{:S(2)}) %collective-permute-start) | collective-permute-done | bytes 2097184 | tf_op jit(solution)/shard_map/ppermute | solution.py:105
  54.6 2.9 %multiply_reduce_fusion = (f32[256]{0:T(256)S(1)}, f32[256,2048]{1,0:T(8,128)S(1)}) fusion(f32[256,2048]{1,0:T(8,128)} %copy-done.6, f32[256,2048]{1,0:T(8,128)} %collective-permute-done, bf16[256,2048]{1,0:T(8,128)(2,1)} %param.15), kind=kLoop, calls=%fused_computation.36 | loop fusion | flops 2621184 | bytes 7341056 | tf_op jit(solution)/shard_map/reduce_sum | solution.py:107
  57.8 1.0 copy-done.3
  58.8 1.5 fusion.37
  60.3 5.5 %all-to-all-start.2 = ((bf16[64,8,1024]{2,1,0:T(8,128)(2,1)}), bf16[64,8,1024]{2,1,0:T(8,128)(2,1)}, u32[]{:S(2)}, u32[]{:S(2)}) async-start(bf16[64,8,1024]{2,1,0:T(8,128)(2,1)} %fusion.37), calls=%async_computation.2 | async-start | bytes 2097152 | tf_op jit(solution)/shard_map/all_to_all | solution.py:157
  66.2 4.4 %convolution_convert_fusion = bf16[1024,2048]{1,0:T(8,128)(2,1)} fusion(pred[256,1024]{0,1:T(32,128)(4,1)S(1)} %fusion.56, bf16[256,2048]{1,0:T(8,128)(2,1)} %copy-done.3), kind=kOutput, calls=%fused_computation.8 | convolution fusion | flops 1075838976 | bytes 5505024 | tf_op jit(solution)/shard_map/ts,td->sd/dot_general | solution.py:174
  70.6 12.9 %all-to-all-done.2 = bf16[64,8,1024]{2,1,0:T(8,128)(2,1)} async-done(((bf16[64,8,1024]{2,1,0:T(8,128)(2,1)}), bf16[64,8,1024]{2,1,0:T(8,128)(2,1)}, u32[]{:S(2)}, u32[]{:S(2)}) %all-to-all-start.2) | async-done | bytes 1048608 | tf_op jit(solution)/shard_map/all_to_all | solution.py:157
  83.5 5.8 %all-to-all-start.4 = ((bf16[64,16,2048]{2,1,0:T(8,128)(2,1)}), bf16[64,16,2048]{2,1,0:T(8,128)(2,1)}, u32[]{:S(2)}, u32[]{:S(2)}) async-start(bf16[64,16,2048]{2,1,0:T(8,128)(2,1)} %bitcast.156), calls=%async_computation.4 | async-start | bytes 8388608 | tf_op jit(solution)/shard_map/all_to_all | solution.py:177
  89.3 1.9 collective-permute-start.3
  91.7 3.9 %copy.83 = bf16[1,512,2048]{1,2,0:T(8,128)(2,1)} copy(bf16[1,512,2048]{2,1,0:T(8,128)(2,1)} %param.27) | data formatting | bytes 4194304 | tf_op args[12]
  95.7 2.6 %collective-permute-done.2 = bf16[2048,512]{1,0:T(8,128)(2,1)} collective-permute-done((bf16[2048,512]{1,0:T(8,128)(2,1)}, bf16[2048,512]{1,0:T(8,128)(2,1)}, u32[]{:S(2)}, u32[]{:S(2)}) %collective-permute-start.2) | collective-permute-done | bytes 2097184 | tf_op jit(solution)/shard_map/ppermute | solution.py:39
  98.3 1.5 collective-permute-done.1
  99.8 11.6 %fusion.14 = f32[512,2048]{1,0:T(8,128)S(1)} fusion(bf16[512,1024]{1,0:T(8,128)(2,1)} %collective-permute-done.1, bf16[512,1024]{1,0:T(8,128)(2,1)} %bitcast.20, pred[]{:T(512)S(6)} %eq.146, bf16[2048,512]{1,0:T(8,128)(2,1)} %collective-permute-done.3, bf16[2048,512]{1,0:T(8,128)(2,1)} %bitcast.183, bf16[2048,512]{1,0:T(8,128)(2,1)} %collective-permute-done.2, ...), kind=kOutput, calls=%fused_computation.23 | convolution fusion | flops 4337958912 | bytes 14680065 | tf_op jit(solution)/shard_map/dot_general | solution.py:143
  111.4 3.6 %fusion.38 = bf16[64,8,1024]{2,1,0:T(8,128)(2,1)} fusion(s32[]{:T(128)S(6)} %select_n.56, bf16[512,2,1024]{0,2,1:T(8,128)(2,1)S(1)} %bitcast.162, bf16[512,2,1024]{0,2,1:T(8,128)(2,1)} %bitcast.25, f32[512,2048]{1,0:T(8,128)S(1)} %fusion.14), kind=kOutput, calls=%fused_computation.50 | convolution fusion | flops 1081606144 | bytes 9437188 | tf_op jit(solution)/shard_map/dot_general | solution.py:166
  115.0 23.9 %all-to-all-done.4 = bf16[64,16,2048]{2,1,0:T(8,128)(2,1)} async-done(((bf16[64,16,2048]{2,1,0:T(8,128)(2,1)}), bf16[64,16,2048]{2,1,0:T(8,128)(2,1)}, u32[]{:S(2)}, u32[]{:S(2)}) %all-to-all-start.4) | async-done | bytes 4194336 | tf_op jit(solution)/shard_map/all_to_all | solution.py:177
  138.9 10.2 %all-to-all-start.3 = ((bf16[64,8,1024]{2,1,0:T(8,128)(2,1)}), bf16[64,8,1024]{2,1,0:T(8,128)(2,1)}, u32[]{:S(2)}, u32[]{:S(2)}) async-start(bf16[64,8,1024]{2,1,0:T(8,128)(2,1)} %fusion.38), calls=%async_computation.3 | async-start | bytes 2097152 | tf_op jit(solution)/shard_map/all_to_all | solution.py:170
  149.1 12.9 %fusion.36 = f32[1024,2048]{1,0:T(8,128)S(1)} fusion(bf16[1024,2048]{1,0:T(8,128)(2,1)} %bitcast.35, bf16[2048,512]{1,0:T(8,128)(2,1)} %collective-permute-done.3, bf16[2048,512]{1,0:T(8,128)(2,1)} %bitcast.184, bf16[2048,512]{1,0:T(8,128)(2,1)} %collective-permute-done.2, bf16[2048,512]{1,0:T(8,128)(2,1)} %bitcast.187), kind=kOutput, calls=%fused_computation.48 | convolution fusion | flops 8623489024 | bytes 20971520 | tf_op jit(solution)/shard_map/dot_general | solution.py:143
  162.0 1.4 fusion
  163.6 3.6 %fusion.25 = bf16[1024,1024]{1,0:T(8,128)(2,1)S(1)} fusion(bf16[1024,1024]{1,0:T(8,128)(2,1)S(1)} %fusion, bf16[512,2,1024]{0,2,1:T(8,128)(2,1)} %bitcast.25, bf16[512,2,1024]{0,2,1:T(8,128)(2,1)S(1)} %bitcast.163), kind=kOutput, calls=%fused_computation.42 | convolution fusion | flops 2152726528 | bytes 8388608 | tf_op jit(solution)/shard_map/dot_general | solution.py:183
  167.2 3.6 %fusion.28 = bf16[1024,1024]{1,0:T(8,128)(2,1)S(1)} fusion(bf16[1024,1024]{1,0:T(8,128)(2,1)S(1)} %fusion, bf16[512,2,1024]{0,2,1:T(8,128)(2,1)S(1)} %bitcast.164, bf16[512,2,1024]{0,2,1:T(8,128)(2,1)} %bitcast.25), kind=kOutput, calls=%fused_computation.43 | convolution fusion | flops 2152726528 | bytes 8388608 | tf_op jit(solution)/shard_map/dot_general | solution.py:183
  170.8 2.3 pad_maximum_fusion.1
  173.1 10.8 %all-to-all-start.5 = ((bf16[128,16,1024]{2,1,0:T(8,128)(2,1)}), bf16[128,16,1024]{2,1,0:T(8,128)(2,1)}, u32[]{:S(2)}, u32[]{:S(2)}) async-start(bf16[128,16,1024]{2,1,0:T(8,128)(2,1)} %bitcast.157), calls=%async_computation.5 | async-start | bytes 8388608 | tf_op jit(solution)/shard_map/all_to_all | solution.py:190
  184.1 0.6 fusion.22
  184.8 0.6 fusion.21
  185.3 1.5 pad_maximum_fusion.3
  187.3 3.3 %fusion.51 = f32[512,1024]{1,0:T(8,128)} fusion(bf16[512,512]{0,1:T(8,128)(2,1)S(1)} %pad_maximum_fusion.6, bf16[64,8,1024]{2,1,0:T(8,128)(2,1)} %all-to-all-done.3), kind=kOutput, calls=%fused_computation.66 | convolution fusion | flops 536870912 | bytes 3670016 | tf_op jit(solution)/shard_map/dot_general | solution.py:136
  190.6 46.1 %all-to-all-done.5 = bf16[128,16,1024]{2,1,0:T(8,128)(2,1)} async-done(((bf16[128,16,1024]{2,1,0:T(8,128)(2,1)}), bf16[128,16,1024]{2,1,0:T(8,128)(2,1)}, u32[]{:S(2)}, u32[]{:S(2)}) %all-to-all-start.5) | async-done | bytes 4194336 | tf_op jit(solution)/shard_map/all_to_all | solution.py:190
  236.7 5.3 %fusion.92 = f32[512,1024]{1,0:T(8,128)S(1)} fusion(bf16[512,2048]{0,1:T(8,128)(2,1)} %pad_maximum_fusion.3, bf16[2048,1024]{1,0:T(8,128)(2,1)} %bitcast.43), kind=kOutput, calls=%fused_computation.132 | convolution fusion | flops 2147483648 | bytes 8388608 | tf_op jit(solution)/shard_map/dot_general | solution.py:206
  242.0 1.2 fusion.50
  (65 shorter events, 5.0 us)
Async XLA Ops:
  0.0 31.4 %copy-start = (bf16[256,1024]{1,0:T(8,128)(2,1)S(1)}, bf16[256,1024]{1,0:T(8,128)(2,1)}, u32[]{:S(2)}) copy-start(bf16[256,1024]{1,0:T(8,128)(2,1)} %param.16) | copy-start | bytes 1572868
  3.7 21.4 %all-to-all-start = ((bf16[64,9,128]{2,1,0:T(8,128)(2,1)}), bf16[64,9,128]{2,1,0:T(8,128)(2,1)S(1)}, u32[]{:S(2)}, u32[]{:S(2)}) async-start(bf16[64,9,128]{2,1,0:T(8,128)(2,1)} %reshape.226), calls=%async_computation | async-start | bytes 524288 | tf_op jit(solution)/shard_map/all_to_all | solution.py:49
  26.5 15.1 %all-to-all-start.1 = ((bf16[64,24,128]{2,1,0:T(8,128)(2,1)}), bf16[64,24,128]{2,1,0:T(8,128)(2,1)S(1)}, u32[]{:S(2)}, u32[]{:S(2)}) async-start(bf16[64,24,128]{2,1,0:T(8,128)(2,1)} %reshape.228), calls=%async_computation.1 | async-start | bytes 786432 | tf_op jit(solution)/shard_map/all_to_all | solution.py:57
  43.0 1.0 copy-start.7
  44.0 2.2 copy-start.11
  46.2 4.6 %copy-start.8 = (s32[256,8]{0,1:T(8,128)S(1)}, s32[256,8]{0,1:T(8,128)}, u32[]{:S(2)}) copy-start(s32[256,8]{0,1:T(8,128)} %param.23) | copy-start | bytes 24580
  47.5 3.6 %copy-start.6 = (f32[256,2048]{1,0:T(8,128)}, f32[256,2048]{1,0:T(8,128)S(1)}, u32[]{:S(2)}) copy-start(f32[256,2048]{1,0:T(8,128)S(1)} %convolution_bitcast_fusion) | copy-start | bytes 6291460
  47.5 7.1 %collective-permute-start = (f32[256,2048]{1,0:T(8,128)S(1)}, f32[256,2048]{1,0:T(8,128)}, u32[]{:S(2)}, u32[]{:S(2)}) collective-permute-start(f32[256,2048]{1,0:T(8,128)S(1)} %convolution_bitcast_fusion), channel_id=1, source_target_pairs={{0,1},{1,0},{2,3},{3,2},{4,5},{5,4},{6,7},{7,6},{8,9},{9,8},{10,11... | collective-permute-start | bytes 6291464 | tf_op jit(solution)/shard_map/ppermute | solution.py:105
  51.1 6.4 %copy-start.9 = (f32[2048]{0:T(1024)S(1)}, f32[2048]{0:T(1024)}, u32[]{:S(2)}) copy-start(f32[2048]{0:T(1024)} %param.22) | copy-start | bytes 24580
  57.8 1.0 copy-start.3
  60.3 23.2 %all-to-all-start.2 = ((bf16[64,8,1024]{2,1,0:T(8,128)(2,1)}), bf16[64,8,1024]{2,1,0:T(8,128)(2,1)}, u32[]{:S(2)}, u32[]{:S(2)}) async-start(bf16[64,8,1024]{2,1,0:T(8,128)(2,1)} %fusion.37), calls=%async_computation.2 | async-start | bytes 2097152 | tf_op jit(solution)/shard_map/all_to_all | solution.py:157
  83.5 55.4 %all-to-all-start.4 = ((bf16[64,16,2048]{2,1,0:T(8,128)(2,1)}), bf16[64,16,2048]{2,1,0:T(8,128)(2,1)}, u32[]{:S(2)}, u32[]{:S(2)}) async-start(bf16[64,16,2048]{2,1,0:T(8,128)(2,1)} %bitcast.156), calls=%async_computation.4 | async-start | bytes 8388608 | tf_op jit(solution)/shard_map/all_to_all | solution.py:177
  89.3 6.4 %collective-permute-start.3 = (bf16[2048,512]{1,0:T(8,128)(2,1)}, bf16[2048,512]{1,0:T(8,128)(2,1)}, u32[]{:S(2)}, u32[]{:S(2)}) collective-permute-start(bf16[2048,512]{1,0:T(8,128)(2,1)} %bitcast.182), channel_id=1, source_target_pairs={{0,1},{1,0},{2,3},{3,2},{4,5},{5,4},{6,7},{7,6},{8,9},{9,8},{10,11... | collective-permute-start | bytes 6291464 | tf_op jit(solution)/shard_map/ppermute | solution.py:40
  91.2 7.1 %collective-permute-start.2 = (bf16[2048,512]{1,0:T(8,128)(2,1)}, bf16[2048,512]{1,0:T(8,128)(2,1)}, u32[]{:S(2)}, u32[]{:S(2)}) collective-permute-start(bf16[2048,512]{1,0:T(8,128)(2,1)} %bitcast.185), channel_id=1, source_target_pairs={{0,1},{1,0},{2,3},{3,2},{4,5},{5,4},{6,7},{7,6},{8,9},{9,8},{10,11... | collective-permute-start | bytes 6291464 | tf_op jit(solution)/shard_map/ppermute | solution.py:39
  91.3 8.5 %collective-permute-start.1 = (bf16[512,1024]{1,0:T(8,128)(2,1)}, bf16[512,1024]{1,0:T(8,128)(2,1)}, u32[]{:S(2)}, u32[]{:S(2)}) collective-permute-start(bf16[512,1024]{1,0:T(8,128)(2,1)} %bitcast.20), channel_id=1, source_target_pairs={{0,1},{1,0},{2,3},{3,2},{4,5},{5,4},{6,7},{7,6},{8,9},{9,8},{10,11... | collective-permute-start | bytes 3145736 | tf_op jit(solution)/shard_map/ppermute | solution.py:159
  95.6 15.8 %collective-permute-start.4 = (bf16[512,2048]{0,1:T(8,128)(2,1)}, bf16[512,2048]{0,1:T(8,128)(2,1)}, u32[]{:S(2)}, u32[]{:S(2)}) collective-permute-start(bf16[512,2048]{0,1:T(8,128)(2,1)} %bitcast.161), channel_id=1, source_target_pairs={{0,1},{1,0},{2,3},{3,2},{4,5},{5,4},{6,7},{7,6},{8,9},{9,8},{10,11... | collective-permute-start | bytes 6291464 | tf_op jit(solution)/shard_map/ppermute | solution.py:41
  95.7 15.7 %copy-start.4 = (bf16[1,512,2048]{1,2,0:T(8,128)(2,1)S(1)}, bf16[1,512,2048]{1,2,0:T(8,128)(2,1)}, u32[]{:S(2)}) copy-start(bf16[1,512,2048]{1,2,0:T(8,128)(2,1)} %copy.83) | copy-start | bytes 6291460
  138.9 34.2 %all-to-all-start.3 = ((bf16[64,8,1024]{2,1,0:T(8,128)(2,1)}), bf16[64,8,1024]{2,1,0:T(8,128)(2,1)}, u32[]{:S(2)}, u32[]{:S(2)}) async-start(bf16[64,8,1024]{2,1,0:T(8,128)(2,1)} %fusion.38), calls=%async_computation.3 | async-start | bytes 2097152 | tf_op jit(solution)/shard_map/all_to_all | solution.py:170
  162.0 1.6 copy-start.5
  173.1 11.0 %copy-start.10 = (f32[256,8]{0,1:T(8,128)S(1)}, f32[256,8]{0,1:T(8,128)}, u32[]{:S(2)}) copy-start(f32[256,8]{0,1:T(8,128)} %param.24) | copy-start | bytes 24580
  173.1 63.6 %all-to-all-start.5 = ((bf16[128,16,1024]{2,1,0:T(8,128)(2,1)}), bf16[128,16,1024]{2,1,0:T(8,128)(2,1)}, u32[]{:S(2)}, u32[]{:S(2)}) async-start(bf16[128,16,1024]{2,1,0:T(8,128)(2,1)} %bitcast.157), calls=%async_computation.5 | async-start | bytes 8388608 | tf_op jit(solution)/shard_map/all_to_all | solution.py:190
  236.7 5.3 %copy-start.2 = (f32[512,1024]{1,0:T(8,128)S(1)}, f32[512,1024]{1,0:T(8,128)}, u32[]{:S(2)}) copy-start(f32[512,1024]{1,0:T(8,128)} %fusion.51) | copy-start | bytes 6291460
  236.7 6.6 %copy-start.1 = (bf16[256,1024]{1,0:T(8,128)(2,1)S(1)}, bf16[256,1024]{1,0:T(8,128)(2,1)}, u32[]{:S(2)}) copy-start(bf16[256,1024]{1,0:T(8,128)(2,1)} %param.16) | copy-start | bytes 1572868
